TPU v7x, 32 devices: a whole 2x2x4 slice. The times are simulated.
32 devices in a mesh: grp: 4 (over z), emb: 8 (over y, x, core).
Axes of the slice: x: 2, y: 2, z: 4, core: 2. Of those that a mesh axis runs over, the one named last changes fastest.
Arguments:
- bottom_out: bfloat16 [4096, 128], P(('grp', 'emb')), may hold values from -6 to 6
- owner_ids: int32 [106496, 1], P(('grp', 'emb')), may hold values from 0 to 7; in each aligned block of 3328 rows (0 to 3327, 3328 to 6655, ...) at most 624 rows name the same one
- row_ids: int32 [4096, 26], P(('grp', 'emb')), may hold values from 0 to 95
- positions: int32 [4096], P(('grp', 'emb')), may hold values from 0 to 15
- labels: int32 [4096], P(('grp', 'emb')), may hold values 0 or 1
- tables: bfloat16 [26, 768, 128], P(None, 'emb'), may hold values from -6 to 6
- cross_down: bfloat16 [3456, 512], replicated, may hold values from -0.109375 to 0.109375
- cross_up: bfloat16 [512, 3456], replicated, may hold values from -0.25 to 0.25
- cross_bias: float32 [3456], replicated, may hold values from -3 to 3
- out_weight: bfloat16 [3456], replicated, may hold values from -0.109375 to 0.109375
- position_bias: float32 [16], replicated, may hold values from -2 to 2
Outputs:
- table_grad: float32 [26, 768, 128], P(None, 'emb')
- bottom_grad: bfloat16 [4096, 128], P(('grp', 'emb'))
- bias_grad: float32 [3456], replicated
Inputs may be any that keep to these rules, and one draw needn't show every extreme that they name: `owner_ids`: in every aligned block of 3328 lookups (the lookups of one device) no owner is named more than 624 times, and in some block one owner is named exactly 624 times.
All inputs are finite; a program needn't handle non-finite values. No bound on the sum of `labels` on one device may be relied on, other than what follows from the above.
Results may differ from a plain program's by a relative error of at most 0.0085.
Values may be sent and summed in bfloat16 or wider, within the bound.
No kernel may reach another device: no remote copies, remote signals or barrier semaphores. Data moves between devices by JAX's collectives and lax.ppermute only.
A program may use at most 64 MiB of HBM per device.

v0:
```python
import jax
import jax.numpy as jnp
from jax import lax
from jax.sharding import PartitionSpec as P


def local(
    bottom_out,
    owner_ids,
    row_ids,
    positions,
    labels,
    tables,
    cross_down,
    cross_up,
    cross_bias,
    out_weight,
    position_bias,
):
    sample_count, table_count = row_ids.shape
    rows_local = tables.shape[1]
    row_width = tables.shape[2]
    owner_count = lax.axis_size("emb")
    capacity = 3 * sample_count * table_count // (2 * owner_count)
    lookup_count = sample_count * table_count
    owners = owner_ids.reshape(sample_count, table_count)
    flat_owner = owners.reshape(-1)
    local_grid = jnp.arange(table_count, dtype=jnp.int32)[None, :] * rows_local + row_ids
    local_index = local_grid.reshape(-1)
    owner_marks = (flat_owner[:, None] == jnp.arange(owner_count, dtype=jnp.int32)[None, :]).astype(
        jnp.int32
    )
    ranking = jnp.cumsum(owner_marks, axis=0) - 1
    slot_index = jnp.sum(ranking * owner_marks, axis=1)
    buffer_place = flat_owner * capacity + slot_index
    flat_table = tables.reshape(table_count * rows_local, row_width)
    request = jnp.zeros((owner_count * capacity,), jnp.int32).at[buffer_place].set(local_index)
    request = request.reshape(owner_count, capacity)
    received = lax.all_to_all(request, "emb", split_axis=0, concat_axis=0, tiled=True)
    fetched = flat_table[received]
    arrived = lax.all_to_all(fetched, "emb", split_axis=0, concat_axis=0, tiled=True)
    pooled = arrived.reshape(owner_count * capacity, row_width)[buffer_place].reshape(
        sample_count, table_count * row_width
    )
    first = jnp.concatenate([bottom_out, pooled], axis=1)
    first_wide = first.astype(jnp.float32)
    weight_row = out_weight.astype(jnp.float32)
    reduced = jnp.dot(first, cross_down, preferred_element_type=jnp.float32).astype(jnp.bfloat16)
    gate_scale = jnp.dot(reduced, cross_up, preferred_element_type=jnp.float32) + cross_bias
    crossed = first_wide * gate_scale + first_wide
    position_marks = (
        positions[:, None] == jnp.arange(position_bias.shape[0], dtype=jnp.int32)[None, :]
    ).astype(jnp.float32)
    logit = jnp.sum(crossed * weight_row[None, :], axis=1) + jnp.sum(
        position_marks * position_bias[None, :], axis=1
    )
    err = jax.nn.sigmoid(logit) - labels.astype(jnp.float32)
    cotangent = err[:, None] * weight_row[None, :]
    scaled = cotangent * first_wide
    down_grad = lax.dot_general(
        scaled.astype(jnp.bfloat16),
        cross_up,
        (((1,), (1,)), ((), ())),
        preferred_element_type=jnp.float32,
    ).astype(jnp.bfloat16)
    back_term = lax.dot_general(
        down_grad, cross_down, (((1,), (1,)), ((), ())), preferred_element_type=jnp.float32
    )
    input_grad = (cotangent * (gate_scale + 1.0) + back_term).astype(jnp.bfloat16)
    bottom_grad = input_grad[:, :row_width]
    row_grads = input_grad[:, row_width:].reshape(lookup_count, row_width)
    outgoing = (
        jnp.zeros((owner_count * capacity, row_width), jnp.bfloat16).at[buffer_place].set(row_grads)
    )
    incoming = lax.all_to_all(
        outgoing.reshape(owner_count, capacity, row_width),
        "emb",
        split_axis=0,
        concat_axis=0,
        tiled=True,
    )
    local_grad = (
        jnp.zeros((table_count * rows_local, row_width), jnp.float32)
        .at[received.reshape(-1)]
        .add(incoming.reshape(owner_count * capacity, row_width).astype(jnp.float32))
    )
    summed_grad = lax.psum(local_grad.astype(jnp.bfloat16), "grp").astype(jnp.float32)
    table_grad = summed_grad.reshape(table_count, rows_local, row_width)
    bias_local = jnp.sum(scaled, axis=0)
    bias_grad = lax.psum(bias_local, ("grp", "emb"))
    return (table_grad, bottom_grad, bias_grad)


def solution(mesh):
    placed = (
        P(("grp", "emb"), None),
        P(("grp", "emb"), None),
        P(("grp", "emb"), None),
        P(("grp", "emb")),
        P(("grp", "emb")),
        P(None, "emb", None),
        P(),
        P(),
        P(),
        P(),
        P(),
    )
    return jax.shard_map(
        local,
        mesh=mesh,
        in_specs=placed,
        out_specs=(P(None, "emb", None), P(("grp", "emb"), None), P()),
        check_vma=False,
    )
```

profile of v0, /device:TPU:0, one launch (start us, length us, event | category | flops | bytes accessed | tf_op | source)
XLA Modules:
  0.0 241.9 jit_solution(920060485825970964)
XLA Ops:
  7.2 0.0 copy-start
  7.2 0.9 broadcast_add_fusion
  8.1 0.7 copy.15
  8.9 1.6 reshape.157
  10.4 0.7 reduce
  11.2 0.7 fusion.17
  11.9 5.2 %reduce-window.6 = s32[8,26,128]{2,1,0:T(8,128)} reduce-window(s32[8,26,128]{2,1,0:T(8,128)} %fusion.17, s32[]{:T(128)} %constant.10.clone.1), window={size=1x1x128 pad=0_0x0_0x127_0}, to_apply=%region_0.0 | reduce-window | flops 3381248 | bytes 212996 | tf_op jit(solution)/shard_map/reduce-window
  17.1 1.8 slice_reduce_fusion
  18.9 1.5 reduce-window.9
  20.3 1.0 add_bitcast_fusion
  21.4 0.1 fusion.19
  21.5 0.8 fusion.22
  22.2 0.0 copy-start.2
  22.2 13.5 %scatter_custom_fusion = s32[4992]{0:T(1024)} fusion(s32[3328]{0:T(1024)S(1)} %fusion.22, s32[3328]{0:T(1024)} %reshape.157, s32[]{:T(128)} %constant.10.clone.1), kind=kCustom, calls=%fused_computation.40 | custom fusion | bytes 20480 | tf_op jit(solution)/shard_map/scatter | solution.py:37
  35.7 1.4 all_to_all.14
  37.1 9.9 %all_to_all.22 = s32[8,1,624]{2,1,0:T(1,128)S(1)} all-to-all(s32[8,1,624]{2,1,0:T(1,128)} %all_to_all.14), channel_id=1, replica_groups=mesh['grp'=4,'emb'=8] {'emb'}, dimensions={0} | all-to-all | bytes 39936 | tf_op jit(solution)/shard_map/all_to_all | solution.py:39
  47.1 0.0 copy-start.1
  47.1 0.6 copy-done.1
  47.7 0.7 fusion.20
  48.3 1.4 reshape.139
  49.8 1.3 pad_clamp_fusion
  51.1 12.3 %gather_fusion = bf16[4992,128]{1,0:T(8,128)(2,1)} fusion(bf16[2496,128]{1,0:T(8,128)(2,1)} %bitcast.32, s32[5120]{0:T(1024)} %pad_clamp_fusion), kind=kCustom, calls=%fused_computation | custom fusion | bytes 2575872 | tf_op jit(solution)/shard_map/gather | solution.py:40
  63.4 0.0 copy-done.2
  63.4 4.3 %all-to-all-start.1 = ((bf16[8,624,128]{2,1,0:T(8,128)(2,1)}), bf16[8,624,128]{2,1,0:T(8,128)(2,1)}, u32[]{:S(2)}, u32[]{:S(2)}) async-start(bf16[8,624,128]{2,1,0:T(8,128)(2,1)} %bitcast.34), calls=%async_computation.1 | async-start | bytes 2555904 | tf_op jit(solution)/shard_map/all_to_all | solution.py:41
  67.6 0.7 convert_element_type.40
  68.3 1.3 pad_clamp_fusion.1
  69.7 1.4 constant_dynamic-update-slice_fusion.1
  71.1 1.2 select_reduce_fusion
  72.3 13.2 %all-to-all-done.1 = bf16[8,624,128]{2,1,0:T(8,128)(2,1)} async-done(((bf16[8,624,128]{2,1,0:T(8,128)(2,1)}), bf16[8,624,128]{2,1,0:T(8,128)(2,1)}, u32[]{:S(2)}, u32[]{:S(2)}) %all-to-all-start.1) | async-done | bytes 1277984 | tf_op jit(solution)/shard_map/all_to_all | solution.py:41
  85.5 9.2 %gather_fusion.1 = bf16[3328,128]{1,0:T(8,128)(2,1)} fusion(bf16[4992,128]{1,0:T(8,128)(2,1)} %bitcast.4, s32[4096]{0:T(1024)} %pad_clamp_fusion.1), kind=kCustom, calls=%fused_computation.1 | custom fusion | bytes 1717248 | tf_op jit(solution)/shard_map/gather | solution.py:42
  94.7 2.8 %reshape.131 = bf16[128,3328]{1,0:T(8,128)(2,1)} reshape(bf16[3328,128]{1,0:T(8,128)(2,1)} %gather_fusion.1) | data formatting | bytes 1703936 | tf_op jit(solution)/shard_map/reshape | solution.py:42
  97.5 2.1 constant_dynamic-update-slice_fusion
  99.6 0.0 copy-done
  99.6 5.6 %fusion.6 = (f32[128]{0:T(128)}, f32[128,3456]{1,0:T(8,128)}) fusion(bf16[128,3456]{1,0:T(8,128)(2,1)} %constant_dynamic-update-slice_fusion, f32[3456]{0:T(1024)S(1)} %convert_element_type.40, f32[3456]{0:T(1024)} %param.19, bf16[512,3456]{1,0:T(8,128)(2,1)} %param.18, bf16[3456,512]{1,0:T(8,128)(2,1)S(1)} %copy-done), kind=kOutput, calls=%fused_computation.16 | convolution fusion | flops 908689280 | bytes 9760256 | tf_op jit(solution)/shard_map/dot_general | solution.py:49
  105.2 1.2 divide_subtract_fusion
  106.4 6.1 %fusion = bf16[128,3456]{1,0:T(8,128)(2,1)} fusion(bf16[3456,512]{1,0:T(8,128)(2,1)S(1)} %copy-done, f32[128,3456]{1,0:T(8,128)} %get-tuple-element.4, bf16[512,3456]{1,0:T(8,128)(2,1)} %param.18, bf16[128,3456]{1,0:T(8,128)(2,1)} %constant_dynamic-update-slice_fusion, f32[128]{0:T(128)} %divide_subtract_fusion, f32[3456]{0:T(1024)S(1)} %convert_element_type.40), kind=kOutput, calls=%fused_computation.7 | convolution fusion | flops 910016512 | bytes 10631168 | tf_op jit(solution)/shard_map/dot_general | solution.py:66
  112.4 2.1 slice.21
  114.5 2.9 %reshape.165 = bf16[3328,128]{1,0:T(8,128)(2,1)} reshape(bf16[128,3328]{1,0:T(8,128)(2,1)} %slice.21) | data formatting | bytes 1703936 | tf_op jit(solution)/shard_map/reshape | solution.py:71
  117.4 14.9 %scatter_custom_fusion.1 = bf16[4992,128]{1,0:T(8,128)(2,1)} fusion(s32[3328]{0:T(1024)} %copy-done.2, bf16[3328,128]{1,0:T(8,128)(2,1)} %reshape.165, bf16[]{:T(256)} %constant.5.clone.1), kind=kCustom, calls=%fused_computation.21 | custom fusion | bytes 1278464 | tf_op jit(solution)/shard_map/scatter | solution.py:73
  132.3 4.3 %all-to-all-start.2 = ((bf16[8,624,128]{2,1,0:T(8,128)(2,1)}), bf16[8,624,128]{2,1,0:T(8,128)(2,1)}, u32[]{:S(2)}, u32[]{:S(2)}) async-start(bf16[8,624,128]{2,1,0:T(8,128)(2,1)} %bitcast.33), calls=%async_computation.2 | async-start | bytes 2555904 | tf_op jit(solution)/shard_map/all_to_all | solution.py:75
  136.5 0.2 all-reduce.2.cloned.1.call-start
  136.8 1.4 reduce.4
  138.2 1.4 reshape.128
  139.6 1.4 fusion.21
  141.0 13.4 %all-to-all-done.2 = bf16[8,624,128]{2,1,0:T(8,128)(2,1)} async-done(((bf16[8,624,128]{2,1,0:T(8,128)(2,1)}), bf16[8,624,128]{2,1,0:T(8,128)(2,1)}, u32[]{:S(2)}, u32[]{:S(2)}) %all-to-all-start.2) | async-done | bytes 1277984 | tf_op jit(solution)/shard_map/all_to_all | solution.py:75
  154.4 29.6 %scatter_custom_fusion.2 = f32[2496,128]{1,0:T(8,128)} fusion(s32[4992]{0:T(1024)} %fusion.21, bf16[4992,128]{1,0:T(8,128)(2,1)} %bitcast.8, f32[]{:T(128)} %constant.9.clone.1), kind=kCustom, calls=%fused_computation.9 | custom fusion | flops 1277952 | bytes 2556416 | tf_op jit(solution)/shard_map/scatter-add | solution.py:85
  184.0 2.2 convert_element_type.47
  186.2 0.0 all-reduce.2.cloned.1.call-update
  186.2 1.4 slice.22
  187.6 2.1 fusion.3
  189.7 43.1 %psum.15 = f32[3456]{0:T(1024)} all-reduce(f32[3456]{0:T(1024)} %fusion.3), channel_id=1, replica_groups=mesh['grp'=4,'emb'=8] {'grp','emb'}, use_global_device_ids=true, to_apply=%region_10.11 | all-reduce | flops 3456 | bytes 27648 | tf_op jit(solution)/shard_map/psum | solution.py:90
  232.8 0.0 all-reduce.2.cloned.1.call-done
  232.8 2.3 reshape.135
  (1 shorter events, 0.0 us)
Async XLA Ops:
  7.2 92.5 %copy-start = (bf16[3456,512]{1,0:T(8,128)(2,1)S(1)}, bf16[3456,512]{1,0:T(8,128)(2,1)}, u32[]{:S(2)}) copy-start(bf16[3456,512]{1,0:T(8,128)(2,1)} %param.17) | copy-start | bytes 10616836
  22.2 41.2 %copy-start.2 = (s32[3328]{0:T(1024)}, s32[3328]{0:T(1024)S(1)}, u32[]{:S(2)}) copy-start(s32[3328]{0:T(1024)S(1)} %fusion.22) | copy-start | bytes 39940
  47.1 0.6 copy-start.1
  63.4 22.1 %all-to-all-start.1 = ((bf16[8,624,128]{2,1,0:T(8,128)(2,1)}), bf16[8,624,128]{2,1,0:T(8,128)(2,1)}, u32[]{:S(2)}, u32[]{:S(2)}) async-start(bf16[8,624,128]{2,1,0:T(8,128)(2,1)} %bitcast.34), calls=%async_computation.1 | async-start | bytes 2555904 | tf_op jit(solution)/shard_map/all_to_all | solution.py:41
  132.3 22.1 %all-to-all-start.2 = ((bf16[8,624,128]{2,1,0:T(8,128)(2,1)}), bf16[8,624,128]{2,1,0:T(8,128)(2,1)}, u32[]{:S(2)}, u32[]{:S(2)}) async-start(bf16[8,624,128]{2,1,0:T(8,128)(2,1)} %bitcast.33), calls=%async_computation.2 | async-start | bytes 2555904 | tf_op jit(solution)/shard_map/all_to_all | solution.py:75
  136.5 96.3 %all-reduce.2.cloned.1.call-start = ((), (), s32[]{:S(2)}) async-start(), calls=%async_computation.3 | async-start | bytes 1277952 | tf_op jit(solution)/shard_map/psum | solution.py:87
Sparse Core Ops, SparseCore 0:
  186.4 44.5 all-reduce.1
where the time goes:
time: 245 us; the launch traced here: 242 us
  local copies, waits for them, and re-layouts  71.5 us (29%)
  other arithmetic  56.3 us (23%)
  blocking collectives  53 us (22%)
  waiting for transfers between devices  26.7 us (11%)
  between operations  14.1 us (6%)
  matrix products  11.6 us (5%)
  starting transfers between devices  8.73 us (4%)
    psum x1, blocking collectives, local(): bias_grad = lax.psum(bias_local, ('grp', 'emb'))  43.1 us
    scatter-add x1, other arithmetic, local(): local_grad = jnp.zeros((table_count * rows_local, row_width), jnp.float32...  29.6 us
    scatter x1, local copies, waits for them, and re-layouts, local(): jnp.zeros((owner_count * capacity, row_width), jnp.bfloat16)  14.9 us
    scatter x1, local copies, waits for them, and re-layouts, local(): jnp.zeros((owner_count * capacity,), jnp.int32).at[buffer_place]  13.5 us
    all_to_all x1, waiting for transfers between devices, local(): lax.all_to_all(outgoing.reshape(owner_count, capacity, row_width), 'emb',...  13.4 us
    all_to_all x1, waiting for transfers between devices, local(): lax.all_to_all(fetched, 'emb', split_axis=0, concat_axis=0, tiled=True)  13.2 us
    gather x1, local copies, waits for them, and re-layouts, local(): fetched = flat_table[received]  12.3 us
    all_to_all x1, blocking collectives, local(): lax.all_to_all(request, 'emb', split_axis=0, concat_axis=0, tiled=True)  9.94 us
  transfers between devices with their start and end apart: 3, of which 2 were waited for; matrix products, arithmetic and copies ran while one was open for 5% of the time, Pallas kernels for 0%

commit v1 on v0

--- a/solution.py
+++ b/solution.py
@@ -57,6 +57,7 @@
     err = jax.nn.sigmoid(logit) - labels.astype(jnp.float32)
     cotangent = err[:, None] * weight_row[None, :]
     scaled = cotangent * first_wide
+    bias_local = jnp.sum(scaled, axis=0)
     down_grad = lax.dot_general(
         scaled.astype(jnp.bfloat16),
         cross_up,
@@ -84,10 +85,12 @@
         .at[received.reshape(-1)]
         .add(incoming.reshape(owner_count * capacity, row_width).astype(jnp.float32))
     )
-    summed_grad = lax.psum(local_grad.astype(jnp.bfloat16), "grp").astype(jnp.float32)
+    bias_emb = lax.psum(bias_local, "emb")
+    packed = jnp.concatenate([local_grad.reshape(-1), bias_emb])
+    packed = lax.psum(packed, "grp")
+    summed_grad = packed[: local_grad.size].reshape(local_grad.shape)
+    bias_grad = packed[local_grad.size :]
     table_grad = summed_grad.reshape(table_count, rows_local, row_width)
-    bias_local = jnp.sum(scaled, axis=0)
-    bias_grad = lax.psum(bias_local, ("grp", "emb"))
     return (table_grad, bottom_grad, bias_grad)
 
 

time: 245 us -> 280 us (1.14)
  waiting for transfers between devices: 26.7 us -> 71.4 us
  blocking collectives: 53 us -> 38.2 us
  local copies, waits for them, and re-layouts: 71.5 us -> 75.2 us
    psum x1, waiting for transfers between devices: 0.01 us -> 58.2 us  [local(): packed = lax.psum(packed, 'grp')]
    psum x1, blocking collectives: 43.1 us -> 28.3 us  [local(): bias_emb = lax.psum(bias_local, 'emb')]
    all_to_all x1, waiting for transfers between devices: 13.4 us -> 0.01 us  [local(): lax.all_to_all(outgoing.reshape(owner_count, capacity, row_width), 'emb',...]
    scatter-add x1, other arithmetic: 29.6 us -> 33.6 us  [local(): local_grad = jnp.zeros((table_count * rows_local, row_width), jnp.float32...]
    slice x1 -> x3, local copies, waits for them, and re-layouts: 1.8 us -> 5.55 us  [the longest x1 2.43 us: local(): summed_grad = packed[:local_grad.size].reshape(local_grad.shape)]
  transfers between devices with their start and end apart: 3 -> 3, of which waited for: 2 -> 2; matrix products, arithmetic and copies ran while one was open for 5% -> 4% of each run, Pallas kernels for 0% -> 0%
where the time goes in v1:
time: 280 us; the launch traced here: 277 us
  local copies, waits for them, and re-layouts  75.2 us (27%)
  waiting for transfers between devices  71.4 us (26%)
  other arithmetic  58.3 us (21%)
  blocking collectives  38.2 us (14%)
  between operations  14.1 us (5%)
  matrix products  11.6 us (4%)
  starting transfers between devices  8.55 us (3%)
    psum x1, waiting for transfers between devices, local(): packed = lax.psum(packed, 'grp')  58.2 us
    scatter-add x1, other arithmetic, local(): local_grad = jnp.zeros((table_count * rows_local, row_width), jnp.float32...  33.6 us
    psum x1, blocking collectives, local(): bias_emb = lax.psum(bias_local, 'emb')  28.3 us
    scatter x1, local copies, waits for them, and re-layouts, local(): jnp.zeros((owner_count * capacity, row_width), jnp.bfloat16)  14.9 us
    scatter x1, local copies, waits for them, and re-layouts, local(): jnp.zeros((owner_count * capacity,), jnp.int32).at[buffer_place]  13.5 us
    all_to_all x1, waiting for transfers between devices, local(): lax.all_to_all(fetched, 'emb', split_axis=0, concat_axis=0, tiled=True)  13.2 us
    gather x1, local copies, waits for them, and re-layouts, local(): fetched = flat_table[received]  12.3 us
    all_to_all x1, blocking collectives, local(): lax.all_to_all(request, 'emb', split_axis=0, concat_axis=0, tiled=True)  9.94 us
  transfers between devices with their start and end apart: 3, of which 2 were waited for; matrix products, arithmetic and copies ran while one was open for 4% of the time, Pallas kernels for 0%

profile of v1, /device:TPU:0, one launch (start us, length us, event | category | flops | bytes accessed | tf_op | source)
XLA Modules:
  0.0 277.4 jit_solution(10590677054743617805)
XLA Ops:
  7.2 0.0 copy-start
  7.2 0.9 broadcast_add_fusion
  8.1 0.7 copy.15
  8.9 1.6 reshape.153
  10.4 0.7 reduce
  11.2 0.7 fusion.17
  11.9 5.2 %reduce-window.6 = s32[8,26,128]{2,1,0:T(8,128)} reduce-window(s32[8,26,128]{2,1,0:T(8,128)} %fusion.17, s32[]{:T(128)} %constant.10.clone.1), window={size=1x1x128 pad=0_0x0_0x127_0}, to_apply=%region_0.0 | reduce-window | flops 3381248 | bytes 212996 | tf_op jit(solution)/shard_map/reduce-window
  17.1 1.8 slice_reduce_fusion
  18.9 1.5 reduce-window.9
  20.3 1.0 add_bitcast_fusion
  21.4 0.1 fusion.19
  21.5 0.8 fusion.22
  22.2 0.0 copy-start.2
  22.2 13.5 %scatter_custom_fusion = s32[4992]{0:T(1024)} fusion(s32[3328]{0:T(1024)S(1)} %fusion.22, s32[3328]{0:T(1024)} %reshape.153, s32[]{:T(128)} %constant.10.clone.1), kind=kCustom, calls=%fused_computation.41 | custom fusion | bytes 20480 | tf_op jit(solution)/shard_map/scatter | solution.py:37
  35.7 1.4 all_to_all.14
  37.1 9.9 %all_to_all.22 = s32[8,1,624]{2,1,0:T(1,128)S(1)} all-to-all(s32[8,1,624]{2,1,0:T(1,128)} %all_to_all.14), channel_id=1, replica_groups=mesh['grp'=4,'emb'=8] {'emb'}, dimensions={0} | all-to-all | bytes 39936 | tf_op jit(solution)/shard_map/all_to_all | solution.py:39
  47.1 0.0 copy-start.1
  47.1 0.6 copy-done.1
  47.7 0.7 fusion.20
  48.3 1.4 reshape.135
  49.8 1.3 pad_clamp_fusion
  51.1 12.3 %gather_fusion = bf16[4992,128]{1,0:T(8,128)(2,1)} fusion(bf16[2496,128]{1,0:T(8,128)(2,1)} %bitcast.33, s32[5120]{0:T(1024)} %pad_clamp_fusion), kind=kCustom, calls=%fused_computation | custom fusion | bytes 2575872 | tf_op jit(solution)/shard_map/gather | solution.py:40
  63.4 0.0 copy-done.2
  63.4 4.3 %all-to-all-start.1 = ((bf16[8,624,128]{2,1,0:T(8,128)(2,1)}), bf16[8,624,128]{2,1,0:T(8,128)(2,1)}, u32[]{:S(2)}, u32[]{:S(2)}) async-start(bf16[8,624,128]{2,1,0:T(8,128)(2,1)} %bitcast.36), calls=%async_computation.1 | async-start | bytes 2555904 | tf_op jit(solution)/shard_map/all_to_all | solution.py:41
  67.6 0.7 convert_element_type.36
  68.3 1.3 pad_clamp_fusion.1
  69.7 1.4 constant_dynamic-update-slice_fusion.1
  71.1 1.3 select_reduce_fusion
  72.3 13.2 %all-to-all-done.1 = bf16[8,624,128]{2,1,0:T(8,128)(2,1)} async-done(((bf16[8,624,128]{2,1,0:T(8,128)(2,1)}), bf16[8,624,128]{2,1,0:T(8,128)(2,1)}, u32[]{:S(2)}, u32[]{:S(2)}) %all-to-all-start.1) | async-done | bytes 1277984 | tf_op jit(solution)/shard_map/all_to_all | solution.py:41
  85.5 9.2 %gather_fusion.1 = bf16[3328,128]{1,0:T(8,128)(2,1)} fusion(bf16[4992,128]{1,0:T(8,128)(2,1)} %bitcast.4, s32[4096]{0:T(1024)} %pad_clamp_fusion.1), kind=kCustom, calls=%fused_computation.1 | custom fusion | bytes 1717248 | tf_op jit(solution)/shard_map/gather | solution.py:42
  94.7 2.8 reshape.128
  97.5 2.1 constant_dynamic-update-slice_fusion
  99.6 0.0 copy-done
  99.6 5.6 %fusion.6 = (f32[128]{0:T(128)}, f32[128,3456]{1,0:T(8,128)}) fusion(bf16[128,3456]{1,0:T(8,128)(2,1)} %constant_dynamic-update-slice_fusion, f32[3456]{0:T(1024)S(1)} %convert_element_type.36, f32[3456]{0:T(1024)} %param.19, bf16[512,3456]{1,0:T(8,128)(2,1)S(1)} %copy-done, bf16[3456,512]{1,0:T(8,128)(2,1)} %param.17), kind=kOutput, calls=%fused_computation.16 | convolution fusion | flops 908689280 | bytes 9760256 | tf_op jit(solution)/shard_map/dot_general | solution.py:49
  105.2 1.2 divide_subtract_fusion
  106.4 6.1 %fusion = bf16[128,3456]{1,0:T(8,128)(2,1)} fusion(bf16[3456,512]{1,0:T(8,128)(2,1)} %param.17, f32[128,3456]{1,0:T(8,128)} %get-tuple-element.4, bf16[512,3456]{1,0:T(8,128)(2,1)S(1)} %copy-done, bf16[128,3456]{1,0:T(8,128)(2,1)} %constant_dynamic-update-slice_fusion, f32[128]{0:T(128)} %divide_subtract_fusion, f32[3456]{0:T(1024)S(1)} %convert_element_type.36), kind=kOutput, calls=%fused_computation.7 | convolution fusion | flops 910016512 | bytes 10631168 | tf_op jit(solution)/shard_map/dot_general | solution.py:67
  112.5 2.1 slice.29
  114.6 2.9 %reshape.161 = bf16[3328,128]{1,0:T(8,128)(2,1)} reshape(bf16[128,3328]{1,0:T(8,128)(2,1)} %slice.29) | data formatting | bytes 1703936 | tf_op jit(solution)/shard_map/reshape | solution.py:72
  117.5 14.9 %scatter_custom_fusion.1 = bf16[4992,128]{1,0:T(8,128)(2,1)} fusion(s32[3328]{0:T(1024)} %copy-done.2, bf16[3328,128]{1,0:T(8,128)(2,1)} %reshape.161, bf16[]{:T(256)} %constant.5.clone.1), kind=kCustom, calls=%fused_computation.22 | custom fusion | bytes 1278464 | tf_op jit(solution)/shard_map/scatter | solution.py:74
  132.3 4.3 %all-to-all-start.2 = ((bf16[8,624,128]{2,1,0:T(8,128)(2,1)}), bf16[8,624,128]{2,1,0:T(8,128)(2,1)}, u32[]{:S(2)}, u32[]{:S(2)}) async-start(bf16[8,624,128]{2,1,0:T(8,128)(2,1)} %bitcast.34), calls=%async_computation.2 | async-start | bytes 2555904 | tf_op jit(solution)/shard_map/all_to_all | solution.py:76
  136.6 0.0 all-reduce.2.cloned.1.call-start
  136.7 1.4 reduce.4
  138.0 1.4 reshape.125
  139.5 1.4 fusion.21
  140.9 2.1 fusion.3
  143.0 28.3 %psum.14 = f32[3456]{0:T(1024)S(1)} all-reduce(f32[3456]{0:T(1024)} %fusion.3), channel_id=1, replica_groups=mesh['grp'=4,'emb'=8] {'emb'}, use_global_device_ids=true, to_apply=%region_9.10 | all-reduce | flops 3456 | bytes 27648 | tf_op jit(solution)/shard_map/psum | solution.py:88
  171.2 0.0 all-to-all-done.2
  171.2 33.6 %scatter_custom_fusion.2 = f32[2496,128]{1,0:T(8,128)} fusion(s32[4992]{0:T(1024)} %fusion.21, bf16[4992,128]{1,0:T(8,128)(2,1)} %bitcast.9, f32[]{:T(128)} %constant.9.clone.1), kind=kCustom, calls=%fused_computation.9 | custom fusion | flops 1277952 | bytes 2556416 | tf_op jit(solution)/shard_map/scatter-add | solution.py:86
  204.8 2.5 pad_maximum_fusion
  207.3 0.0 all-reduce.2.cloned.1.call-update
  207.3 1.4 slice.31
  208.7 58.2 %all-reduce.2.cloned.1.call-done = f32[322944]{0:T(1024)} async-done(((f32[322944]{0:T(1024)}), f32[322944]{0:T(1024)}) %all-reduce.2.cloned.1.call-update) | async-done | bytes 1291792 | tf_op jit(solution)/shard_map/psum | solution.py:90
  266.8 1.3 slice.32
  268.2 2.4 slice.30
  (1 shorter events, 0.0 us)
Async XLA Ops:
  7.2 92.5 %copy-start = (bf16[512,3456]{1,0:T(8,128)(2,1)S(1)}, bf16[512,3456]{1,0:T(8,128)(2,1)}, u32[]{:S(2)}) copy-start(bf16[512,3456]{1,0:T(8,128)(2,1)} %param.18) | copy-start | bytes 10616836
  22.2 41.2 %copy-start.2 = (s32[3328]{0:T(1024)}, s32[3328]{0:T(1024)S(1)}, u32[]{:S(2)}) copy-start(s32[3328]{0:T(1024)S(1)} %fusion.22) | copy-start | bytes 39940
  47.1 0.6 copy-start.1
  63.4 22.1 %all-to-all-start.1 = ((bf16[8,624,128]{2,1,0:T(8,128)(2,1)}), bf16[8,624,128]{2,1,0:T(8,128)(2,1)}, u32[]{:S(2)}, u32[]{:S(2)}) async-start(bf16[8,624,128]{2,1,0:T(8,128)(2,1)} %bitcast.36), calls=%async_computation.1 | async-start | bytes 2555904 | tf_op jit(solution)/shard_map/all_to_all | solution.py:41
  132.3 38.9 %all-to-all-start.2 = ((bf16[8,624,128]{2,1,0:T(8,128)(2,1)}), bf16[8,624,128]{2,1,0:T(8,128)(2,1)}, u32[]{:S(2)}, u32[]{:S(2)}) async-start(bf16[8,624,128]{2,1,0:T(8,128)(2,1)} %bitcast.34), calls=%async_computation.2 | async-start | bytes 2555904 | tf_op jit(solution)/shard_map/all_to_all | solution.py:76
  136.6 130.2 %all-reduce.2.cloned.1.call-start = ((), (), s32[]{:S(2)}) async-start(), calls=%async_computation.3 | async-start | bytes 2588672 | tf_op jit(solution)/shard_map/psum | solution.py:90
Sparse Core Ops, SparseCore 0:
  207.4 59.3 all-reduce.1

commit v2 on v0

--- a/solution.py
+++ b/solution.py
@@ -1,7 +1,61 @@
+import functools
+
 import jax
 import jax.numpy as jnp
 from jax import lax
+from jax.experimental import pallas as pl
+from jax.experimental.pallas import tpu as pltpu
 from jax.sharding import PartitionSpec as P
+
+CHUNK = 512
+
+
+def _row_block(rows):
+    for size in range(512, 7, -8):
+        if rows % size == 0:
+            return size
+    return rows
+
+
+def _select_kernel(chunks, left_ref, right_ref, data_ref, out_ref):
+    left = left_ref[...]
+
+    def step(j, acc):
+        start = pl.multiple_of(j * CHUNK, CHUNK)
+        right = right_ref[:, pl.ds(start, CHUNK)]
+        picks = jnp.where(left == right, 1.0, 0.0).astype(data_ref.dtype)
+        block = data_ref[pl.ds(start, CHUNK), :]
+        return acc + jnp.dot(picks, block, preferred_element_type=jnp.float32)
+
+    acc = jnp.zeros(out_ref.shape, jnp.float32)
+    acc = lax.fori_loop(0, chunks, step, acc)
+    out_ref[...] = acc.astype(out_ref.dtype)
+
+
+def select_rows(left, right, data, out_dtype):
+    rows = left.shape[0]
+    count, width = data.shape
+    padded = -(-count // CHUNK) * CHUNK
+    right = jnp.pad(right, (0, padded - count), constant_values=-1).reshape(1, padded)
+    data = jnp.pad(data, ((0, padded - count), (0, 0)))
+    block = _row_block(rows)
+    return pl.pallas_call(
+        functools.partial(_select_kernel, padded // CHUNK),
+        out_shape=jax.ShapeDtypeStruct((rows, width), out_dtype),
+        grid=(rows // block,),
+        in_specs=[
+            pl.BlockSpec((block, 1), lambda i: (i, 0)),
+            pl.BlockSpec((1, padded), lambda i: (0, 0)),
+            pl.BlockSpec((padded, width), lambda i: (0, 0)),
+        ],
+        out_specs=pl.BlockSpec((block, width), lambda i: (i, 0)),
+        cost_estimate=pl.CostEstimate(
+            flops=2 * rows * padded * width,
+            transcendentals=0,
+            bytes_accessed=padded * width * data.dtype.itemsize
+            + rows * width * jnp.dtype(out_dtype).itemsize,
+        ),
+    )(left.reshape(rows, 1), right, data)
 
 
 def local(
@@ -37,11 +91,18 @@
     request = jnp.zeros((owner_count * capacity,), jnp.int32).at[buffer_place].set(local_index)
     request = request.reshape(owner_count, capacity)
     received = lax.all_to_all(request, "emb", split_axis=0, concat_axis=0, tiled=True)
-    fetched = flat_table[received]
+    slot_count = owner_count * capacity
+    received_flat = received.reshape(-1)
+    fetched = select_rows(
+        received_flat, jnp.arange(flat_table.shape[0], dtype=jnp.int32), flat_table, flat_table.dtype
+    )
     arrived = lax.all_to_all(fetched, "emb", split_axis=0, concat_axis=0, tiled=True)
-    pooled = arrived.reshape(owner_count * capacity, row_width)[buffer_place].reshape(
-        sample_count, table_count * row_width
-    )
+    pooled = select_rows(
+        buffer_place,
+        jnp.arange(slot_count, dtype=jnp.int32),
+        arrived.reshape(slot_count, row_width),
+        arrived.dtype,
+    ).reshape(sample_count, table_count * row_width)
     first = jnp.concatenate([bottom_out, pooled], axis=1)
     first_wide = first.astype(jnp.float32)
     weight_row = out_weight.astype(jnp.float32)
@@ -69,8 +130,8 @@
     input_grad = (cotangent * (gate_scale + 1.0) + back_term).astype(jnp.bfloat16)
     bottom_grad = input_grad[:, :row_width]
     row_grads = input_grad[:, row_width:].reshape(lookup_count, row_width)
-    outgoing = (
-        jnp.zeros((owner_count * capacity, row_width), jnp.bfloat16).at[buffer_place].set(row_grads)
+    outgoing = select_rows(
+        jnp.arange(slot_count, dtype=jnp.int32), buffer_place, row_grads, jnp.bfloat16
     )
     incoming = lax.all_to_all(
         outgoing.reshape(owner_count, capacity, row_width),
@@ -79,10 +140,11 @@
         concat_axis=0,
         tiled=True,
     )
-    local_grad = (
-        jnp.zeros((table_count * rows_local, row_width), jnp.float32)
-        .at[received.reshape(-1)]
-        .add(incoming.reshape(owner_count * capacity, row_width).astype(jnp.float32))
+    local_grad = select_rows(
+        jnp.arange(table_count * rows_local, dtype=jnp.int32),
+        received_flat,
+        incoming.reshape(slot_count, row_width),
+        jnp.float32,
     )
     summed_grad = lax.psum(local_grad.astype(jnp.bfloat16), "grp").astype(jnp.float32)
     table_grad = summed_grad.reshape(table_count, rows_local, row_width)

time: 245 us -> 294 us (1.20)
  Pallas kernels: 0 us -> 99 us
  other arithmetic: 56.3 us -> 28.7 us
  local copies, waits for them, and re-layouts: 71.5 us -> 53.5 us
  blocking collectives: 53 us -> 40.2 us
  starting transfers between devices: 8.73 us -> 13.7 us
  waiting for transfers between devices: 26.7 us -> 31.2 us
    pallas_call x0 -> x4, Pallas kernels: none -> 99 us  [select_rows(): pl.pallas_call(functools.partial(_select_kernel, padded // CHUNK), out_sh...]
    scatter-add x1 -> x0, other arithmetic: 29.6 us -> none  [local(): local_grad = jnp.zeros((table_count * rows_local, row_width), jnp.float32...]
    gather x2 -> x0, local copies, waits for them, and re-layouts: 21.5 us -> none  [the longest x1 12.3 us: local(): fetched = flat_table[received]]
    scatter x1 -> x0, local copies, waits for them, and re-layouts: 14.9 us -> none  [local(): jnp.zeros((owner_count * capacity, row_width), jnp.bfloat16)]
    pad x0 -> x6, local copies, waits for them, and re-layouts: none -> 10.4 us  [the longest x4 9.06 us: select_rows(): data = jnp.pad(data, ((0, padded - count), (0, 0)))]
    all_to_all x1 -> x0, blocking collectives: 9.94 us -> none  [local(): lax.all_to_all(request, 'emb', split_axis=0, concat_axis=0, tiled=True)]
    all_to_all x0 -> x1, starting transfers between devices: none -> 5.17 us  [local(): lax.all_to_all(request, 'emb', split_axis=0, concat_axis=0, tiled=True)]
    select_n x1, other arithmetic: 0.76 us -> 4.33 us  [local(): jnp.zeros((owner_count * capacity,), jnp.int32).at[buffer_place]]
  transfers between devices with their start and end apart: 3 -> 4, of which waited for: 2 -> 3; matrix products, arithmetic and copies ran while one was open for 5% -> 4% of each run, Pallas kernels for 0% -> 0%
where the time goes in v2:
time: 294 us; the launch traced here: 292 us
  Pallas kernels  99 us (34%)
  local copies, waits for them, and re-layouts  53.5 us (18%)
  blocking collectives  40.2 us (14%)
  waiting for transfers between devices  31.2 us (11%)
  other arithmetic  28.7 us (10%)
  between operations  14.1 us (5%)
  starting transfers between devices  13.7 us (5%)
  matrix products  11.6 us (4%)
    pallas_call x4, Pallas kernels, select_rows(): pl.pallas_call(functools.partial(_select_kernel, padded // CHUNK), out_sh...  99 us
    psum x1, blocking collectives, local(): bias_grad = lax.psum(bias_local, ('grp', 'emb'))  40.2 us
    all_to_all x1, waiting for transfers between devices, local(): lax.all_to_all(outgoing.reshape(owner_count, capacity, row_width), 'emb',...  15.1 us
    scatter x1, local copies, waits for them, and re-layouts, local(): jnp.zeros((owner_count * capacity,), jnp.int32).at[buffer_place]  13.4 us
    all_to_all x1, waiting for transfers between devices, local(): lax.all_to_all(fetched, 'emb', split_axis=0, concat_axis=0, tiled=True)  13.2 us
    pad x4, local copies, waits for them, and re-layouts, select_rows(): data = jnp.pad(data, ((0, padded - count), (0, 0)))  9.06 us
    another operation x2, other arithmetic  6.67 us
    dot_general x1, matrix products, local(): lax.dot_general(down_grad, cross_down, (((1,), (1,)), ((), ())), preferre...  6.07 us
  transfers between devices with their start and end apart: 4, of which 3 were waited for; matrix products, arithmetic and copies ran while one was open for 4% of the time, Pallas kernels for 0%

profile of v2, /device:TPU:0, one launch (start us, length us, event | category | flops | bytes accessed | tf_op | source)
XLA Modules:
  0.0 291.9 jit_solution(13950631728745582882)
XLA Ops:
  7.2 0.0 copy-start
  7.2 0.5 iota_multiply_fusion
  7.7 1.6 fusion.18
  9.3 0.0 copy-start.1
  9.3 0.7 fusion.13
  9.9 5.2 %reduce-window.6 = s32[8,26,128]{2,1,0:T(8,128)} reduce-window(s32[8,26,128]{2,1,0:T(8,128)} %fusion.13, s32[]{:T(128)} %constant.10.clone.1), window={size=1x1x128 pad=0_0x0_0x127_0}, to_apply=%region_0.0 | reduce-window | flops 3381248 | bytes 212996 | tf_op jit(solution)/shard_map/reduce-window
  15.2 1.8 slice_reduce_fusion
  17.0 1.5 reduce-window.9
  18.4 1.0 add_bitcast_fusion
  19.4 0.7 fusion.15
  20.1 2.5 copy.31
  22.6 1.4 broadcast_add_fusion
  24.0 1.4 copy.33
  25.4 1.6 reshape.98
  27.0 4.3 %fusion.5 = (s32[3328]{0:T(1024)}, s32[3328,1]{1,0:T(8,128)}) fusion(s32[3328,1]{1,0:T(8,128)} %copy.31, s32[3328]{0:T(1024)} %fusion.15), kind=kLoop, calls=%fused_computation.12 | loop fusion | flops 13312 | bytes 53248 | tf_op jit(solution)/shard_map/select_n | solution.py:91
  31.4 0.0 copy-done.1
  31.4 13.4 %scatter_custom_fusion = s32[4992]{0:T(1024)} fusion(s32[3328]{0:T(1024)} %get-tuple-element.3, s32[3328]{0:T(1024)} %reshape.98, s32[]{:T(128)} %constant.10.clone.1), kind=kCustom, calls=%fused_computation.27 | custom fusion | bytes 20480 | tf_op jit(solution)/shard_map/scatter | solution.py:91
  44.8 1.4 all_to_all.17
  46.2 5.2 %all-to-all-start = ((s32[8,1,624]{2,1,0:T(1,128)}), s32[8,1,624]{2,1,0:T(1,128)}, u32[]{:S(2)}, u32[]{:S(2)}) async-start(s32[8,1,624]{2,1,0:T(1,128)} %all_to_all.17), calls=%async_computation | async-start | bytes 40960 | tf_op jit(solution)/shard_map/all_to_all | solution.py:93
  51.4 2.0 pad.28.data_ref
  53.4 2.9 all-to-all-done
  56.3 1.4 reduce.4
  57.7 3.4 %reshape_reshape.5.left_ref = s32[4992,1]{1,0:T(8,128)} reshape(s32[8,624]{1,0:T(8,128)} %reduce.4) | data formatting | bytes 39936 | tf_op jit(solution)/shard_map/reshape;reshape | solution.py:58
  61.1 21.3 %shard_map.130 = bf16[4992,128]{1,0:T(8,128)(2,1)} custom-call(s32[4992,1]{1,0:T(8,128)} %reshape_reshape.5.left_ref, s32[1,2560]{1,0:T(1,128)} %constant.29.clone.1.right_ref, bf16[2560,128]{1,0:T(8,128)(2,1)} %pad.28.data_ref), custom_call_target="tpu_custom_call" | custom-call | flops 3271557120 | bytes 1933312 | tf_op jit(solution)/shard_map/pallas_call | solution.py:42
  82.4 4.3 %all-to-all-start.1 = ((bf16[8,624,128]{2,1,0:T(8,128)(2,1)}), bf16[8,624,128]{2,1,0:T(8,128)(2,1)}, u32[]{:S(2)}, u32[]{:S(2)}) async-start(bf16[8,624,128]{2,1,0:T(8,128)(2,1)} %bitcast.29), calls=%async_computation.1 | async-start | bytes 2555904 | tf_op jit(solution)/shard_map/all_to_all | solution.py:99
  86.7 0.7 convert_element_type.41
  87.4 0.7 multiply_add_fusion.1
  88.1 0.6 reshape.86.right_ref
  88.7 1.4 constant_dynamic-update-slice_fusion.1
  90.1 1.3 select_reduce_fusion
  91.3 13.2 %all-to-all-done.1 = bf16[8,624,128]{2,1,0:T(8,128)(2,1)} async-done(((bf16[8,624,128]{2,1,0:T(8,128)(2,1)}), bf16[8,624,128]{2,1,0:T(8,128)(2,1)}, u32[]{:S(2)}, u32[]{:S(2)}) %all-to-all-start.1) | async-done | bytes 1277984 | tf_op jit(solution)/shard_map/all_to_all | solution.py:99
  104.5 2.5 pad.29.data_ref
  107.0 27.7 %shard_map.131 = bf16[3328,128]{1,0:T(8,128)(2,1)} custom-call(s32[3328,1]{1,0:T(8,128)} %get-tuple-element.4.left_ref, s32[1,5120]{1,0:T(1,128)} %constant.28.clone.1.right_ref, bf16[5120,128]{1,0:T(8,128)(2,1)} %pad.29.data_ref), custom_call_target="tpu_custom_call" | custom-call | flops 4362076160 | bytes 2162688 | tf_op jit(solution)/shard_map/pallas_call | solution.py:42
  134.7 2.8 reshape.88
  137.4 2.1 constant_dynamic-update-slice_fusion
  139.6 0.0 copy-done
  139.6 5.6 %fusion.4 = (f32[128]{0:T(128)}, f32[128,3456]{1,0:T(8,128)}) fusion(bf16[128,3456]{1,0:T(8,128)(2,1)} %constant_dynamic-update-slice_fusion, f32[3456]{0:T(1024)S(1)} %convert_element_type.41, f32[3456]{0:T(1024)} %param.19, bf16[512,3456]{1,0:T(8,128)(2,1)} %param.18, bf16[3456,512]{1,0:T(8,128)(2,1)S(1)} %copy-done), kind=kOutput, calls=%fused_computation.11 | convolution fusion | flops 908689280 | bytes 9760256 | tf_op jit(solution)/shard_map/dot_general | solution.py:110
  145.1 1.2 divide_subtract_fusion
  146.3 6.1 %fusion = bf16[128,3456]{1,0:T(8,128)(2,1)} fusion(bf16[3456,512]{1,0:T(8,128)(2,1)S(1)} %copy-done, f32[128,3456]{1,0:T(8,128)} %get-tuple-element.8, bf16[512,3456]{1,0:T(8,128)(2,1)} %param.18, bf16[128,3456]{1,0:T(8,128)(2,1)} %constant_dynamic-update-slice_fusion, f32[128]{0:T(128)} %divide_subtract_fusion, f32[3456]{0:T(1024)S(1)} %convert_element_type.41), kind=kOutput, calls=%fused_computation.4 | convolution fusion | flops 910016512 | bytes 10631168 | tf_op jit(solution)/shard_map/dot_general | solution.py:127
  152.4 2.1 slice.17
  154.5 2.9 reshape.89
  157.4 2.1 pad.30.data_ref
  159.5 1.7 iota.29.left_ref
  161.2 28.7 %shard_map.132 = bf16[4992,128]{1,0:T(8,128)(2,1)} custom-call(s32[4992,1]{1,0:T(8,128)} %iota.29.left_ref, s32[1,3584]{1,0:T(1,128)} %reshape.86.right_ref, bf16[3584,128]{1,0:T(8,128)(2,1)} %pad.30.data_ref), custom_call_target="tpu_custom_call" | custom-call | flops 4580179968 | bytes 2195456 | tf_op jit(solution)/shard_map/pallas_call | solution.py:42
  190.0 4.3 %all-to-all-start.2 = ((bf16[8,624,128]{2,1,0:T(8,128)(2,1)}), bf16[8,624,128]{2,1,0:T(8,128)(2,1)}, u32[]{:S(2)}, u32[]{:S(2)}) async-start(bf16[8,624,128]{2,1,0:T(8,128)(2,1)} %bitcast.30), calls=%async_computation.2 | async-start | bytes 2555904 | tf_op jit(solution)/shard_map/all_to_all | solution.py:136
  194.2 0.0 all-reduce.8.cloned.1.call-start
  194.3 1.4 reshape.84
  195.7 1.3 pad.26
  197.0 15.1 %all-to-all-done.2 = bf16[8,624,128]{2,1,0:T(8,128)(2,1)} async-done(((bf16[8,624,128]{2,1,0:T(8,128)(2,1)}), bf16[8,624,128]{2,1,0:T(8,128)(2,1)}, u32[]{:S(2)}, u32[]{:S(2)}) %all-to-all-start.2) | async-done | bytes 1277984 | tf_op jit(solution)/shard_map/all_to_all | solution.py:136
  212.1 2.5 pad.31.data_ref
  214.6 1.1 iota.27.left_ref
  215.7 21.2 %shard_map.133 = f32[2496,128]{1,0:T(8,128)} custom-call(s32[2496,1]{1,0:T(8,128)} %iota.27.left_ref, s32[1,5120]{1,0:T(1,128)} %bitcast.33, bf16[5120,128]{1,0:T(8,128)(2,1)} %pad.31.data_ref), custom_call_target="tpu_custom_call" | custom-call | flops 3271557120 | bytes 2588672 | tf_op jit(solution)/shard_map/pallas_call | solution.py:42
  236.9 2.2 convert_element_type.46
  239.1 0.0 all-reduce.8.cloned.1.call-update
  239.1 1.4 slice.18
  240.5 2.1 fusion.1
  242.6 40.2 %psum.15 = f32[3456]{0:T(1024)} all-reduce(f32[3456]{0:T(1024)} %fusion.1), channel_id=1, replica_groups=mesh['grp'=4,'emb'=8] {'grp','emb'}, use_global_device_ids=true, to_apply=%region_8.9 | all-reduce | flops 3456 | bytes 27648 | tf_op jit(solution)/shard_map/psum | solution.py:152
  282.8 0.0 all-reduce.8.cloned.1.call-done
  282.8 2.3 reshape.93
  (1 shorter events, 0.0 us)
Async XLA Ops:
  7.2 132.4 %copy-start = (bf16[3456,512]{1,0:T(8,128)(2,1)S(1)}, bf16[3456,512]{1,0:T(8,128)(2,1)}, u32[]{:S(2)}) copy-start(bf16[3456,512]{1,0:T(8,128)(2,1)} %param.17) | copy-start | bytes 10616836
  9.3 22.1 %copy-start.1 = (s32[3328]{0:T(1024)}, s32[3328]{0:T(1024)S(1)}, u32[]{:S(2)}) copy-start(s32[3328]{0:T(1024)S(1)} %get-tuple-element.5) | copy-start | bytes 39940
  46.2 10.1 %all-to-all-start = ((s32[8,1,624]{2,1,0:T(1,128)}), s32[8,1,624]{2,1,0:T(1,128)}, u32[]{:S(2)}, u32[]{:S(2)}) async-start(s32[8,1,624]{2,1,0:T(1,128)} %all_to_all.17), calls=%async_computation | async-start | bytes 40960 | tf_op jit(solution)/shard_map/all_to_all | solution.py:93
  82.4 22.1 %all-to-all-start.1 = ((bf16[8,624,128]{2,1,0:T(8,128)(2,1)}), bf16[8,624,128]{2,1,0:T(8,128)(2,1)}, u32[]{:S(2)}, u32[]{:S(2)}) async-start(bf16[8,624,128]{2,1,0:T(8,128)(2,1)} %bitcast.29), calls=%async_computation.1 | async-start | bytes 2555904 | tf_op jit(solution)/shard_map/all_to_all | solution.py:99
  190.0 22.1 %all-to-all-start.2 = ((bf16[8,624,128]{2,1,0:T(8,128)(2,1)}), bf16[8,624,128]{2,1,0:T(8,128)(2,1)}, u32[]{:S(2)}, u32[]{:S(2)}) async-start(bf16[8,624,128]{2,1,0:T(8,128)(2,1)} %bitcast.30), calls=%async_computation.2 | async-start | bytes 2555904 | tf_op jit(solution)/shard_map/all_to_all | solution.py:136
  194.2 88.6 %all-reduce.8.cloned.1.call-start = ((), (), s32[]{:S(2)}) async-start(), calls=%async_computation.3 | async-start | bytes 1277952 | tf_op jit(solution)/shard_map/psum | solution.py:149
Sparse Core Ops, SparseCore 0:
  239.3 40.0 all-reduce.7

commit v3 on v2

--- a/solution.py
+++ b/solution.py
@@ -11,7 +11,9 @@
 
 
 def _row_block(rows):
-    for size in range(512, 7, -8):
+    if rows <= 4096:
+        return rows
+    for size in range(4096, 7, -8):
         if rows % size == 0:
             return size
     return rows
@@ -30,6 +32,19 @@
     acc = jnp.zeros(out_ref.shape, jnp.float32)
     acc = lax.fori_loop(0, chunks, step, acc)
     out_ref[...] = acc.astype(out_ref.dtype)
+
+
+def _running_count(marks):
+    count, width = marks.shape
+    block = 128 if count % 128 == 0 else count
+    grouped = marks.reshape(count // block, block, width).astype(jnp.bfloat16)
+    lower = (
+        jnp.arange(block, dtype=jnp.int32)[:, None] >= jnp.arange(block, dtype=jnp.int32)[None, :]
+    ).astype(jnp.bfloat16)
+    within = jnp.einsum("rc,bcj->brj", lower, grouped, preferred_element_type=jnp.float32)
+    totals = within[:, -1, :]
+    before = jnp.cumsum(totals, axis=0) - totals
+    return (within + before[:, None, :]).reshape(count, width).astype(jnp.int32)
 
 
 def select_rows(left, right, data, out_dtype):
@@ -84,7 +99,7 @@
     owner_marks = (flat_owner[:, None] == jnp.arange(owner_count, dtype=jnp.int32)[None, :]).astype(
         jnp.int32
     )
-    ranking = jnp.cumsum(owner_marks, axis=0) - 1
+    ranking = _running_count(owner_marks) - 1
     slot_index = jnp.sum(ranking * owner_marks, axis=1)
     buffer_place = flat_owner * capacity + slot_index
     flat_table = tables.reshape(table_count * rows_local, row_width)
@@ -93,16 +108,11 @@
     received = lax.all_to_all(request, "emb", split_axis=0, concat_axis=0, tiled=True)
     slot_count = owner_count * capacity
     received_flat = received.reshape(-1)
-    fetched = select_rows(
-        received_flat, jnp.arange(flat_table.shape[0], dtype=jnp.int32), flat_table, flat_table.dtype
+    fetched = flat_table[received]
+    arrived = lax.all_to_all(fetched, "emb", split_axis=0, concat_axis=0, tiled=True)
+    pooled = arrived.reshape(slot_count, row_width)[buffer_place].reshape(
+        sample_count, table_count * row_width
     )
-    arrived = lax.all_to_all(fetched, "emb", split_axis=0, concat_axis=0, tiled=True)
-    pooled = select_rows(
-        buffer_place,
-        jnp.arange(slot_count, dtype=jnp.int32),
-        arrived.reshape(slot_count, row_width),
-        arrived.dtype,
-    ).reshape(sample_count, table_count * row_width)
     first = jnp.concatenate([bottom_out, pooled], axis=1)
     first_wide = first.astype(jnp.float32)
     weight_row = out_weight.astype(jnp.float32)
@@ -130,9 +140,7 @@
     input_grad = (cotangent * (gate_scale + 1.0) + back_term).astype(jnp.bfloat16)
     bottom_grad = input_grad[:, :row_width]
     row_grads = input_grad[:, row_width:].reshape(lookup_count, row_width)
-    outgoing = select_rows(
-        jnp.arange(slot_count, dtype=jnp.int32), buffer_place, row_grads, jnp.bfloat16
-    )
+    outgoing = jnp.zeros((slot_count, row_width), jnp.bfloat16).at[buffer_place].set(row_grads)
     incoming = lax.all_to_all(
         outgoing.reshape(owner_count, capacity, row_width),
         "emb",

time: 294 us -> 234 us (0.80)
  Pallas kernels: 99 us -> 13 us
  local copies, waits for them, and re-layouts: 53.5 us -> 82.7 us
  blocking collectives: 40.2 us -> 50 us
  other arithmetic: 28.7 us -> 23 us
  starting transfers between devices: 13.7 us -> 8.74 us
  waiting for transfers between devices: 31.2 us -> 26.7 us
    pallas_call x4 -> x1, Pallas kernels: 99 us -> 13 us  [select_rows(): pl.pallas_call(functools.partial(_select_kernel, padded // CHUNK), out_sh...]
    gather x0 -> x2, local copies, waits for them, and re-layouts: none -> 21.5 us  [the longest x1 12.3 us: local(): fetched = flat_table[received]]
    scatter x0 -> x1, local copies, waits for them, and re-layouts: none -> 14.9 us  [local(): jnp.zeros((slot_count, row_width), jnp.bfloat16).at[buffer_place]]
    all_to_all x0 -> x1, blocking collectives: none -> 9.94 us  [local(): lax.all_to_all(request, 'emb', split_axis=0, concat_axis=0, tiled=True)]
    pad x4 -> x1, local copies, waits for them, and re-layouts: 9.06 us -> 2.45 us  [select_rows(): data = jnp.pad(data, ((0, padded - count), (0, 0)))]
    another operation x2 -> x1, other arithmetic: 6.67 us -> 0.63 us  [_running_count(): before = jnp.cumsum(totals, axis=0) - totals]
    all_to_all x1 -> x0, starting transfers between devices: 5.17 us -> none  [local(): lax.all_to_all(request, 'emb', split_axis=0, concat_axis=0, tiled=True)]
    select_n x1, other arithmetic: 4.33 us -> 1.39 us  [local(): jnp.zeros((owner_count * capacity,), jnp.int32).at[buffer_place]]
  transfers between devices with their start and end apart: 4 -> 3, of which waited for: 3 -> 2; matrix products, arithmetic and copies ran while one was open for 4% -> 5% of each run, Pallas kernels for 0% -> 0%
where the time goes in v3:
time: 234 us; the launch traced here: 232 us
  local copies, waits for them, and re-layouts  82.7 us (35%)
  blocking collectives  50 us (21%)
  waiting for transfers between devices  26.7 us (11%)
  other arithmetic  23 us (10%)
  between operations  14.1 us (6%)
  matrix products  13.2 us (6%)
  Pallas kernels  13 us (6%)
  starting transfers between devices  8.74 us (4%)
    psum x1, blocking collectives, local(): bias_grad = lax.psum(bias_local, ('grp', 'emb'))  40.1 us
    scatter x1, local copies, waits for them, and re-layouts, local(): jnp.zeros((slot_count, row_width), jnp.bfloat16).at[buffer_place]  14.9 us
    all_to_all x1, waiting for transfers between devices, local(): lax.all_to_all(outgoing.reshape(owner_count, capacity, row_width), 'emb',...  13.5 us
    scatter x1, local copies, waits for them, and re-layouts, local(): jnp.zeros((owner_count * capacity,), jnp.int32).at[buffer_place]  13.4 us
    all_to_all x1, waiting for transfers between devices, local(): lax.all_to_all(fetched, 'emb', split_axis=0, concat_axis=0, tiled=True)  13.2 us
    pallas_call x1, Pallas kernels, select_rows(): pl.pallas_call(functools.partial(_select_kernel, padded // CHUNK), out_sh...  13 us
    gather x1, local copies, waits for them, and re-layouts, local(): fetched = flat_table[received]  12.3 us
    all_to_all x1, blocking collectives, local(): lax.all_to_all(request, 'emb', split_axis=0, concat_axis=0, tiled=True)  9.94 us
  transfers between devices with their start and end apart: 3, of which 2 were waited for; matrix products, arithmetic and copies ran while one was open for 5% of the time, Pallas kernels for 0%

profile of v3, /device:TPU:0, one launch (start us, length us, event | category | flops | bytes accessed | tf_op | source)
XLA Modules:
  0.0 231.6 jit_solution(9310627740400118748)
XLA Ops:
  7.2 0.0 copy-start
  7.2 0.5 iota_multiply_fusion
  7.7 1.0 reduce.1
  8.7 0.7 copy.38
  9.4 0.8 broadcast_add_fusion
  10.2 0.7 copy.44
  11.0 1.6 reshape.138
  12.5 1.6 convert_convert_fusion
  14.1 1.8 copy.39
  15.9 1.6 fusion.15
  17.5 1.9 copy.40
  19.4 1.3 slice.16
  20.7 0.8 copy.41
  21.5 0.6 fusion.21
  22.1 0.8 copy.42
  22.9 0.7 subtract_bitcast_fusion
  23.6 1.9 select_reduce_fusion
  25.5 0.9 copy.43
  26.4 1.4 fusion.18
  27.8 13.4 %scatter_custom_fusion = s32[4992]{0:T(1024)} fusion(s32[3328]{0:T(1024)} %fusion.18, s32[3328]{0:T(1024)} %reshape.138, s32[]{:T(128)} %constant.9.clone.1), kind=kCustom, calls=%fused_computation.33 | custom fusion | bytes 20480 | tf_op jit(solution)/shard_map/scatter | solution.py:106
  41.3 1.4 all_to_all.14
  42.7 9.9 %all_to_all.22 = s32[8,1,624]{2,1,0:T(1,128)S(1)} all-to-all(s32[8,1,624]{2,1,0:T(1,128)} %all_to_all.14), channel_id=1, replica_groups=mesh['grp'=4,'emb'=8] {'emb'}, dimensions={0} | all-to-all | bytes 39936 | tf_op jit(solution)/shard_map/all_to_all | solution.py:108
  52.6 0.0 copy-start.1
  52.6 0.6 copy-done.1
  53.3 0.7 fusion.17
  53.9 1.4 reshape.120
  55.3 1.3 pad_clamp_fusion
  56.7 12.3 %gather_fusion = bf16[4992,128]{1,0:T(8,128)(2,1)} fusion(bf16[2496,128]{1,0:T(8,128)(2,1)} %bitcast.33, s32[5120]{0:T(1024)} %pad_clamp_fusion), kind=kCustom, calls=%fused_computation | custom fusion | bytes 2575872 | tf_op jit(solution)/shard_map/gather | solution.py:111
  68.9 4.3 %all-to-all-start.1 = ((bf16[8,624,128]{2,1,0:T(8,128)(2,1)}), bf16[8,624,128]{2,1,0:T(8,128)(2,1)}, u32[]{:S(2)}, u32[]{:S(2)}) async-start(bf16[8,624,128]{2,1,0:T(8,128)(2,1)} %bitcast.35), calls=%async_computation.1 | async-start | bytes 2555904 | tf_op jit(solution)/shard_map/all_to_all | solution.py:112
  73.2 0.7 convert_element_type.45
  73.9 1.3 pad_clamp_fusion.1
  75.2 1.4 constant_dynamic-update-slice_fusion.1
  76.6 1.3 select_reduce_fusion.1
  77.9 13.2 %all-to-all-done.1 = bf16[8,624,128]{2,1,0:T(8,128)(2,1)} async-done(((bf16[8,624,128]{2,1,0:T(8,128)(2,1)}), bf16[8,624,128]{2,1,0:T(8,128)(2,1)}, u32[]{:S(2)}, u32[]{:S(2)}) %all-to-all-start.1) | async-done | bytes 1277984 | tf_op jit(solution)/shard_map/all_to_all | solution.py:112
  91.1 9.2 %gather_fusion.1 = bf16[3328,128]{1,0:T(8,128)(2,1)} fusion(bf16[4992,128]{1,0:T(8,128)(2,1)} %bitcast.7, s32[4096]{0:T(1024)} %pad_clamp_fusion.1), kind=kCustom, calls=%fused_computation.1 | custom fusion | bytes 1717248 | tf_op jit(solution)/shard_map/gather | solution.py:113
  100.3 2.8 %reshape.112 = bf16[128,3328]{1,0:T(8,128)(2,1)} reshape(bf16[3328,128]{1,0:T(8,128)(2,1)} %gather_fusion.1) | data formatting | bytes 1703936 | tf_op jit(solution)/shard_map/reshape | solution.py:113
  103.1 2.1 constant_dynamic-update-slice_fusion
  105.2 0.0 copy-done
  105.2 5.6 %fusion.4 = (f32[128]{0:T(128)}, f32[128,3456]{1,0:T(8,128)}) fusion(bf16[128,3456]{1,0:T(8,128)(2,1)} %constant_dynamic-update-slice_fusion, f32[3456]{0:T(1024)S(1)} %convert_element_type.45, f32[3456]{0:T(1024)} %param.19, bf16[512,3456]{1,0:T(8,128)(2,1)} %param.18, bf16[3456,512]{1,0:T(8,128)(2,1)S(1)} %copy-done), kind=kOutput, calls=%fused_computation.13 | convolution fusion | flops 908689280 | bytes 9760256 | tf_op jit(solution)/shard_map/dot_general | solution.py:120
  110.8 1.2 divide_subtract_fusion
  112.0 6.1 %fusion = bf16[128,3456]{1,0:T(8,128)(2,1)} fusion(bf16[3456,512]{1,0:T(8,128)(2,1)S(1)} %copy-done, f32[128,3456]{1,0:T(8,128)} %get-tuple-element.4, bf16[512,3456]{1,0:T(8,128)(2,1)} %param.18, bf16[128,3456]{1,0:T(8,128)(2,1)} %constant_dynamic-update-slice_fusion, f32[128]{0:T(128)} %divide_subtract_fusion, f32[3456]{0:T(1024)S(1)} %convert_element_type.45), kind=kOutput, calls=%fused_computation.6 | convolution fusion | flops 910016512 | bytes 10631168 | tf_op jit(solution)/shard_map/dot_general | solution.py:137
  118.1 2.1 slice.17
  120.2 2.9 %reshape.146 = bf16[3328,128]{1,0:T(8,128)(2,1)} reshape(bf16[128,3328]{1,0:T(8,128)(2,1)} %slice.17) | data formatting | bytes 1703936 | tf_op jit(solution)/shard_map/reshape | solution.py:142
  123.0 14.9 %scatter_custom_fusion.1 = bf16[4992,128]{1,0:T(8,128)(2,1)} fusion(s32[3328]{0:T(1024)} %fusion.18, bf16[3328,128]{1,0:T(8,128)(2,1)} %reshape.146, bf16[]{:T(256)} %constant.6.clone.1), kind=kCustom, calls=%fused_computation.18 | custom fusion | bytes 1278464 | tf_op jit(solution)/shard_map/scatter | solution.py:143
  137.9 4.3 %all-to-all-start.2 = ((bf16[8,624,128]{2,1,0:T(8,128)(2,1)}), bf16[8,624,128]{2,1,0:T(8,128)(2,1)}, u32[]{:S(2)}, u32[]{:S(2)}) async-start(bf16[8,624,128]{2,1,0:T(8,128)(2,1)} %bitcast.34), calls=%async_computation.2 | async-start | bytes 2555904 | tf_op jit(solution)/shard_map/all_to_all | solution.py:144
  142.2 0.2 all-reduce.4.cloned.1.call-start
  142.4 1.4 reduce.3
  143.8 1.4 reshape.108
  145.2 1.3 pad.8
  146.5 13.5 %all-to-all-done.2 = bf16[8,624,128]{2,1,0:T(8,128)(2,1)} async-done(((bf16[8,624,128]{2,1,0:T(8,128)(2,1)}), bf16[8,624,128]{2,1,0:T(8,128)(2,1)}, u32[]{:S(2)}, u32[]{:S(2)}) %all-to-all-start.2) | async-done | bytes 1277984 | tf_op jit(solution)/shard_map/all_to_all | solution.py:144
  160.1 2.5 %pad.9.data_ref = bf16[5120,128]{1,0:T(8,128)(2,1)} pad(bf16[4992,128]{1,0:T(8,128)(2,1)} %bitcast.9, bf16[]{:T(256)} %constant.6.clone.1), padding=0_128x0_0 | pad | bytes 2588674 | tf_op jit(solution)/shard_map/jit(_pad)/pad | solution.py:55
  162.5 1.1 iota.32.left_ref
  163.6 13.0 %shard_map.130 = f32[2496,128]{1,0:T(8,128)} custom-call(s32[2496,1]{1,0:T(8,128)} %iota.32.left_ref, s32[1,5120]{1,0:T(1,128)} %bitcast.41, bf16[5120,128]{1,0:T(8,128)(2,1)} %pad.9.data_ref), custom_call_target="tpu_custom_call" | custom-call | flops 3271557120 | bytes 2588672 | tf_op jit(solution)/shard_map/pallas_call | solution.py:57
  176.7 2.2 convert_element_type.50
  178.9 0.0 all-reduce.4.cloned.1.call-update
  178.9 1.4 slice.18
  180.3 2.1 fusion.1
  182.4 40.1 %psum.15 = f32[3456]{0:T(1024)} all-reduce(f32[3456]{0:T(1024)} %fusion.1), channel_id=1, replica_groups=mesh['grp'=4,'emb'=8] {'grp','emb'}, use_global_device_ids=true, to_apply=%region_8.9 | all-reduce | flops 3456 | bytes 27648 | tf_op jit(solution)/shard_map/psum | solution.py:160
  222.4 0.0 all-reduce.4.cloned.1.call-done
  222.4 2.3 reshape.117
Async XLA Ops:
  7.2 98.0 %copy-start = (bf16[3456,512]{1,0:T(8,128)(2,1)S(1)}, bf16[3456,512]{1,0:T(8,128)(2,1)}, u32[]{:S(2)}) copy-start(bf16[3456,512]{1,0:T(8,128)(2,1)} %param.17) | copy-start | bytes 10616836
  52.6 0.6 copy-start.1
  68.9 22.1 %all-to-all-start.1 = ((bf16[8,624,128]{2,1,0:T(8,128)(2,1)}), bf16[8,624,128]{2,1,0:T(8,128)(2,1)}, u32[]{:S(2)}, u32[]{:S(2)}) async-start(bf16[8,624,128]{2,1,0:T(8,128)(2,1)} %bitcast.35), calls=%async_computation.1 | async-start | bytes 2555904 | tf_op jit(solution)/shard_map/all_to_all | solution.py:112
  137.9 22.2 %all-to-all-start.2 = ((bf16[8,624,128]{2,1,0:T(8,128)(2,1)}), bf16[8,624,128]{2,1,0:T(8,128)(2,1)}, u32[]{:S(2)}, u32[]{:S(2)}) async-start(bf16[8,624,128]{2,1,0:T(8,128)(2,1)} %bitcast.34), calls=%async_computation.2 | async-start | bytes 2555904 | tf_op jit(solution)/shard_map/all_to_all | solution.py:144
  142.2 80.3 %all-reduce.4.cloned.1.call-start = ((), (), s32[]{:S(2)}) async-start(), calls=%async_computation.3 | async-start | bytes 1277952 | tf_op jit(solution)/shard_map/psum | solution.py:157
Sparse Core Ops, SparseCore 0:
  179.0 39.9 all-reduce.3

commit v4 on v3

--- a/solution.py
+++ b/solution.py
@@ -32,6 +32,44 @@
     acc = jnp.zeros(out_ref.shape, jnp.float32)
     acc = lax.fori_loop(0, chunks, step, acc)
     out_ref[...] = acc.astype(out_ref.dtype)
+
+
+def _slot_kernel(capacity, table_count, rows_local, owner_ref, row_ref, place_ref, request_ref, count_ref):
+    owner_count = count_ref.shape[0]
+    for owner in range(owner_count):
+        count_ref[owner] = 0
+
+    def clear(slot, carry):
+        request_ref[slot] = 0
+        return carry
+
+    lax.fori_loop(0, request_ref.shape[0], clear, 0)
+
+    def assign(lookup, carry):
+        owner = owner_ref[lookup]
+        taken = count_ref[owner]
+        slot = owner * capacity + taken
+        count_ref[owner] = taken + 1
+        place_ref[lookup] = slot
+        request_ref[slot] = (lookup % table_count) * rows_local + row_ref[lookup]
+        return carry
+
+    lax.fori_loop(0, owner_ref.shape[0], assign, 0)
+
+
+def assign_slots(owners, rows, owner_count, capacity, table_count, rows_local):
+    lookups = owners.shape[0]
+    smem = pltpu.SMEM
+    return pl.pallas_call(
+        functools.partial(_slot_kernel, capacity, table_count, rows_local),
+        out_shape=(
+            jax.ShapeDtypeStruct((lookups,), jnp.int32),
+            jax.ShapeDtypeStruct((owner_count * capacity,), jnp.int32),
+        ),
+        in_specs=[pl.BlockSpec(memory_space=smem), pl.BlockSpec(memory_space=smem)],
+        out_specs=(pl.BlockSpec(memory_space=smem), pl.BlockSpec(memory_space=smem)),
+        scratch_shapes=[pltpu.SMEM((owner_count,), jnp.int32)],
+    )(owners, rows)
 
 
 def _running_count(marks):
@@ -92,18 +130,15 @@
     owner_count = lax.axis_size("emb")
     capacity = 3 * sample_count * table_count // (2 * owner_count)
     lookup_count = sample_count * table_count
-    owners = owner_ids.reshape(sample_count, table_count)
-    flat_owner = owners.reshape(-1)
-    local_grid = jnp.arange(table_count, dtype=jnp.int32)[None, :] * rows_local + row_ids
-    local_index = local_grid.reshape(-1)
-    owner_marks = (flat_owner[:, None] == jnp.arange(owner_count, dtype=jnp.int32)[None, :]).astype(
-        jnp.int32
-    )
-    ranking = _running_count(owner_marks) - 1
-    slot_index = jnp.sum(ranking * owner_marks, axis=1)
-    buffer_place = flat_owner * capacity + slot_index
+    buffer_place, request = assign_slots(
+        owner_ids.reshape(-1),
+        row_ids.reshape(-1),
+        owner_count,
+        capacity,
+        table_count,
+        rows_local,
+    )
     flat_table = tables.reshape(table_count * rows_local, row_width)
-    request = jnp.zeros((owner_count * capacity,), jnp.int32).at[buffer_place].set(local_index)
     request = request.reshape(owner_count, capacity)
     received = lax.all_to_all(request, "emb", split_axis=0, concat_axis=0, tiled=True)
     slot_count = owner_count * capacity

time: 234 us -> 280 us (1.20)
  Pallas kernels: 13 us -> 88.7 us
  local copies, waits for them, and re-layouts: 82.7 us -> 62.6 us
  other arithmetic: 23 us -> 15.8 us
    pallas_call x0 -> x1, Pallas kernels: none -> 75.7 us  [assign_slots(): pl.pallas_call(functools.partial(_slot_kernel, capacity, table_count, row...]
    scatter x1 -> x0, local copies, waits for them, and re-layouts: 13.4 us -> none  [local(): jnp.zeros((owner_count * capacity,), jnp.int32).at[buffer_place]]
  transfers between devices with their start and end apart: 3 -> 3, of which waited for: 2 -> 2; matrix products, arithmetic and copies ran while one was open for 5% -> 4% of each run, Pallas kernels for 0% -> 0%
where the time goes in v4:
time: 280 us; the launch traced here: 278 us
  Pallas kernels  88.7 us (32%)
  local copies, waits for them, and re-layouts  62.6 us (22%)
  blocking collectives  50 us (18%)
  waiting for transfers between devices  26.3 us (9%)
  other arithmetic  15.8 us (6%)
  between operations  14.1 us (5%)
  matrix products  11.6 us (4%)
  starting transfers between devices  8.56 us (3%)
    pallas_call x1, Pallas kernels, assign_slots(): pl.pallas_call(functools.partial(_slot_kernel, capacity, table_count, row...  75.7 us
    psum x1, blocking collectives, local(): bias_grad = lax.psum(bias_local, ('grp', 'emb'))  40.1 us
    scatter x1, local copies, waits for them, and re-layouts, local(): jnp.zeros((slot_count, row_width), jnp.bfloat16).at[buffer_place]  14.9 us
    all_to_all x1, waiting for transfers between devices, local(): lax.all_to_all(outgoing.reshape(owner_count, capacity, row_width), 'emb',...  13.7 us
    pallas_call x1, Pallas kernels, select_rows(): pl.pallas_call(functools.partial(_select_kernel, padded // CHUNK), out_sh...  13 us
    all_to_all x1, waiting for transfers between devices, local(): lax.all_to_all(fetched, 'emb', split_axis=0, concat_axis=0, tiled=True)  12.6 us
    gather x1, local copies, waits for them, and re-layouts, local(): fetched = flat_table[received]  12.3 us
    all_to_all x1, blocking collectives, local(): lax.all_to_all(request, 'emb', split_axis=0, concat_axis=0, tiled=True)  9.94 us
  transfers between devices with their start and end apart: 3, of which 2 were waited for; matrix products, arithmetic and copies ran while one was open for 4% of the time, Pallas kernels for 0%

profile of v4, /device:TPU:0, one launch (start us, length us, event | category | flops | bytes accessed | tf_op | source)
XLA Modules:
  0.0 277.7 jit_solution(11903012113288561600)
XLA Ops:
  7.2 0.0 copy-start
  7.2 1.6 copy.15
  8.8 1.6 reshape.82.row_ref
  10.3 1.3 reduce.owner_ref
  11.7 75.7 %shard_map.130 = (s32[3328]{0:T(1024)}, s32[4992]{0:T(1024)}) custom-call(s32[3328]{0:T(1024)} %reduce.owner_ref, s32[3328]{0:T(1024)} %reshape.82.row_ref), custom_call_target="tpu_custom_call" | custom-call | tf_op jit(solution)/shard_map/pallas_call | solution.py:63
  87.4 1.4 all_to_all.14
  88.9 9.9 %all_to_all.22 = s32[8,1,624]{2,1,0:T(1,128)S(1)} all-to-all(s32[8,1,624]{2,1,0:T(1,128)} %all_to_all.14), channel_id=1, replica_groups=mesh['grp'=4,'emb'=8] {'emb'}, dimensions={0} | all-to-all | bytes 39936 | tf_op jit(solution)/shard_map/all_to_all | solution.py:143
  98.8 0.0 copy-start.1
  98.8 0.6 copy-done.1
  99.4 0.7 fusion.14
  100.1 1.4 reshape.95
  101.5 1.3 pad_clamp_fusion
  102.8 12.3 %gather_fusion = bf16[4992,128]{1,0:T(8,128)(2,1)} fusion(bf16[2496,128]{1,0:T(8,128)(2,1)} %bitcast.15, s32[5120]{0:T(1024)} %pad_clamp_fusion), kind=kCustom, calls=%fused_computation | custom fusion | bytes 2575872 | tf_op jit(solution)/shard_map/gather | solution.py:146
  115.1 4.3 %all-to-all-start.1 = ((bf16[8,624,128]{2,1,0:T(8,128)(2,1)}), bf16[8,624,128]{2,1,0:T(8,128)(2,1)}, u32[]{:S(2)}, u32[]{:S(2)}) async-start(bf16[8,624,128]{2,1,0:T(8,128)(2,1)} %bitcast.17), calls=%async_computation.1 | async-start | bytes 2555904 | tf_op jit(solution)/shard_map/all_to_all | solution.py:147
  119.4 0.7 convert_element_type.30
  120.1 0.7 compare_select_fusion.1
  120.8 0.0 copy-start.2
  120.8 0.6 copy-done.2
  121.4 0.6 pad_clamp_fusion.1
  122.0 1.4 constant_dynamic-update-slice_fusion.1
  123.4 1.3 select_reduce_fusion
  124.7 12.6 %all-to-all-done.1 = bf16[8,624,128]{2,1,0:T(8,128)(2,1)} async-done(((bf16[8,624,128]{2,1,0:T(8,128)(2,1)}), bf16[8,624,128]{2,1,0:T(8,128)(2,1)}, u32[]{:S(2)}, u32[]{:S(2)}) %all-to-all-start.1) | async-done | bytes 1277984 | tf_op jit(solution)/shard_map/all_to_all | solution.py:147
  137.2 9.2 %gather_fusion.1 = bf16[3328,128]{1,0:T(8,128)(2,1)} fusion(bf16[4992,128]{1,0:T(8,128)(2,1)} %bitcast.4, s32[4096]{0:T(1024)} %pad_clamp_fusion.1), kind=kCustom, calls=%fused_computation.1 | custom fusion | bytes 1717248 | tf_op jit(solution)/shard_map/gather | solution.py:148
  146.4 2.8 reshape.87
  149.2 2.1 constant_dynamic-update-slice_fusion
  151.4 0.0 copy-done
  151.4 5.6 %fusion.4 = (f32[128]{0:T(128)}, f32[128,3456]{1,0:T(8,128)}) fusion(bf16[128,3456]{1,0:T(8,128)(2,1)} %constant_dynamic-update-slice_fusion, f32[3456]{0:T(1024)S(1)} %convert_element_type.30, f32[3456]{0:T(1024)} %param.19, bf16[512,3456]{1,0:T(8,128)(2,1)} %param.18, bf16[3456,512]{1,0:T(8,128)(2,1)S(1)} %copy-done), kind=kOutput, calls=%fused_computation.12 | convolution fusion | flops 908689280 | bytes 9760256 | tf_op jit(solution)/shard_map/dot_general | solution.py:155
  156.9 1.2 divide_subtract_fusion
  158.1 6.1 %fusion = bf16[128,3456]{1,0:T(8,128)(2,1)} fusion(bf16[3456,512]{1,0:T(8,128)(2,1)S(1)} %copy-done, f32[128,3456]{1,0:T(8,128)} %get-tuple-element.8, bf16[512,3456]{1,0:T(8,128)(2,1)} %param.18, bf16[128,3456]{1,0:T(8,128)(2,1)} %constant_dynamic-update-slice_fusion, f32[128]{0:T(128)} %divide_subtract_fusion, f32[3456]{0:T(1024)S(1)} %convert_element_type.30), kind=kOutput, calls=%fused_computation.5 | convolution fusion | flops 910016512 | bytes 10631168 | tf_op jit(solution)/shard_map/dot_general | solution.py:172
  164.2 2.1 slice.12
  166.3 2.9 %reshape.113 = bf16[3328,128]{1,0:T(8,128)(2,1)} reshape(bf16[128,3328]{1,0:T(8,128)(2,1)} %slice.12) | data formatting | bytes 1703936 | tf_op jit(solution)/shard_map/reshape | solution.py:177
  169.2 14.9 %scatter_custom_fusion = bf16[4992,128]{1,0:T(8,128)(2,1)} fusion(s32[3328]{0:T(1024)} %copy-done.2, bf16[3328,128]{1,0:T(8,128)(2,1)} %reshape.113, bf16[]{:T(256)} %constant.8.clone.1), kind=kCustom, calls=%fused_computation.17 | custom fusion | bytes 1278464 | tf_op jit(solution)/shard_map/scatter | solution.py:178
  184.0 4.3 %all-to-all-start.2 = ((bf16[8,624,128]{2,1,0:T(8,128)(2,1)}), bf16[8,624,128]{2,1,0:T(8,128)(2,1)}, u32[]{:S(2)}, u32[]{:S(2)}) async-start(bf16[8,624,128]{2,1,0:T(8,128)(2,1)} %bitcast.16), calls=%async_computation.2 | async-start | bytes 2555904 | tf_op jit(solution)/shard_map/all_to_all | solution.py:179
  188.3 0.0 all-reduce.4.cloned.1.call-start
  188.4 1.4 reduce.1
  189.7 1.4 reshape.83
  191.2 1.3 pad.8
  192.5 13.7 %all-to-all-done.2 = bf16[8,624,128]{2,1,0:T(8,128)(2,1)} async-done(((bf16[8,624,128]{2,1,0:T(8,128)(2,1)}), bf16[8,624,128]{2,1,0:T(8,128)(2,1)}, u32[]{:S(2)}, u32[]{:S(2)}) %all-to-all-start.2) | async-done | bytes 1277984 | tf_op jit(solution)/shard_map/all_to_all | solution.py:179
  206.2 2.5 pad.9.data_ref
  208.7 1.1 iota.8.left_ref
  209.8 13.0 %shard_map.131 = f32[2496,128]{1,0:T(8,128)} custom-call(s32[2496,1]{1,0:T(8,128)} %iota.8.left_ref, s32[1,5120]{1,0:T(1,128)} %bitcast.19, bf16[5120,128]{1,0:T(8,128)(2,1)} %pad.9.data_ref), custom_call_target="tpu_custom_call" | custom-call | flops 3271557120 | bytes 2588672 | tf_op jit(solution)/shard_map/pallas_call | solution.py:95
  222.8 2.2 convert_element_type.35
  225.0 0.0 all-reduce.4.cloned.1.call-update
  225.0 1.4 slice.13
  226.4 2.1 fusion.1
  228.5 40.1 %psum.15 = f32[3456]{0:T(1024)} all-reduce(f32[3456]{0:T(1024)} %fusion.1), channel_id=1, replica_groups=mesh['grp'=4,'emb'=8] {'grp','emb'}, use_global_device_ids=true, to_apply=%region_5.6 | all-reduce | flops 3456 | bytes 27648 | tf_op jit(solution)/shard_map/psum | solution.py:195
  268.6 0.0 all-reduce.4.cloned.1.call-done
  268.6 2.3 reshape.92
Async XLA Ops:
  7.2 144.2 %copy-start = (bf16[3456,512]{1,0:T(8,128)(2,1)S(1)}, bf16[3456,512]{1,0:T(8,128)(2,1)}, u32[]{:S(2)}) copy-start(bf16[3456,512]{1,0:T(8,128)(2,1)} %param.17) | copy-start | bytes 10616836
  98.8 0.6 copy-start.1
  115.1 22.1 %all-to-all-start.1 = ((bf16[8,624,128]{2,1,0:T(8,128)(2,1)}), bf16[8,624,128]{2,1,0:T(8,128)(2,1)}, u32[]{:S(2)}, u32[]{:S(2)}) async-start(bf16[8,624,128]{2,1,0:T(8,128)(2,1)} %bitcast.17), calls=%async_computation.1 | async-start | bytes 2555904 | tf_op jit(solution)/shard_map/all_to_all | solution.py:147
  120.8 0.6 copy-start.2
  184.0 22.2 %all-to-all-start.2 = ((bf16[8,624,128]{2,1,0:T(8,128)(2,1)}), bf16[8,624,128]{2,1,0:T(8,128)(2,1)}, u32[]{:S(2)}, u32[]{:S(2)}) async-start(bf16[8,624,128]{2,1,0:T(8,128)(2,1)} %bitcast.16), calls=%async_computation.2 | async-start | bytes 2555904 | tf_op jit(solution)/shard_map/all_to_all | solution.py:179
  188.3 80.3 %all-reduce.4.cloned.1.call-start = ((), (), s32[]{:S(2)}) async-start(), calls=%async_computation.3 | async-start | bytes 1277952 | tf_op jit(solution)/shard_map/psum | solution.py:192
Sparse Core Ops, SparseCore 0:
  225.2 39.9 all-reduce.3

commit v5 on v3

--- a/solution.py
+++ b/solution.py
@@ -128,6 +128,15 @@
     err = jax.nn.sigmoid(logit) - labels.astype(jnp.float32)
     cotangent = err[:, None] * weight_row[None, :]
     scaled = cotangent * first_wide
+    bias_local = jnp.sum(scaled, axis=0)
+    device_count = lax.axis_size(("grp", "emb"))
+    bias_parts = lax.all_to_all(
+        jnp.broadcast_to(bias_local[None, :], (device_count, bias_local.shape[0])),
+        ("grp", "emb"),
+        split_axis=0,
+        concat_axis=0,
+        tiled=True,
+    )
     down_grad = lax.dot_general(
         scaled.astype(jnp.bfloat16),
         cross_up,
@@ -156,8 +165,7 @@
     )
     summed_grad = lax.psum(local_grad.astype(jnp.bfloat16), "grp").astype(jnp.float32)
     table_grad = summed_grad.reshape(table_count, rows_local, row_width)
-    bias_local = jnp.sum(scaled, axis=0)
-    bias_grad = lax.psum(bias_local, ("grp", "emb"))
+    bias_grad = jnp.sum(bias_parts, axis=0)
     return (table_grad, bottom_grad, bias_grad)
 
 

time: 234 us -> 238 us (1.017)
  blocking collectives: 50 us -> 9.94 us
  waiting for transfers between devices: 26.7 us -> 63.1 us
  starting transfers between devices: 8.74 us -> 12.8 us
    psum x1 -> x0, blocking collectives: 40.1 us -> none  [local(): bias_grad = lax.psum(bias_local, ('grp', 'emb'))]
    psum x1, waiting for transfers between devices: 0.01 us -> 38.4 us  [local(): lax.psum(local_grad.astype(jnp.bfloat16), 'grp').astype(jnp.float32)]
    all_to_all x0 -> x1, starting transfers between devices: none -> 4.09 us  [local(): lax.all_to_all(jnp.broadcast_to(bias_local[None, :], (device_count, bias_...]
  transfers between devices with their start and end apart: 3 -> 4, of which waited for: 2 -> 3; matrix products, arithmetic and copies ran while one was open for 5% -> 8% of each run, Pallas kernels for 0% -> 6%
where the time goes in v5:
time: 238 us; the launch traced here: 235 us
  local copies, waits for them, and re-layouts  84.4 us (35%)
  waiting for transfers between devices  63.1 us (27%)
  other arithmetic  24.9 us (10%)
  between operations  14.1 us (6%)
  matrix products  13.2 us (6%)
  Pallas kernels  13 us (5%)
  starting transfers between devices  12.8 us (5%)
  blocking collectives  9.94 us (4%)
    psum x1, waiting for transfers between devices, local(): lax.psum(local_grad.astype(jnp.bfloat16), 'grp').astype(jnp.float32)  38.4 us
    scatter x1, local copies, waits for them, and re-layouts, local(): jnp.zeros((slot_count, row_width), jnp.bfloat16).at[buffer_place]  14.9 us
    scatter x1, local copies, waits for them, and re-layouts, local(): jnp.zeros((owner_count * capacity,), jnp.int32).at[buffer_place]  13.4 us
    all_to_all x1, waiting for transfers between devices, local(): lax.all_to_all(fetched, 'emb', split_axis=0, concat_axis=0, tiled=True)  13.2 us
    pallas_call x1, Pallas kernels, select_rows(): pl.pallas_call(functools.partial(_select_kernel, padded // CHUNK), out_sh...  13 us
    gather x1, local copies, waits for them, and re-layouts, local(): fetched = flat_table[received]  12.3 us
    all_to_all x1, waiting for transfers between devices, local(): lax.all_to_all(outgoing.reshape(owner_count, capacity, row_width), 'emb',...  11.5 us
    all_to_all x1, blocking collectives, local(): lax.all_to_all(request, 'emb', split_axis=0, concat_axis=0, tiled=True)  9.94 us
  transfers between devices with their start and end apart: 4, of which 3 were waited for; matrix products, arithmetic and copies ran while one was open for 8% of the time, Pallas kernels for 6%

profile of v5, /device:TPU:0, one launch (start us, length us, event | category | flops | bytes accessed | tf_op | source)
XLA Modules:
  0.0 235.5 jit_solution(15055583621637893352)
XLA Ops:
  7.2 0.0 copy-start
  7.2 0.5 iota_multiply_fusion
  7.7 1.0 reduce.2
  8.7 0.7 copy.46
  9.4 0.8 broadcast_add_fusion
  10.2 0.7 copy.52
  11.0 1.6 reshape.144
  12.5 1.6 convert_convert_fusion
  14.1 1.8 copy.47
  15.9 1.6 fusion.15
  17.5 1.9 copy.48
  19.4 1.3 slice.16
  20.7 0.8 copy.49
  21.5 0.6 fusion.21
  22.1 0.8 copy.50
  22.9 0.7 subtract_bitcast_fusion
  23.6 1.9 select_reduce_fusion
  25.5 0.9 copy.51
  26.4 1.4 fusion.18
  27.8 13.4 %scatter_custom_fusion = s32[4992]{0:T(1024)} fusion(s32[3328]{0:T(1024)} %fusion.18, s32[3328]{0:T(1024)} %reshape.144, s32[]{:T(128)} %constant.9.clone.1), kind=kCustom, calls=%fused_computation.33 | custom fusion | bytes 20480 | tf_op jit(solution)/shard_map/scatter | solution.py:106
  41.3 1.4 all_to_all.18
  42.7 9.9 %all_to_all.28 = s32[8,1,624]{2,1,0:T(1,128)S(1)} all-to-all(s32[8,1,624]{2,1,0:T(1,128)} %all_to_all.18), channel_id=1, replica_groups=mesh['grp'=4,'emb'=8] {'emb'}, dimensions={0} | all-to-all | bytes 39936 | tf_op jit(solution)/shard_map/all_to_all | solution.py:108
  52.6 0.0 copy-start.1
  52.6 0.6 copy-done.1
  53.3 0.7 fusion.17
  53.9 1.4 reshape.126
  55.3 1.3 pad_clamp_fusion
  56.7 12.3 %gather_fusion = bf16[4992,128]{1,0:T(8,128)(2,1)} fusion(bf16[2496,128]{1,0:T(8,128)(2,1)} %bitcast.33, s32[5120]{0:T(1024)} %pad_clamp_fusion), kind=kCustom, calls=%fused_computation | custom fusion | bytes 2575872 | tf_op jit(solution)/shard_map/gather | solution.py:111
  68.9 4.3 %all-to-all-start.1 = ((bf16[8,624,128]{2,1,0:T(8,128)(2,1)}), bf16[8,624,128]{2,1,0:T(8,128)(2,1)}, u32[]{:S(2)}, u32[]{:S(2)}) async-start(bf16[8,624,128]{2,1,0:T(8,128)(2,1)} %bitcast.35), calls=%async_computation.1 | async-start | bytes 2555904 | tf_op jit(solution)/shard_map/all_to_all | solution.py:112
  73.2 0.7 convert_element_type.45
  73.9 1.3 pad_clamp_fusion.1
  75.2 1.4 constant_dynamic-update-slice_fusion.1
  76.6 1.3 select_reduce_fusion.1
  77.9 13.2 %all-to-all-done.1 = bf16[8,624,128]{2,1,0:T(8,128)(2,1)} async-done(((bf16[8,624,128]{2,1,0:T(8,128)(2,1)}), bf16[8,624,128]{2,1,0:T(8,128)(2,1)}, u32[]{:S(2)}, u32[]{:S(2)}) %all-to-all-start.1) | async-done | bytes 1277984 | tf_op jit(solution)/shard_map/all_to_all | solution.py:112
  91.1 9.2 %gather_fusion.1 = bf16[3328,128]{1,0:T(8,128)(2,1)} fusion(bf16[4992,128]{1,0:T(8,128)(2,1)} %bitcast.7, s32[4096]{0:T(1024)} %pad_clamp_fusion.1), kind=kCustom, calls=%fused_computation.1 | custom fusion | bytes 1717248 | tf_op jit(solution)/shard_map/gather | solution.py:113
  100.3 2.8 %reshape.118 = bf16[128,3328]{1,0:T(8,128)(2,1)} reshape(bf16[3328,128]{1,0:T(8,128)(2,1)} %gather_fusion.1) | data formatting | bytes 1703936 | tf_op jit(solution)/shard_map/reshape | solution.py:113
  103.1 2.1 constant_dynamic-update-slice_fusion
  105.2 0.0 copy-done
  105.2 5.6 %fusion.4 = (f32[128]{0:T(128)}, f32[128,3456]{1,0:T(8,128)}) fusion(bf16[128,3456]{1,0:T(8,128)(2,1)} %constant_dynamic-update-slice_fusion, f32[3456]{0:T(1024)S(1)} %convert_element_type.45, f32[3456]{0:T(1024)} %param.19, bf16[512,3456]{1,0:T(8,128)(2,1)} %param.18, bf16[3456,512]{1,0:T(8,128)(2,1)S(1)} %copy-done), kind=kOutput, calls=%fused_computation.13 | convolution fusion | flops 908689280 | bytes 9760256 | tf_op jit(solution)/shard_map/dot_general | solution.py:120
  110.8 1.2 divide_subtract_fusion
  112.0 6.1 %fusion = bf16[128,3456]{1,0:T(8,128)(2,1)} fusion(bf16[3456,512]{1,0:T(8,128)(2,1)S(1)} %copy-done, f32[128,3456]{1,0:T(8,128)} %get-tuple-element.4, bf16[512,3456]{1,0:T(8,128)(2,1)} %param.18, bf16[128,3456]{1,0:T(8,128)(2,1)} %constant_dynamic-update-slice_fusion, f32[128]{0:T(128)} %divide_subtract_fusion, f32[3456]{0:T(1024)S(1)} %convert_element_type.45), kind=kOutput, calls=%fused_computation.6 | convolution fusion | flops 910016512 | bytes 10631168 | tf_op jit(solution)/shard_map/dot_general | solution.py:146
  118.0 2.1 slice.17
  120.2 2.9 %reshape.152 = bf16[3328,128]{1,0:T(8,128)(2,1)} reshape(bf16[128,3328]{1,0:T(8,128)(2,1)} %slice.17) | data formatting | bytes 1703936 | tf_op jit(solution)/shard_map/reshape | solution.py:151
  123.0 14.9 %scatter_custom_fusion.1 = bf16[4992,128]{1,0:T(8,128)(2,1)} fusion(s32[3328]{0:T(1024)} %fusion.18, bf16[3328,128]{1,0:T(8,128)(2,1)} %reshape.152, bf16[]{:T(256)} %constant.6.clone.1), kind=kCustom, calls=%fused_computation.18 | custom fusion | bytes 1278464 | tf_op jit(solution)/shard_map/scatter | solution.py:152
  137.9 4.4 %all-to-all-start.2 = ((bf16[8,624,128]{2,1,0:T(8,128)(2,1)}), bf16[8,624,128]{2,1,0:T(8,128)(2,1)}, u32[]{:S(2)}, u32[]{:S(2)}) async-start(bf16[8,624,128]{2,1,0:T(8,128)(2,1)} %bitcast.34), calls=%async_computation.2 | async-start | bytes 2555904 | tf_op jit(solution)/shard_map/all_to_all | solution.py:153
  142.3 1.4 reduce.4
  143.7 1.4 reshape.114
  145.1 1.3 pad.8
  146.5 2.1 fusion.1
  148.6 11.5 %all-to-all-done.2 = bf16[8,624,128]{2,1,0:T(8,128)(2,1)} async-done(((bf16[8,624,128]{2,1,0:T(8,128)(2,1)}), bf16[8,624,128]{2,1,0:T(8,128)(2,1)}, u32[]{:S(2)}, u32[]{:S(2)}) %all-to-all-start.2) | async-done | bytes 1277984 | tf_op jit(solution)/shard_map/all_to_all | solution.py:153
  160.0 1.7 broadcast_in_dim.8
  161.8 4.1 %all-to-all-start.3 = ((f32[32,1,3456]{2,1,0:T(1,128)}), f32[32,1,3456]{2,1,0:T(1,128)}, u32[]{:S(2)}, u32[]{:S(2)}) async-start(f32[32,1,3456]{2,1,0:T(1,128)} %broadcast_in_dim.8), calls=%async_computation.3 | async-start | bytes 884736 | tf_op jit(solution)/shard_map/all_to_all | solution.py:133
  165.9 0.0 all-reduce.4.cloned.1.call-start
  165.9 2.5 %pad.9.data_ref = bf16[5120,128]{1,0:T(8,128)(2,1)} pad(bf16[4992,128]{1,0:T(8,128)(2,1)} %bitcast.9, bf16[]{:T(256)} %constant.6.clone.1), padding=0_128x0_0 | pad | bytes 2588674 | tf_op jit(solution)/shard_map/jit(_pad)/pad | solution.py:55
  168.4 1.1 iota.32.left_ref
  169.5 13.0 %shard_map.130 = f32[2496,128]{1,0:T(8,128)} custom-call(s32[2496,1]{1,0:T(8,128)} %iota.32.left_ref, s32[1,5120]{1,0:T(1,128)} %bitcast.41, bf16[5120,128]{1,0:T(8,128)(2,1)} %pad.9.data_ref), custom_call_target="tpu_custom_call" | custom-call | flops 3271557120 | bytes 2588672 | tf_op jit(solution)/shard_map/pallas_call | solution.py:57
  182.5 2.2 convert_element_type.50
  184.7 0.0 all-reduce.4.cloned.1.call-update
  184.7 1.4 slice.18
  186.1 0.0 all-to-all-done.3
  186.1 1.9 reduce_sum.52
  188.0 38.4 %all-reduce.4.cloned.1.call-done = bf16[26,96,128]{2,1,0:T(8,128)(2,1)} async-done(((bf16[26,96,128]{2,1,0:T(8,128)(2,1)}), bf16[26,96,128]{2,1,0:T(8,128)(2,1)}) %all-reduce.4.cloned.1.call-update) | async-done | bytes 638992 | tf_op jit(solution)/shard_map/psum | solution.py:166
  226.4 2.3 reshape.123
Async XLA Ops:
  7.2 98.0 %copy-start = (bf16[3456,512]{1,0:T(8,128)(2,1)S(1)}, bf16[3456,512]{1,0:T(8,128)(2,1)}, u32[]{:S(2)}) copy-start(bf16[3456,512]{1,0:T(8,128)(2,1)} %param.17) | copy-start | bytes 10616836
  52.6 0.6 copy-start.1
  68.9 22.1 %all-to-all-start.1 = ((bf16[8,624,128]{2,1,0:T(8,128)(2,1)}), bf16[8,624,128]{2,1,0:T(8,128)(2,1)}, u32[]{:S(2)}, u32[]{:S(2)}) async-start(bf16[8,624,128]{2,1,0:T(8,128)(2,1)} %bitcast.35), calls=%async_computation.1 | async-start | bytes 2555904 | tf_op jit(solution)/shard_map/all_to_all | solution.py:112
  137.9 22.2 %all-to-all-start.2 = ((bf16[8,624,128]{2,1,0:T(8,128)(2,1)}), bf16[8,624,128]{2,1,0:T(8,128)(2,1)}, u32[]{:S(2)}, u32[]{:S(2)}) async-start(bf16[8,624,128]{2,1,0:T(8,128)(2,1)} %bitcast.34), calls=%async_computation.2 | async-start | bytes 2555904 | tf_op jit(solution)/shard_map/all_to_all | solution.py:153
  161.8 24.4 %all-to-all-start.3 = ((f32[32,1,3456]{2,1,0:T(1,128)}), f32[32,1,3456]{2,1,0:T(1,128)}, u32[]{:S(2)}, u32[]{:S(2)}) async-start(f32[32,1,3456]{2,1,0:T(1,128)} %broadcast_in_dim.8), calls=%async_computation.3 | async-start | bytes 884736 | tf_op jit(solution)/shard_map/all_to_all | solution.py:133
  165.9 60.5 %all-reduce.4.cloned.1.call-start = ((), (), s32[]{:S(2)}) async-start(), calls=%async_computation.4 | async-start | bytes 1277952 | tf_op jit(solution)/shard_map/psum | solution.py:166
Sparse Core Ops, SparseCore 0:
  184.9 41.4 all-reduce.3

commit v6 on v5

--- a/solution.py
+++ b/solution.py
@@ -163,7 +163,14 @@
         incoming.reshape(slot_count, row_width),
         jnp.float32,
     )
-    summed_grad = lax.psum(local_grad.astype(jnp.bfloat16), "grp").astype(jnp.float32)
+    copies = lax.axis_size("grp")
+    part_rows = local_grad.shape[0] // copies
+    parts = local_grad.astype(jnp.bfloat16).reshape(copies, part_rows, row_width)
+    parts = lax.all_to_all(parts, "grp", split_axis=0, concat_axis=0, tiled=True)
+    owned = jnp.sum(parts.astype(jnp.float32), axis=0).astype(jnp.bfloat16)
+    spread = jnp.broadcast_to(owned[None], (copies, part_rows, row_width))
+    spread = lax.all_to_all(spread, "grp", split_axis=0, concat_axis=0, tiled=True)
+    summed_grad = spread.reshape(copies * part_rows, row_width).astype(jnp.float32)
     table_grad = summed_grad.reshape(table_count, rows_local, row_width)
     bias_grad = jnp.sum(bias_parts, axis=0)
     return (table_grad, bottom_grad, bias_grad)

time: 238 us -> 240 us (level)
  between operations: 14.1 us -> 0.7 us
  starting transfers between devices: 12.8 us -> 22.9 us
    psum x1 -> x0, waiting for transfers between devices: 38.4 us -> none  [local(): lax.psum(local_grad.astype(jnp.bfloat16), 'grp').astype(jnp.float32)]
    all_to_all x0 -> x2, waiting for transfers between devices: none -> 25.9 us  [the longest x1 14 us: local(): lax.all_to_all(spread, 'grp', split_axis=0, concat_axis=0, tiled=True)]
    all_to_all x1, waiting for transfers between devices: 0.01 us -> 12.2 us  [local(): lax.all_to_all(jnp.broadcast_to(bias_local[None, :], (device_count, bias_...]
    all_to_all x0 -> x2, starting transfers between devices: none -> 9.02 us  [the longest x1 4.87 us: local(): lax.all_to_all(parts, 'grp', split_axis=0, concat_axis=0, tiled=True)]
  transfers between devices with their start and end apart: 4 -> 5, of which waited for: 3 -> 5; matrix products, arithmetic and copies ran while one was open for 8% -> 7% of each run, Pallas kernels for 6% -> 0%
where the time goes in v6:
time: 240 us; the launch traced here: 238 us
  local copies, waits for them, and re-layouts  86.2 us (36%)
  waiting for transfers between devices  64.8 us (27%)
  other arithmetic  26.8 us (11%)
  starting transfers between devices  22.9 us (10%)
  matrix products  13.2 us (6%)
  Pallas kernels  13 us (5%)
  blocking collectives  9.94 us (4%)
    scatter x1, local copies, waits for them, and re-layouts, local(): jnp.zeros((slot_count, row_width), jnp.bfloat16).at[buffer_place]  14.9 us
    all_to_all x1, waiting for transfers between devices, local(): lax.all_to_all(spread, 'grp', split_axis=0, concat_axis=0, tiled=True)  14 us
    all_to_all x1, waiting for transfers between devices, local(): lax.all_to_all(outgoing.reshape(owner_count, capacity, row_width), 'emb',...  13.6 us
    scatter x1, local copies, waits for them, and re-layouts, local(): jnp.zeros((owner_count * capacity,), jnp.int32).at[buffer_place]  13.4 us
    all_to_all x1, waiting for transfers between devices, local(): lax.all_to_all(fetched, 'emb', split_axis=0, concat_axis=0, tiled=True)  13.2 us
    pallas_call x1, Pallas kernels, select_rows(): pl.pallas_call(functools.partial(_select_kernel, padded // CHUNK), out_sh...  13 us
    gather x1, local copies, waits for them, and re-layouts, local(): fetched = flat_table[received]  12.3 us
    all_to_all x1, waiting for transfers between devices, local(): lax.all_to_all(jnp.broadcast_to(bias_local[None, :], (device_count, bias_...  12.2 us
  transfers between devices with their start and end apart: 5, of which 5 were waited for; matrix products, arithmetic and copies ran while one was open for 7% of the time, Pallas kernels for 0%

profile of v6, /device:TPU:0, one launch (start us, length us, event | category | flops | bytes accessed | tf_op | source)
XLA Modules:
  0.0 237.6 jit_solution(2432024172093223845)
XLA Ops:
  0.6 0.0 copy-start
  0.6 0.5 iota_multiply_fusion
  1.2 1.0 reduce.3
  2.2 0.7 copy.46
  2.9 0.8 broadcast_add_fusion
  3.7 0.7 copy.52
  4.4 1.6 reshape.147
  6.0 1.6 convert_convert_fusion
  7.6 1.8 copy.47
  9.4 1.6 fusion.15
  11.0 1.9 copy.48
  12.9 1.3 slice.16
  14.2 0.8 copy.49
  15.0 0.6 fusion.21
  15.6 0.8 copy.50
  16.4 0.7 subtract_bitcast_fusion
  17.1 1.9 select_reduce_fusion
  19.0 0.9 copy.51
  19.9 1.4 fusion.18
  21.3 13.4 %scatter_custom_fusion = s32[4992]{0:T(1024)} fusion(s32[3328]{0:T(1024)} %fusion.18, s32[3328]{0:T(1024)} %reshape.147, s32[]{:T(128)} %constant.9.clone.1), kind=kCustom, calls=%fused_computation.33 | custom fusion | bytes 20480 | tf_op jit(solution)/shard_map/scatter | solution.py:106
  34.7 1.4 all_to_all.24
  36.2 9.9 %all_to_all.38 = s32[8,1,624]{2,1,0:T(1,128)S(1)} all-to-all(s32[8,1,624]{2,1,0:T(1,128)} %all_to_all.24), channel_id=1, replica_groups=mesh['grp'=4,'emb'=8] {'emb'}, dimensions={0} | all-to-all | bytes 39936 | tf_op jit(solution)/shard_map/all_to_all | solution.py:108
  46.1 0.6 copy-done.1
  46.7 0.7 fusion.17
  47.4 1.4 reshape.129
  48.8 1.3 pad_clamp_fusion
  50.1 12.3 %gather_fusion = bf16[4992,128]{1,0:T(8,128)(2,1)} fusion(bf16[2496,128]{1,0:T(8,128)(2,1)} %bitcast.35, s32[5120]{0:T(1024)} %pad_clamp_fusion), kind=kCustom, calls=%fused_computation | custom fusion | bytes 2575872 | tf_op jit(solution)/shard_map/gather | solution.py:111
  62.4 4.3 %all-to-all-start.1 = ((bf16[8,624,128]{2,1,0:T(8,128)(2,1)}), bf16[8,624,128]{2,1,0:T(8,128)(2,1)}, u32[]{:S(2)}, u32[]{:S(2)}) async-start(bf16[8,624,128]{2,1,0:T(8,128)(2,1)} %bitcast.37), calls=%async_computation.1 | async-start | bytes 2555904 | tf_op jit(solution)/shard_map/all_to_all | solution.py:112
  66.7 0.7 convert_element_type.53
  67.4 1.3 pad_clamp_fusion.1
  68.7 1.4 constant_dynamic-update-slice_fusion.1
  70.1 1.3 select_reduce_fusion.1
  71.4 13.2 %all-to-all-done.1 = bf16[8,624,128]{2,1,0:T(8,128)(2,1)} async-done(((bf16[8,624,128]{2,1,0:T(8,128)(2,1)}), bf16[8,624,128]{2,1,0:T(8,128)(2,1)}, u32[]{:S(2)}, u32[]{:S(2)}) %all-to-all-start.1) | async-done | bytes 1277984 | tf_op jit(solution)/shard_map/all_to_all | solution.py:112
  84.6 9.2 %gather_fusion.1 = bf16[3328,128]{1,0:T(8,128)(2,1)} fusion(bf16[4992,128]{1,0:T(8,128)(2,1)} %bitcast.7, s32[4096]{0:T(1024)} %pad_clamp_fusion.1), kind=kCustom, calls=%fused_computation.1 | custom fusion | bytes 1717248 | tf_op jit(solution)/shard_map/gather | solution.py:113
  93.8 2.8 %reshape.121 = bf16[128,3328]{1,0:T(8,128)(2,1)} reshape(bf16[3328,128]{1,0:T(8,128)(2,1)} %gather_fusion.1) | data formatting | bytes 1703936 | tf_op jit(solution)/shard_map/reshape | solution.py:113
  96.5 2.1 constant_dynamic-update-slice_fusion
  98.7 5.6 %fusion.4 = (f32[128]{0:T(128)}, f32[128,3456]{1,0:T(8,128)}) fusion(bf16[128,3456]{1,0:T(8,128)(2,1)} %constant_dynamic-update-slice_fusion, f32[3456]{0:T(1024)S(1)} %convert_element_type.53, f32[3456]{0:T(1024)} %param.19, bf16[512,3456]{1,0:T(8,128)(2,1)} %param.18, bf16[3456,512]{1,0:T(8,128)(2,1)S(1)} %copy-done), kind=kOutput, calls=%fused_computation.13 | convolution fusion | flops 908689280 | bytes 9760256 | tf_op jit(solution)/shard_map/dot_general | solution.py:120
  104.3 1.2 divide_subtract_fusion
  105.5 6.1 %fusion = bf16[128,3456]{1,0:T(8,128)(2,1)} fusion(bf16[3456,512]{1,0:T(8,128)(2,1)S(1)} %copy-done, f32[128,3456]{1,0:T(8,128)} %get-tuple-element.4, bf16[512,3456]{1,0:T(8,128)(2,1)} %param.18, bf16[128,3456]{1,0:T(8,128)(2,1)} %constant_dynamic-update-slice_fusion, f32[128]{0:T(128)} %divide_subtract_fusion, f32[3456]{0:T(1024)S(1)} %convert_element_type.53), kind=kOutput, calls=%fused_computation.6 | convolution fusion | flops 910016512 | bytes 10631168 | tf_op jit(solution)/shard_map/dot_general | solution.py:146
  111.5 2.1 slice.17
  113.6 2.9 %reshape.155 = bf16[3328,128]{1,0:T(8,128)(2,1)} reshape(bf16[128,3328]{1,0:T(8,128)(2,1)} %slice.17) | data formatting | bytes 1703936 | tf_op jit(solution)/shard_map/reshape | solution.py:151
  116.5 14.9 %scatter_custom_fusion.1 = bf16[4992,128]{1,0:T(8,128)(2,1)} fusion(s32[3328]{0:T(1024)} %fusion.18, bf16[3328,128]{1,0:T(8,128)(2,1)} %reshape.155, bf16[]{:T(256)} %constant.7.clone.1), kind=kCustom, calls=%fused_computation.18 | custom fusion | bytes 1278464 | tf_op jit(solution)/shard_map/scatter | solution.py:152
  131.4 4.4 %all-to-all-start.2 = ((bf16[8,624,128]{2,1,0:T(8,128)(2,1)}), bf16[8,624,128]{2,1,0:T(8,128)(2,1)}, u32[]{:S(2)}, u32[]{:S(2)}) async-start(bf16[8,624,128]{2,1,0:T(8,128)(2,1)} %bitcast.36), calls=%async_computation.2 | async-start | bytes 2555904 | tf_op jit(solution)/shard_map/all_to_all | solution.py:153
  135.8 1.4 reduce.5
  137.2 1.4 reshape.117
  138.6 1.3 pad.8
  139.9 13.6 %all-to-all-done.2 = bf16[8,624,128]{2,1,0:T(8,128)(2,1)} async-done(((bf16[8,624,128]{2,1,0:T(8,128)(2,1)}), bf16[8,624,128]{2,1,0:T(8,128)(2,1)}, u32[]{:S(2)}, u32[]{:S(2)}) %all-to-all-start.2) | async-done | bytes 1277984 | tf_op jit(solution)/shard_map/all_to_all | solution.py:153
  153.5 2.5 %pad.9.data_ref = bf16[5120,128]{1,0:T(8,128)(2,1)} pad(bf16[4992,128]{1,0:T(8,128)(2,1)} %bitcast.9, bf16[]{:T(256)} %constant.7.clone.1), padding=0_128x0_0 | pad | bytes 2588674 | tf_op jit(solution)/shard_map/jit(_pad)/pad | solution.py:55
  156.0 1.1 iota.32.left_ref
  157.1 13.0 %shard_map.130 = f32[2496,128]{1,0:T(8,128)} custom-call(s32[2496,1]{1,0:T(8,128)} %iota.32.left_ref, s32[1,5120]{1,0:T(1,128)} %bitcast.43, bf16[5120,128]{1,0:T(8,128)(2,1)} %pad.9.data_ref), custom_call_target="tpu_custom_call" | custom-call | flops 3271557120 | bytes 2588672 | tf_op jit(solution)/shard_map/pallas_call | solution.py:57
  170.1 2.2 convert_element_type.58
  172.3 4.9 %all-to-all-start.3 = ((bf16[4,624,128]{2,1,0:T(8,128)(2,1)}), bf16[4,624,128]{2,1,0:T(8,128)(2,1)}, u32[]{:S(2)}, u32[]{:S(2)}) async-start(bf16[4,624,128]{2,1,0:T(8,128)(2,1)} %bitcast.38), calls=%async_computation.3 | async-start | bytes 1277952 | tf_op jit(solution)/shard_map/all_to_all | solution.py:169
  177.2 2.1 fusion.1
  179.3 11.9 %all-to-all-done.3 = bf16[4,624,128]{2,1,0:T(8,128)(2,1)} async-done(((bf16[4,624,128]{2,1,0:T(8,128)(2,1)}), bf16[4,624,128]{2,1,0:T(8,128)(2,1)}, u32[]{:S(2)}, u32[]{:S(2)}) %all-to-all-start.3) | async-done | bytes 639008 | tf_op jit(solution)/shard_map/all_to_all | solution.py:169
  191.2 1.7 broadcast_in_dim.11
  192.9 5.2 %all-to-all-start.5 = ((f32[32,1,3456]{2,1,0:T(1,128)}), f32[32,1,3456]{2,1,0:T(1,128)}, u32[]{:S(2)}, u32[]{:S(2)}) async-start(f32[32,1,3456]{2,1,0:T(1,128)} %broadcast_in_dim.11), calls=%async_computation.5 | async-start | bytes 884736 | tf_op jit(solution)/shard_map/all_to_all | solution.py:133
  198.1 1.9 reduce_sum.63
  200.0 12.2 %all-to-all-done.5 = f32[32,1,3456]{2,1,0:T(1,128)} async-done(((f32[32,1,3456]{2,1,0:T(1,128)}), f32[32,1,3456]{2,1,0:T(1,128)}, u32[]{:S(2)}, u32[]{:S(2)}) %all-to-all-start.5) | async-done | bytes 442400 | tf_op jit(solution)/shard_map/all_to_all | solution.py:133
  212.1 1.8 broadcast_in_dim.10
  214.0 4.2 %all-to-all-start.4 = ((bf16[4,624,128]{2,1,0:T(8,128)(2,1)}), bf16[4,624,128]{2,1,0:T(8,128)(2,1)}, u32[]{:S(2)}, u32[]{:S(2)}) async-start(bf16[4,624,128]{2,1,0:T(8,128)(2,1)} %broadcast_in_dim.10), calls=%async_computation.4 | async-start | bytes 1277952 | tf_op jit(solution)/shard_map/all_to_all | solution.py:172
  218.1 1.4 slice.18
  219.5 1.9 reduce_sum.65
  221.4 14.0 %all-to-all-done.4 = bf16[4,624,128]{2,1,0:T(8,128)(2,1)} async-done(((bf16[4,624,128]{2,1,0:T(8,128)(2,1)}), bf16[4,624,128]{2,1,0:T(8,128)(2,1)}, u32[]{:S(2)}, u32[]{:S(2)}) %all-to-all-start.4) | async-done | bytes 639008 | tf_op jit(solution)/shard_map/all_to_all | solution.py:172
  235.3 2.3 convert.2
  (2 shorter events, 0.0 us)
Async XLA Ops:
  0.6 98.0 %copy-start = (bf16[3456,512]{1,0:T(8,128)(2,1)S(1)}, bf16[3456,512]{1,0:T(8,128)(2,1)}, u32[]{:S(2)}) copy-start(bf16[3456,512]{1,0:T(8,128)(2,1)} %param.17) | copy-start | bytes 10616836
  46.1 0.6 copy-start.1
  62.4 22.1 %all-to-all-start.1 = ((bf16[8,624,128]{2,1,0:T(8,128)(2,1)}), bf16[8,624,128]{2,1,0:T(8,128)(2,1)}, u32[]{:S(2)}, u32[]{:S(2)}) async-start(bf16[8,624,128]{2,1,0:T(8,128)(2,1)} %bitcast.37), calls=%async_computation.1 | async-start | bytes 2555904 | tf_op jit(solution)/shard_map/all_to_all | solution.py:112
  131.4 22.2 %all-to-all-start.2 = ((bf16[8,624,128]{2,1,0:T(8,128)(2,1)}), bf16[8,624,128]{2,1,0:T(8,128)(2,1)}, u32[]{:S(2)}, u32[]{:S(2)}) async-start(bf16[8,624,128]{2,1,0:T(8,128)(2,1)} %bitcast.36), calls=%async_computation.2 | async-start | bytes 2555904 | tf_op jit(solution)/shard_map/all_to_all | solution.py:153
  172.3 18.9 %all-to-all-start.3 = ((bf16[4,624,128]{2,1,0:T(8,128)(2,1)}), bf16[4,624,128]{2,1,0:T(8,128)(2,1)}, u32[]{:S(2)}, u32[]{:S(2)}) async-start(bf16[4,624,128]{2,1,0:T(8,128)(2,1)} %bitcast.38), calls=%async_computation.3 | async-start | bytes 1277952 | tf_op jit(solution)/shard_map/all_to_all | solution.py:169
  192.9 19.2 %all-to-all-start.5 = ((f32[32,1,3456]{2,1,0:T(1,128)}), f32[32,1,3456]{2,1,0:T(1,128)}, u32[]{:S(2)}, u32[]{:S(2)}) async-start(f32[32,1,3456]{2,1,0:T(1,128)} %broadcast_in_dim.11), calls=%async_computation.5 | async-start | bytes 884736 | tf_op jit(solution)/shard_map/all_to_all | solution.py:133
  214.0 21.4 %all-to-all-start.4 = ((bf16[4,624,128]{2,1,0:T(8,128)(2,1)}), bf16[4,624,128]{2,1,0:T(8,128)(2,1)}, u32[]{:S(2)}, u32[]{:S(2)}) async-start(bf16[4,624,128]{2,1,0:T(8,128)(2,1)} %broadcast_in_dim.10), calls=%async_computation.4 | async-start | bytes 1277952 | tf_op jit(solution)/shard_map/all_to_all | solution.py:172

commit v7 on v3

--- a/solution.py
+++ b/solution.py
@@ -45,6 +45,18 @@
     totals = within[:, -1, :]
     before = jnp.cumsum(totals, axis=0) - totals
     return (within + before[:, None, :]).reshape(count, width).astype(jnp.int32)
+
+
+def _in_thirds(values, width):
+    high = values.astype(jnp.bfloat16)
+    rest = values - high.astype(jnp.float32)
+    middle = rest.astype(jnp.bfloat16)
+    low = (rest - middle.astype(jnp.float32)).astype(jnp.bfloat16)
+    return jnp.stack([high, middle, low]).reshape(-1, width)
+
+
+def _from_thirds(rows, count):
+    return jnp.sum(rows.astype(jnp.float32).reshape(-1, 3, count), axis=(0, 1))
 
 
 def select_rows(left, right, data, out_dtype):
@@ -128,6 +140,8 @@
     err = jax.nn.sigmoid(logit) - labels.astype(jnp.float32)
     cotangent = err[:, None] * weight_row[None, :]
     scaled = cotangent * first_wide
+    bias_rows = _in_thirds(jnp.sum(scaled, axis=0), row_width)
+    bias_count = bias_rows.shape[0]
     down_grad = lax.dot_general(
         scaled.astype(jnp.bfloat16),
         cross_up,
@@ -141,23 +155,38 @@
     bottom_grad = input_grad[:, :row_width]
     row_grads = input_grad[:, row_width:].reshape(lookup_count, row_width)
     outgoing = jnp.zeros((slot_count, row_width), jnp.bfloat16).at[buffer_place].set(row_grads)
-    incoming = lax.all_to_all(
-        outgoing.reshape(owner_count, capacity, row_width),
-        "emb",
-        split_axis=0,
-        concat_axis=0,
-        tiled=True,
-    )
+    outgoing = jnp.concatenate(
+        [
+            outgoing.reshape(owner_count, capacity, row_width),
+            jnp.broadcast_to(bias_rows[None], (owner_count, bias_count, row_width)),
+        ],
+        axis=1,
+    )
+    incoming = lax.all_to_all(outgoing, "emb", split_axis=0, concat_axis=0, tiled=True)
+    bias_emb = _from_thirds(incoming[:, capacity:], scaled.shape[1])
+    incoming = incoming[:, :capacity]
     local_grad = select_rows(
         jnp.arange(table_count * rows_local, dtype=jnp.int32),
         received_flat,
         incoming.reshape(slot_count, row_width),
         jnp.float32,
     )
-    summed_grad = lax.psum(local_grad.astype(jnp.bfloat16), "grp").astype(jnp.float32)
-    table_grad = summed_grad.reshape(table_count, rows_local, row_width)
-    bias_local = jnp.sum(scaled, axis=0)
-    bias_grad = lax.psum(bias_local, ("grp", "emb"))
+    copies = lax.axis_size("grp")
+    payload = jnp.concatenate(
+        [local_grad.astype(jnp.bfloat16), _in_thirds(bias_emb, row_width)], axis=0
+    )
+    spread = lax.all_to_all(
+        jnp.broadcast_to(payload[None], (copies,) + payload.shape),
+        "grp",
+        split_axis=0,
+        concat_axis=0,
+        tiled=True,
+    )
+    grad_rows = local_grad.shape[0]
+    table_grad = jnp.sum(spread[:, :grad_rows].astype(jnp.float32), axis=0).reshape(
+        table_count, rows_local, row_width
+    )
+    bias_grad = _from_thirds(spread[:, grad_rows:], scaled.shape[1])
     return (table_grad, bottom_grad, bias_grad)
 
 

time: 234 us -> 263 us (1.12)
  waiting for transfers between devices: 26.7 us -> 84.5 us
  blocking collectives: 50 us -> 9.94 us
  between operations: 14.1 us -> 0.74 us
  other arithmetic: 23 us -> 32.9 us
  local copies, waits for them, and re-layouts: 82.7 us -> 91.7 us
  starting transfers between devices: 8.74 us -> 13.6 us
    all_to_all x1 -> x2, waiting for transfers between devices: 13.5 us -> 71.4 us  [the longest x1 55.7 us: local(): lax.all_to_all(jnp.broadcast_to(payload[None], (copies,) + payload.shape)...]
    psum x1 -> x0, blocking collectives: 40.1 us -> none  [local(): bias_grad = lax.psum(bias_local, ('grp', 'emb'))]
    reduce_sum x1 -> x6, other arithmetic: 2.1 us -> 10.1 us  [the longest x4 5.39 us: _from_thirds(): return jnp.sum(rows.astype(jnp.float32).reshape(-1, 3, count), axis=(0, 1))]
    all_to_all x1 -> x2, starting transfers between devices: 4.27 us -> 9.32 us  [the longest x1 4.86 us: local(): lax.all_to_all(jnp.broadcast_to(payload[None], (copies,) + payload.shape)...]
    broadcast_in_dim x0 -> x3, local copies, waits for them, and re-layouts: none -> 3.97 us  [the longest x2 2.12 us: local(): jnp.broadcast_to(bias_rows[None], (owner_count, bias_count, row_width))]
    reduce_sum x0 -> x4, local copies, waits for them, and re-layouts: none -> 3.48 us  [the longest x3 2.87 us: _from_thirds(): return jnp.sum(rows.astype(jnp.float32).reshape(-1, 3, count), axis=(0, 1))]
  transfers between devices with their start and end apart: 3 -> 3, of which waited for: 2 -> 3; matrix products, arithmetic and copies ran while one was open for 5% -> 4% of each run, Pallas kernels for 0% -> 0%
where the time goes in v7:
time: 263 us; the launch traced here: 260 us
  local copies, waits for them, and re-layouts  91.7 us (35%)
  waiting for transfers between devices  84.5 us (32%)
  other arithmetic  32.9 us (13%)
  starting transfers between devices  13.6 us (5%)
  matrix products  13.3 us (5%)
  Pallas kernels  13 us (5%)
  blocking collectives  9.94 us (4%)
    all_to_all x1, waiting for transfers between devices, local(): lax.all_to_all(jnp.broadcast_to(payload[None], (copies,) + payload.shape)...  55.7 us
    all_to_all x1, waiting for transfers between devices, local(): lax.all_to_all(outgoing, 'emb', split_axis=0, concat_axis=0, tiled=True)  15.7 us
    scatter x1, local copies, waits for them, and re-layouts, local(): jnp.zeros((slot_count, row_width), jnp.bfloat16).at[buffer_place]  14.9 us
    scatter x1, local copies, waits for them, and re-layouts, local(): jnp.zeros((owner_count * capacity,), jnp.int32).at[buffer_place]  13.4 us
    all_to_all x1, waiting for transfers between devices, local(): lax.all_to_all(fetched, 'emb', split_axis=0, concat_axis=0, tiled=True)  13.1 us
    pallas_call x1, Pallas kernels, select_rows(): pl.pallas_call(functools.partial(_select_kernel, padded // CHUNK), out_sh...  13 us
    gather x1, local copies, waits for them, and re-layouts, local(): fetched = flat_table[received]  12.3 us
    all_to_all x1, blocking collectives, local(): lax.all_to_all(request, 'emb', split_axis=0, concat_axis=0, tiled=True)  9.94 us
  transfers between devices with their start and end apart: 3, of which 3 were waited for; matrix products, arithmetic and copies ran while one was open for 4% of the time, Pallas kernels for 0%

profile of v7, /device:TPU:0, one launch (start us, length us, event | category | flops | bytes accessed | tf_op | source)
XLA Modules:
  0.0 259.6 jit_solution(5336852647696730840)
XLA Ops:
  1.2 1.0 reduce.5
  2.2 0.7 copy.47
  2.9 0.8 broadcast_add_fusion
  3.7 0.7 copy.53
  4.4 1.6 reshape.210
  6.0 1.6 convert_convert_fusion
  7.6 1.8 copy.48
  9.4 1.6 fusion.15
  11.0 1.9 copy.49
  12.9 1.3 slice.32
  14.2 0.8 copy.50
  15.6 0.8 copy.51
  16.4 0.7 subtract_bitcast_fusion
  17.0 1.9 select_reduce_fusion
  19.0 0.9 copy.52
  19.9 1.4 fusion.18
  21.3 13.4 %scatter_custom_fusion = s32[4992]{0:T(1024)} fusion(s32[3328]{0:T(1024)} %fusion.18, s32[3328]{0:T(1024)} %reshape.210, s32[]{:T(128)} %constant.9.clone.1), kind=kCustom, calls=%fused_computation.46 | custom fusion | bytes 20480 | tf_op jit(solution)/shard_map/scatter | solution.py:118
  34.7 1.4 all_to_all.17
  36.2 9.9 %all_to_all.27 = s32[8,1,624]{2,1,0:T(1,128)S(1)} all-to-all(s32[8,1,624]{2,1,0:T(1,128)} %all_to_all.17), channel_id=1, replica_groups=mesh['grp'=4,'emb'=8] {'emb'}, dimensions={0} | all-to-all | bytes 39936 | tf_op jit(solution)/shard_map/all_to_all | solution.py:120
  47.4 1.4 reshape.192
  48.8 1.3 pad_clamp_fusion
  50.1 12.3 %gather_fusion = bf16[4992,128]{1,0:T(8,128)(2,1)} fusion(bf16[2496,128]{1,0:T(8,128)(2,1)} %bitcast.33, s32[5120]{0:T(1024)} %pad_clamp_fusion), kind=kCustom, calls=%fused_computation | custom fusion | bytes 2575872 | tf_op jit(solution)/shard_map/gather | solution.py:123
  62.4 4.3 %all-to-all-start.1 = ((bf16[8,624,128]{2,1,0:T(8,128)(2,1)}), bf16[8,624,128]{2,1,0:T(8,128)(2,1)}, u32[]{:S(2)}, u32[]{:S(2)}) async-start(bf16[8,624,128]{2,1,0:T(8,128)(2,1)} %bitcast.36), calls=%async_computation.1 | async-start | bytes 2555904 | tf_op jit(solution)/shard_map/all_to_all | solution.py:124
  66.7 0.7 convert_element_type.185
  67.4 1.3 pad_clamp_fusion.1
  68.7 1.4 constant_dynamic-update-slice_fusion.1
  70.1 1.3 select_reduce_fusion.1
  71.4 13.1 %all-to-all-done.1 = bf16[8,624,128]{2,1,0:T(8,128)(2,1)} async-done(((bf16[8,624,128]{2,1,0:T(8,128)(2,1)}), bf16[8,624,128]{2,1,0:T(8,128)(2,1)}, u32[]{:S(2)}, u32[]{:S(2)}) %all-to-all-start.1) | async-done | bytes 1277984 | tf_op jit(solution)/shard_map/all_to_all | solution.py:124
  84.5 9.2 %gather_fusion.1 = bf16[3328,128]{1,0:T(8,128)(2,1)} fusion(bf16[4992,128]{1,0:T(8,128)(2,1)} %bitcast.7, s32[4096]{0:T(1024)} %pad_clamp_fusion.1), kind=kCustom, calls=%fused_computation.1 | custom fusion | bytes 1717248 | tf_op jit(solution)/shard_map/gather | solution.py:125
  93.8 2.8 %reshape.184 = bf16[128,3328]{1,0:T(8,128)(2,1)} reshape(bf16[3328,128]{1,0:T(8,128)(2,1)} %gather_fusion.1) | data formatting | bytes 1703936 | tf_op jit(solution)/shard_map/reshape | solution.py:125
  96.5 2.1 constant_dynamic-update-slice_fusion
  98.7 5.6 %fusion.4 = (f32[128]{0:T(128)}, f32[128,3456]{1,0:T(8,128)}) fusion(bf16[128,3456]{1,0:T(8,128)(2,1)} %constant_dynamic-update-slice_fusion, f32[3456]{0:T(1024)S(1)} %convert_element_type.185, f32[3456]{0:T(1024)} %param.19, bf16[512,3456]{1,0:T(8,128)(2,1)S(1)} %copy-done, bf16[3456,512]{1,0:T(8,128)(2,1)} %param.17), kind=kOutput, calls=%fused_computation.14 | convolution fusion | flops 908689280 | bytes 9760256 | tf_op jit(solution)/shard_map/dot_general | solution.py:132
  104.2 0.7 divide_subtract_fusion
  105.0 1.5 fusion.1
  107.7 6.1 %fusion = bf16[128,3456]{1,0:T(8,128)(2,1)} fusion(bf16[3456,512]{1,0:T(8,128)(2,1)} %param.17, f32[128,3456]{1,0:T(8,128)} %get-tuple-element.8, bf16[512,3456]{1,0:T(8,128)(2,1)S(1)} %copy-done, bf16[128,3456]{1,0:T(8,128)(2,1)} %constant_dynamic-update-slice_fusion, f32[128]{0:T(128)} %copy-done.3, f32[3456]{0:T(1024)S(1)} %convert_element_type.185), kind=kOutput, calls=%fused_computation.7 | convolution fusion | flops 910016512 | bytes 10631168 | tf_op jit(solution)/shard_map/dot_general | solution.py:151
  113.8 1.4 pad_maximum_fusion.2
  115.2 1.4 broadcast_in_dim.12
  116.6 2.1 slice.33
  118.7 2.9 %reshape.218 = bf16[3328,128]{1,0:T(8,128)(2,1)} reshape(bf16[128,3328]{1,0:T(8,128)(2,1)} %slice.33) | data formatting | bytes 1703936 | tf_op jit(solution)/shard_map/reshape | solution.py:156
  121.6 14.9 %scatter_custom_fusion.1 = bf16[4992,128]{1,0:T(8,128)(2,1)} fusion(s32[3328]{0:T(1024)} %fusion.18, bf16[3328,128]{1,0:T(8,128)(2,1)} %reshape.218, bf16[]{:T(256)} %constant.6.clone.1), kind=kCustom, calls=%fused_computation.21 | custom fusion | bytes 1278464 | tf_op jit(solution)/shard_map/scatter | solution.py:157
  136.4 0.8 broadcast_in_dim.13
  137.2 2.5 pad_maximum_fusion
  139.7 4.5 %all-to-all-start.2 = ((bf16[8,705,128]{2,1,0:T(8,128)(2,1)}), bf16[8,705,128]{2,1,0:T(8,128)(2,1)}, u32[]{:S(2)}, u32[]{:S(2)}) async-start(bf16[8,705,128]{2,1,0:T(8,128)(2,1)} %pad_maximum_fusion), calls=%async_computation.2 | async-start | bytes 2916352 | tf_op jit(solution)/shard_map/all_to_all | solution.py:165
  144.2 1.4 reduce.7
  145.6 1.4 reshape.180
  147.0 1.3 pad.8
  148.3 15.7 %all-to-all-done.2 = bf16[8,705,128]{2,1,0:T(8,128)(2,1)} async-done(((bf16[8,705,128]{2,1,0:T(8,128)(2,1)}), bf16[8,705,128]{2,1,0:T(8,128)(2,1)}, u32[]{:S(2)}, u32[]{:S(2)}) %all-to-all-start.2) | async-done | bytes 1443872 | tf_op jit(solution)/shard_map/all_to_all | solution.py:165
  164.0 1.6 convert_reduce_fusion.1
  165.5 1.4 reduce_sum.90
  167.0 0.9 reduce_sum.91
  168.5 1.4 reshape.188
  169.9 1.4 slice.34
  171.3 1.2 pad.9.data_ref
  172.5 1.1 iota.32.left_ref
  173.6 13.0 %shard_map.130 = f32[2496,128]{1,0:T(8,128)} custom-call(s32[2496,1]{1,0:T(8,128)} %iota.32.left_ref, s32[1,5120]{1,0:T(1,128)} %bitcast.42, bf16[5120,128]{1,0:T(8,128)(2,1)} %pad.9.data_ref), custom_call_target="tpu_custom_call" | custom-call | flops 3271557120 | bytes 2588672 | tf_op jit(solution)/shard_map/pallas_call | solution.py:69
  186.7 1.4 convert_element_type.195
  188.1 1.8 broadcast_in_dim.14
  190.0 4.9 %all-to-all-start.3 = ((bf16[4,2577,128]{2,1,0:T(8,128)(2,1)}), bf16[4,2577,128]{2,1,0:T(8,128)(2,1)}, u32[]{:S(2)}, u32[]{:S(2)}) async-start(bf16[4,2577,128]{2,1,0:T(8,128)(2,1)} %broadcast_in_dim.14), calls=%async_computation.3 | async-start | bytes 5292032 | tf_op jit(solution)/shard_map/all_to_all | solution.py:178
  194.8 1.4 slice.37
  196.2 55.7 %all-to-all-done.3 = bf16[4,2577,128]{2,1,0:T(8,128)(2,1)} async-done(((bf16[4,2577,128]{2,1,0:T(8,128)(2,1)}), bf16[4,2577,128]{2,1,0:T(8,128)(2,1)}, u32[]{:S(2)}, u32[]{:S(2)}) %all-to-all-start.3) | async-done | bytes 2638880 | tf_op jit(solution)/shard_map/all_to_all | solution.py:178
  251.9 1.5 convert_reduce_fusion.2
  253.4 1.4 reduce_sum.95
  254.9 1.5 reduce_sum.96
  256.3 3.3 %convert_reduce_fusion = f32[2496,128]{1,0:T(8,128)} fusion(bf16[4,2577,128]{2,1,0:T(8,128)(2,1)} %all-to-all-done.3), kind=kLoop, calls=%fused_computation.4 | loop fusion | flops 2236416 | bytes 3833856 | tf_op jit(solution)/shard_map/reduce_sum | solution.py:186
  (17 shorter events, 4.4 us)
Async XLA Ops:
  0.6 98.0 %copy-start = (bf16[512,3456]{1,0:T(8,128)(2,1)S(1)}, bf16[512,3456]{1,0:T(8,128)(2,1)}, u32[]{:S(2)}) copy-start(bf16[512,3456]{1,0:T(8,128)(2,1)} %param.18) | copy-start | bytes 10616836
  46.1 0.6 copy-start.1
  62.4 22.1 %all-to-all-start.1 = ((bf16[8,624,128]{2,1,0:T(8,128)(2,1)}), bf16[8,624,128]{2,1,0:T(8,128)(2,1)}, u32[]{:S(2)}, u32[]{:S(2)}) async-start(bf16[8,624,128]{2,1,0:T(8,128)(2,1)} %bitcast.36), calls=%async_computation.1 | async-start | bytes 2555904 | tf_op jit(solution)/shard_map/all_to_all | solution.py:124
  105.0 2.7 %copy-start.3 = (f32[128]{0:T(128)}, f32[128]{0:T(128)S(1)}, u32[]{:S(2)}) copy-start(f32[128]{0:T(128)S(1)} %divide_subtract_fusion) | copy-start | bytes 1540
  139.7 24.3 %all-to-all-start.2 = ((bf16[8,705,128]{2,1,0:T(8,128)(2,1)}), bf16[8,705,128]{2,1,0:T(8,128)(2,1)}, u32[]{:S(2)}, u32[]{:S(2)}) async-start(bf16[8,705,128]{2,1,0:T(8,128)(2,1)} %pad_maximum_fusion), calls=%async_computation.2 | async-start | bytes 2916352 | tf_op jit(solution)/shard_map/all_to_all | solution.py:165
  186.7 1.4 copy-start.2
  190.0 61.9 %all-to-all-start.3 = ((bf16[4,2577,128]{2,1,0:T(8,128)(2,1)}), bf16[4,2577,128]{2,1,0:T(8,128)(2,1)}, u32[]{:S(2)}, u32[]{:S(2)}) async-start(bf16[4,2577,128]{2,1,0:T(8,128)(2,1)} %broadcast_in_dim.14), calls=%async_computation.3 | async-start | bytes 5292032 | tf_op jit(solution)/shard_map/all_to_all | solution.py:178

commit v8 on v7

--- a/solution.py
+++ b/solution.py
@@ -172,21 +172,26 @@
         jnp.float32,
     )
     copies = lax.axis_size("grp")
-    payload = jnp.concatenate(
-        [local_grad.astype(jnp.bfloat16), _in_thirds(bias_emb, row_width)], axis=0
-    )
+    part_rows = local_grad.shape[0] // copies
+    bias_thirds = _in_thirds(bias_emb, row_width)
+    parts = jnp.concatenate(
+        [
+            local_grad.astype(jnp.bfloat16).reshape(copies, part_rows, row_width),
+            jnp.broadcast_to(bias_thirds[None], (copies,) + bias_thirds.shape),
+        ],
+        axis=1,
+    )
+    parts = lax.all_to_all(parts, "grp", split_axis=0, concat_axis=0, tiled=True)
+    bias_grad = _from_thirds(parts[:, part_rows:], scaled.shape[1])
+    owned = jnp.sum(parts[:, :part_rows].astype(jnp.float32), axis=0).astype(jnp.bfloat16)
     spread = lax.all_to_all(
-        jnp.broadcast_to(payload[None], (copies,) + payload.shape),
+        jnp.broadcast_to(owned[None], (copies, part_rows, row_width)),
         "grp",
         split_axis=0,
         concat_axis=0,
         tiled=True,
     )
-    grad_rows = local_grad.shape[0]
-    table_grad = jnp.sum(spread[:, :grad_rows].astype(jnp.float32), axis=0).reshape(
-        table_count, rows_local, row_width
-    )
-    bias_grad = _from_thirds(spread[:, grad_rows:], scaled.shape[1])
+    table_grad = spread.astype(jnp.float32).reshape(table_count, rows_local, row_width)
     return (table_grad, bottom_grad, bias_grad)
 
 

time: 263 us -> 237 us (0.901)
  waiting for transfers between devices: 84.5 us -> 38.6 us
  blocking collectives: 9.94 us -> 30.5 us
    all_to_all x1, waiting for transfers between devices: 55.7 us -> 9.75 us  [local(): lax.all_to_all(jnp.broadcast_to(owned[None], (copies, part_rows, row_widt...]
    all_to_all x0 -> x1, blocking collectives: none -> 20.6 us  [local(): lax.all_to_all(parts, 'grp', split_axis=0, concat_axis=0, tiled=True)]
    reduce_sum x1, other arithmetic: 3.25 us -> 0.09 us  [local(): jnp.sum(parts[:, :part_rows].astype(jnp.float32), axis=0)]
  transfers between devices with their start and end apart: 3 -> 3, of which waited for: 3 -> 3; matrix products, arithmetic and copies ran while one was open for 4% -> 6% of each run, Pallas kernels for 0% -> 0%
where the time goes in v8:
time: 237 us; the launch traced here: 232 us
  local copies, waits for them, and re-layouts  91.6 us (39%)
  waiting for transfers between devices  38.6 us (16%)
  other arithmetic  31.9 us (13%)
  blocking collectives  30.5 us (13%)
  matrix products  13.2 us (6%)
  Pallas kernels  13 us (5%)
  starting transfers between devices  12.9 us (5%)
    all_to_all x1, blocking collectives, local(): lax.all_to_all(parts, 'grp', split_axis=0, concat_axis=0, tiled=True)  20.6 us
    all_to_all x1, waiting for transfers between devices, local(): lax.all_to_all(outgoing, 'emb', split_axis=0, concat_axis=0, tiled=True)  15.7 us
    scatter x1, local copies, waits for them, and re-layouts, local(): jnp.zeros((slot_count, row_width), jnp.bfloat16).at[buffer_place]  14.9 us
    scatter x1, local copies, waits for them, and re-layouts, local(): jnp.zeros((owner_count * capacity,), jnp.int32).at[buffer_place]  13.4 us
    all_to_all x1, waiting for transfers between devices, local(): lax.all_to_all(fetched, 'emb', split_axis=0, concat_axis=0, tiled=True)  13.2 us
    pallas_call x1, Pallas kernels, select_rows(): pl.pallas_call(functools.partial(_select_kernel, padded // CHUNK), out_sh...  13 us
    gather x1, local copies, waits for them, and re-layouts, local(): fetched = flat_table[received]  12.3 us
    all_to_all x1, blocking collectives, local(): lax.all_to_all(request, 'emb', split_axis=0, concat_axis=0, tiled=True)  9.94 us
  transfers between devices with their start and end apart: 3, of which 3 were waited for; matrix products, arithmetic and copies ran while one was open for 6% of the time, Pallas kernels for 0%

profile of v8, /device:TPU:0, one launch (start us, length us, event | category | flops | bytes accessed | tf_op | source)
XLA Modules:
  0.0 232.5 jit_solution(4043985390856023066)
XLA Ops:
  1.2 1.0 reduce.6
  2.2 0.7 copy.38
  2.9 0.8 broadcast_add_fusion
  3.7 0.7 copy.44
  4.4 1.6 reshape.217
  6.0 1.6 convert_convert_fusion
  7.6 1.8 copy.39
  9.4 1.6 fusion.15
  11.0 1.9 copy.40
  12.9 1.3 slice.32
  14.2 0.8 copy.41
  15.6 0.8 copy.42
  17.1 1.9 select_reduce_fusion
  19.0 0.9 copy.43
  19.9 1.4 fusion.18
  21.3 13.4 %scatter_custom_fusion = s32[4992]{0:T(1024)} fusion(s32[3328]{0:T(1024)} %fusion.18, s32[3328]{0:T(1024)} %reshape.217, s32[]{:T(128)} %constant.9.clone.1), kind=kCustom, calls=%fused_computation.46 | custom fusion | bytes 20480 | tf_op jit(solution)/shard_map/scatter | solution.py:118
  34.7 1.4 all_to_all.20
  36.2 9.9 %all_to_all.32 = s32[8,1,624]{2,1,0:T(1,128)S(1)} all-to-all(s32[8,1,624]{2,1,0:T(1,128)} %all_to_all.20), channel_id=1, replica_groups=mesh['grp'=4,'emb'=8] {'emb'}, dimensions={0} | all-to-all | bytes 39936 | tf_op jit(solution)/shard_map/all_to_all | solution.py:120
  47.4 1.4 reshape.199
  48.8 1.3 pad_clamp_fusion
  50.1 12.3 %gather_fusion = bf16[4992,128]{1,0:T(8,128)(2,1)} fusion(bf16[2496,128]{1,0:T(8,128)(2,1)} %bitcast.35, s32[5120]{0:T(1024)} %pad_clamp_fusion), kind=kCustom, calls=%fused_computation | custom fusion | bytes 2575872 | tf_op jit(solution)/shard_map/gather | solution.py:123
  62.4 4.3 %all-to-all-start.1 = ((bf16[8,624,128]{2,1,0:T(8,128)(2,1)}), bf16[8,624,128]{2,1,0:T(8,128)(2,1)}, u32[]{:S(2)}, u32[]{:S(2)}) async-start(bf16[8,624,128]{2,1,0:T(8,128)(2,1)} %bitcast.38), calls=%async_computation.1 | async-start | bytes 2555904 | tf_op jit(solution)/shard_map/all_to_all | solution.py:124
  66.7 0.7 convert_element_type.185
  67.4 1.3 pad_clamp_fusion.1
  68.7 1.4 constant_dynamic-update-slice_fusion.1
  70.1 1.3 select_reduce_fusion.1
  71.4 13.2 %all-to-all-done.1 = bf16[8,624,128]{2,1,0:T(8,128)(2,1)} async-done(((bf16[8,624,128]{2,1,0:T(8,128)(2,1)}), bf16[8,624,128]{2,1,0:T(8,128)(2,1)}, u32[]{:S(2)}, u32[]{:S(2)}) %all-to-all-start.1) | async-done | bytes 1277984 | tf_op jit(solution)/shard_map/all_to_all | solution.py:124
  84.6 9.2 %gather_fusion.1 = bf16[3328,128]{1,0:T(8,128)(2,1)} fusion(bf16[4992,128]{1,0:T(8,128)(2,1)} %bitcast.7, s32[4096]{0:T(1024)} %pad_clamp_fusion.1), kind=kCustom, calls=%fused_computation.1 | custom fusion | bytes 1717248 | tf_op jit(solution)/shard_map/gather | solution.py:125
  93.8 2.8 %reshape.188 = bf16[128,3328]{1,0:T(8,128)(2,1)} reshape(bf16[3328,128]{1,0:T(8,128)(2,1)} %gather_fusion.1) | data formatting | bytes 1703936 | tf_op jit(solution)/shard_map/reshape | solution.py:125
  96.5 2.1 constant_dynamic-update-slice_fusion
  98.7 5.6 %fusion.4 = (f32[128]{0:T(128)}, f32[128,3456]{1,0:T(8,128)}) fusion(bf16[128,3456]{1,0:T(8,128)(2,1)} %constant_dynamic-update-slice_fusion, f32[3456]{0:T(1024)S(1)} %convert_element_type.185, f32[3456]{0:T(1024)} %param.19, bf16[512,3456]{1,0:T(8,128)(2,1)S(1)} %copy-done, bf16[3456,512]{1,0:T(8,128)(2,1)} %param.17), kind=kOutput, calls=%fused_computation.13 | convolution fusion | flops 908689280 | bytes 9760256 | tf_op jit(solution)/shard_map/dot_general | solution.py:132
  104.9 1.5 fusion.1
  107.7 6.1 %fusion = bf16[128,3456]{1,0:T(8,128)(2,1)} fusion(bf16[3456,512]{1,0:T(8,128)(2,1)} %param.17, f32[128,3456]{1,0:T(8,128)} %get-tuple-element.8, bf16[512,3456]{1,0:T(8,128)(2,1)S(1)} %copy-done, bf16[128,3456]{1,0:T(8,128)(2,1)} %constant_dynamic-update-slice_fusion, f32[128]{0:T(128)} %copy-done.4, f32[3456]{0:T(1024)S(1)} %convert_element_type.185), kind=kOutput, calls=%fused_computation.6 | convolution fusion | flops 910016512 | bytes 10631168 | tf_op jit(solution)/shard_map/dot_general | solution.py:151
  113.7 1.4 pad_maximum_fusion.2
  115.1 1.4 broadcast_in_dim.16
  116.5 2.1 slice.33
  118.6 2.9 %reshape.225 = bf16[3328,128]{1,0:T(8,128)(2,1)} reshape(bf16[128,3328]{1,0:T(8,128)(2,1)} %slice.33) | data formatting | bytes 1703936 | tf_op jit(solution)/shard_map/reshape | solution.py:156
  121.5 14.9 %scatter_custom_fusion.1 = bf16[4992,128]{1,0:T(8,128)(2,1)} fusion(s32[3328]{0:T(1024)} %fusion.18, bf16[3328,128]{1,0:T(8,128)(2,1)} %reshape.225, bf16[]{:T(256)} %constant.7.clone.1), kind=kCustom, calls=%fused_computation.21 | custom fusion | bytes 1278464 | tf_op jit(solution)/shard_map/scatter | solution.py:157
  136.4 0.8 broadcast_in_dim.17
  137.1 2.5 %pad_maximum_fusion = bf16[8,705,128]{2,1,0:T(8,128)(2,1)} fusion(bf16[8,81,128]{2,1,0:T(8,128)(2,1)S(1)} %broadcast_in_dim.17, bf16[8,624,128]{2,1,0:T(8,128)(2,1)} %bitcast.36), kind=kLoop, calls=%fused_computation.14 | loop fusion | flops 2887680 | bytes 2887680 | tf_op jit(solution)/shard_map/concatenate | solution.py:158
  139.7 4.5 %all-to-all-start.2 = ((bf16[8,705,128]{2,1,0:T(8,128)(2,1)}), bf16[8,705,128]{2,1,0:T(8,128)(2,1)}, u32[]{:S(2)}, u32[]{:S(2)}) async-start(bf16[8,705,128]{2,1,0:T(8,128)(2,1)} %pad_maximum_fusion), calls=%async_computation.2 | async-start | bytes 2916352 | tf_op jit(solution)/shard_map/all_to_all | solution.py:165
  144.1 1.4 reduce.8
  145.5 1.4 reshape.184
  146.9 1.3 pad.8
  148.2 15.7 %all-to-all-done.2 = bf16[8,705,128]{2,1,0:T(8,128)(2,1)} async-done(((bf16[8,705,128]{2,1,0:T(8,128)(2,1)}), bf16[8,705,128]{2,1,0:T(8,128)(2,1)}, u32[]{:S(2)}, u32[]{:S(2)}) %all-to-all-start.2) | async-done | bytes 1443872 | tf_op jit(solution)/shard_map/all_to_all | solution.py:165
  163.9 1.6 convert_reduce_fusion
  165.5 1.4 reduce_sum.93
  166.9 0.9 reduce_sum.94
  168.5 1.4 broadcast_in_dim.18
  169.9 1.4 slice.34
  171.3 1.2 pad.9.data_ref
  172.4 1.1 iota.32.left_ref
  173.5 13.0 %shard_map.130 = f32[2496,128]{1,0:T(8,128)} custom-call(s32[2496,1]{1,0:T(8,128)} %iota.32.left_ref, s32[1,5120]{1,0:T(1,128)} %bitcast.44, bf16[5120,128]{1,0:T(8,128)(2,1)} %pad.9.data_ref), custom_call_target="tpu_custom_call" | custom-call | flops 3271557120 | bytes 2588672 | tf_op jit(solution)/shard_map/pallas_call | solution.py:69
  186.6 1.4 convert_element_type.195
  188.0 20.6 %all_to_all.33 = bf16[4,705,128]{2,1,0:T(8,128)(2,1)S(1)} all-to-all(bf16[4,705,128]{2,1,0:T(8,128)(2,1)S(1)} %pad_maximum_fusion.1), channel_id=1, replica_groups=mesh['grp'=4,'emb'=8] {'grp'}, dimensions={0} | all-to-all | bytes 1443840 | tf_op jit(solution)/shard_map/all_to_all | solution.py:184
  208.6 0.9 copy-done.1
  209.6 0.9 broadcast_in_dim.20
  210.5 4.2 %all-to-all-start.4 = ((bf16[4,624,128]{2,1,0:T(8,128)(2,1)}), bf16[4,624,128]{2,1,0:T(8,128)(2,1)}, u32[]{:S(2)}, u32[]{:S(2)}) async-start(bf16[4,624,128]{2,1,0:T(8,128)(2,1)} %broadcast_in_dim.20), calls=%async_computation.4 | async-start | bytes 1277952 | tf_op jit(solution)/shard_map/all_to_all | solution.py:187
  214.7 1.4 slice.37
  216.0 1.5 convert_reduce_fusion.1
  217.6 1.4 reduce_sum.98
  219.0 1.5 reduce_sum.99
  220.4 9.8 %all-to-all-done.4 = bf16[4,624,128]{2,1,0:T(8,128)(2,1)} async-done(((bf16[4,624,128]{2,1,0:T(8,128)(2,1)}), bf16[4,624,128]{2,1,0:T(8,128)(2,1)}, u32[]{:S(2)}, u32[]{:S(2)}) %all-to-all-start.4) | async-done | bytes 639008 | tf_op jit(solution)/shard_map/all_to_all | solution.py:187
  230.2 2.3 convert.2
  (22 shorter events, 5.9 us)
Async XLA Ops:
  0.6 98.1 %copy-start = (bf16[512,3456]{1,0:T(8,128)(2,1)S(1)}, bf16[512,3456]{1,0:T(8,128)(2,1)}, u32[]{:S(2)}) copy-start(bf16[512,3456]{1,0:T(8,128)(2,1)} %param.18) | copy-start | bytes 10616836
  46.1 0.6 copy-start.2
  62.4 22.1 %all-to-all-start.1 = ((bf16[8,624,128]{2,1,0:T(8,128)(2,1)}), bf16[8,624,128]{2,1,0:T(8,128)(2,1)}, u32[]{:S(2)}, u32[]{:S(2)}) async-start(bf16[8,624,128]{2,1,0:T(8,128)(2,1)} %bitcast.38), calls=%async_computation.1 | async-start | bytes 2555904 | tf_op jit(solution)/shard_map/all_to_all | solution.py:124
  104.9 2.7 %copy-start.4 = (f32[128]{0:T(128)}, f32[128]{0:T(128)S(1)}, u32[]{:S(2)}) copy-start(f32[128]{0:T(128)S(1)} %divide_subtract_fusion) | copy-start | bytes 1540
  139.7 24.3 %all-to-all-start.2 = ((bf16[8,705,128]{2,1,0:T(8,128)(2,1)}), bf16[8,705,128]{2,1,0:T(8,128)(2,1)}, u32[]{:S(2)}, u32[]{:S(2)}) async-start(bf16[8,705,128]{2,1,0:T(8,128)(2,1)} %pad_maximum_fusion), calls=%async_computation.2 | async-start | bytes 2916352 | tf_op jit(solution)/shard_map/all_to_all | solution.py:165
  186.6 1.4 copy-start.3
  208.6 0.9 copy-start.1
  210.5 19.7 %all-to-all-start.4 = ((bf16[4,624,128]{2,1,0:T(8,128)(2,1)}), bf16[4,624,128]{2,1,0:T(8,128)(2,1)}, u32[]{:S(2)}, u32[]{:S(2)}) async-start(bf16[4,624,128]{2,1,0:T(8,128)(2,1)} %broadcast_in_dim.20), calls=%async_computation.4 | async-start | bytes 1277952 | tf_op jit(solution)/shard_map/all_to_all | solution.py:187

commit v9 on v3

--- a/solution.py
+++ b/solution.py
@@ -32,19 +32,6 @@
     acc = jnp.zeros(out_ref.shape, jnp.float32)
     acc = lax.fori_loop(0, chunks, step, acc)
     out_ref[...] = acc.astype(out_ref.dtype)
-
-
-def _running_count(marks):
-    count, width = marks.shape
-    block = 128 if count % 128 == 0 else count
-    grouped = marks.reshape(count // block, block, width).astype(jnp.bfloat16)
-    lower = (
-        jnp.arange(block, dtype=jnp.int32)[:, None] >= jnp.arange(block, dtype=jnp.int32)[None, :]
-    ).astype(jnp.bfloat16)
-    within = jnp.einsum("rc,bcj->brj", lower, grouped, preferred_element_type=jnp.float32)
-    totals = within[:, -1, :]
-    before = jnp.cumsum(totals, axis=0) - totals
-    return (within + before[:, None, :]).reshape(count, width).astype(jnp.int32)
 
 
 def select_rows(left, right, data, out_dtype):
@@ -99,7 +86,7 @@
     owner_marks = (flat_owner[:, None] == jnp.arange(owner_count, dtype=jnp.int32)[None, :]).astype(
         jnp.int32
     )
-    ranking = _running_count(owner_marks) - 1
+    ranking = jnp.cumsum(owner_marks, axis=0) - 1
     slot_index = jnp.sum(ranking * owner_marks, axis=1)
     buffer_place = flat_owner * capacity + slot_index
     flat_table = tables.reshape(table_count * rows_local, row_width)

time: 234 us -> 228 us (0.974)
  local copies, waits for them, and re-layouts: 82.7 us -> 76.4 us
    another operation x1 -> x2, other arithmetic: 0.63 us -> 6.68 us  [_running_count(): before = jnp.cumsum(totals, axis=0) - totals]
where the time goes in v9:
time: 228 us; the launch traced here: 226 us
  local copies, waits for them, and re-layouts  76.4 us (34%)
  blocking collectives  50 us (22%)
  waiting for transfers between devices  26.7 us (12%)
  other arithmetic  25.3 us (11%)
  between operations  14.1 us (6%)
  Pallas kernels  13 us (6%)
  matrix products  11.6 us (5%)
  starting transfers between devices  8.75 us (4%)
    psum x1, blocking collectives, local(): bias_grad = lax.psum(bias_local, ('grp', 'emb'))  40.1 us
    scatter x1, local copies, waits for them, and re-layouts, local(): jnp.zeros((slot_count, row_width), jnp.bfloat16).at[buffer_place]  14.9 us
    all_to_all x1, waiting for transfers between devices, local(): lax.all_to_all(outgoing.reshape(owner_count, capacity, row_width), 'emb',...  13.5 us
    scatter x1, local copies, waits for them, and re-layouts, local(): jnp.zeros((owner_count * capacity,), jnp.int32).at[buffer_place]  13.5 us
    all_to_all x1, waiting for transfers between devices, local(): lax.all_to_all(fetched, 'emb', split_axis=0, concat_axis=0, tiled=True)  13.2 us
    pallas_call x1, Pallas kernels, select_rows(): pl.pallas_call(functools.partial(_select_kernel, padded // CHUNK), out_sh...  13 us
    gather x1, local copies, waits for them, and re-layouts, local(): fetched = flat_table[received]  12.3 us
    all_to_all x1, blocking collectives, local(): lax.all_to_all(request, 'emb', split_axis=0, concat_axis=0, tiled=True)  9.94 us
  transfers between devices with their start and end apart: 3, of which 2 were waited for; matrix products, arithmetic and copies ran while one was open for 5% of the time, Pallas kernels for 0%

profile of v9, /device:TPU:0, one launch (start us, length us, event | category | flops | bytes accessed | tf_op | source)
XLA Modules:
  0.0 226.0 jit_solution(4431445138982898102)
XLA Ops:
  7.2 0.0 copy-start
  7.2 0.9 broadcast_add_fusion
  8.1 0.7 copy.15
  8.9 1.6 reshape.134
  10.4 0.7 reduce
  11.2 0.7 fusion.14
  11.9 5.2 %reduce-window.6 = s32[8,26,128]{2,1,0:T(8,128)} reduce-window(s32[8,26,128]{2,1,0:T(8,128)} %fusion.14, s32[]{:T(128)} %constant.9.clone.1), window={size=1x1x128 pad=0_0x0_0x127_0}, to_apply=%region_0.0 | reduce-window | flops 3381248 | bytes 212996 | tf_op jit(solution)/shard_map/reduce-window
  17.1 1.8 slice_reduce_fusion
  18.9 1.5 reduce-window.9
  20.3 1.0 add_bitcast_fusion
  21.4 0.1 fusion.16
  21.5 0.8 fusion.18
  22.2 0.0 copy-start.2
  22.2 13.5 %scatter_custom_fusion = s32[4992]{0:T(1024)} fusion(s32[3328]{0:T(1024)S(1)} %fusion.18, s32[3328]{0:T(1024)} %reshape.134, s32[]{:T(128)} %constant.9.clone.1), kind=kCustom, calls=%fused_computation.34 | custom fusion | bytes 20480 | tf_op jit(solution)/shard_map/scatter | solution.py:93
  35.7 1.4 all_to_all.14
  37.1 9.9 %all_to_all.22 = s32[8,1,624]{2,1,0:T(1,128)S(1)} all-to-all(s32[8,1,624]{2,1,0:T(1,128)} %all_to_all.14), channel_id=1, replica_groups=mesh['grp'=4,'emb'=8] {'emb'}, dimensions={0} | all-to-all | bytes 39936 | tf_op jit(solution)/shard_map/all_to_all | solution.py:95
  47.1 0.0 copy-start.1
  47.1 0.6 copy-done.1
  47.7 0.7 fusion.17
  48.3 1.4 reshape.116
  49.8 1.3 pad_clamp_fusion
  51.1 12.3 %gather_fusion = bf16[4992,128]{1,0:T(8,128)(2,1)} fusion(bf16[2496,128]{1,0:T(8,128)(2,1)} %bitcast.32, s32[5120]{0:T(1024)} %pad_clamp_fusion), kind=kCustom, calls=%fused_computation | custom fusion | bytes 2575872 | tf_op jit(solution)/shard_map/gather | solution.py:98
  63.4 0.0 copy-done.2
  63.4 4.3 %all-to-all-start.1 = ((bf16[8,624,128]{2,1,0:T(8,128)(2,1)}), bf16[8,624,128]{2,1,0:T(8,128)(2,1)}, u32[]{:S(2)}, u32[]{:S(2)}) async-start(bf16[8,624,128]{2,1,0:T(8,128)(2,1)} %bitcast.34), calls=%async_computation.1 | async-start | bytes 2555904 | tf_op jit(solution)/shard_map/all_to_all | solution.py:99
  67.6 0.7 convert_element_type.36
  68.3 1.3 pad_clamp_fusion.1
  69.7 1.4 constant_dynamic-update-slice_fusion.1
  71.1 1.3 select_reduce_fusion
  72.3 13.2 %all-to-all-done.1 = bf16[8,624,128]{2,1,0:T(8,128)(2,1)} async-done(((bf16[8,624,128]{2,1,0:T(8,128)(2,1)}), bf16[8,624,128]{2,1,0:T(8,128)(2,1)}, u32[]{:S(2)}, u32[]{:S(2)}) %all-to-all-start.1) | async-done | bytes 1277984 | tf_op jit(solution)/shard_map/all_to_all | solution.py:99
  85.5 9.2 %gather_fusion.1 = bf16[3328,128]{1,0:T(8,128)(2,1)} fusion(bf16[4992,128]{1,0:T(8,128)(2,1)} %bitcast.5, s32[4096]{0:T(1024)} %pad_clamp_fusion.1), kind=kCustom, calls=%fused_computation.1 | custom fusion | bytes 1717248 | tf_op jit(solution)/shard_map/gather | solution.py:100
  94.7 2.8 %reshape.108 = bf16[128,3328]{1,0:T(8,128)(2,1)} reshape(bf16[3328,128]{1,0:T(8,128)(2,1)} %gather_fusion.1) | data formatting | bytes 1703936 | tf_op jit(solution)/shard_map/reshape | solution.py:100
  97.5 2.1 constant_dynamic-update-slice_fusion
  99.6 0.0 copy-done
  99.6 5.6 %fusion.4 = (f32[128]{0:T(128)}, f32[128,3456]{1,0:T(8,128)}) fusion(bf16[128,3456]{1,0:T(8,128)(2,1)} %constant_dynamic-update-slice_fusion, f32[3456]{0:T(1024)S(1)} %convert_element_type.36, f32[3456]{0:T(1024)} %param.19, bf16[512,3456]{1,0:T(8,128)(2,1)} %param.18, bf16[3456,512]{1,0:T(8,128)(2,1)S(1)} %copy-done), kind=kOutput, calls=%fused_computation.13 | convolution fusion | flops 908689280 | bytes 9760256 | tf_op jit(solution)/shard_map/dot_general | solution.py:107
  105.2 1.2 divide_subtract_fusion
  106.4 6.1 %fusion = bf16[128,3456]{1,0:T(8,128)(2,1)} fusion(bf16[3456,512]{1,0:T(8,128)(2,1)S(1)} %copy-done, f32[128,3456]{1,0:T(8,128)} %get-tuple-element.4, bf16[512,3456]{1,0:T(8,128)(2,1)} %param.18, bf16[128,3456]{1,0:T(8,128)(2,1)} %constant_dynamic-update-slice_fusion, f32[128]{0:T(128)} %divide_subtract_fusion, f32[3456]{0:T(1024)S(1)} %convert_element_type.36), kind=kOutput, calls=%fused_computation.6 | convolution fusion | flops 910016512 | bytes 10631168 | tf_op jit(solution)/shard_map/dot_general | solution.py:124
  112.5 2.1 slice.21
  114.6 2.9 %reshape.142 = bf16[3328,128]{1,0:T(8,128)(2,1)} reshape(bf16[128,3328]{1,0:T(8,128)(2,1)} %slice.21) | data formatting | bytes 1703936 | tf_op jit(solution)/shard_map/reshape | solution.py:129
  117.5 14.9 %scatter_custom_fusion.1 = bf16[4992,128]{1,0:T(8,128)(2,1)} fusion(s32[3328]{0:T(1024)} %copy-done.2, bf16[3328,128]{1,0:T(8,128)(2,1)} %reshape.142, bf16[]{:T(256)} %constant.14.clone.1), kind=kCustom, calls=%fused_computation.18 | custom fusion | bytes 1278464 | tf_op jit(solution)/shard_map/scatter | solution.py:130
  132.3 4.3 %all-to-all-start.2 = ((bf16[8,624,128]{2,1,0:T(8,128)(2,1)}), bf16[8,624,128]{2,1,0:T(8,128)(2,1)}, u32[]{:S(2)}, u32[]{:S(2)}) async-start(bf16[8,624,128]{2,1,0:T(8,128)(2,1)} %bitcast.33), calls=%async_computation.2 | async-start | bytes 2555904 | tf_op jit(solution)/shard_map/all_to_all | solution.py:131
  136.6 0.2 all-reduce.4.cloned.1.call-start
  136.8 1.4 reduce.4
  138.2 1.4 reshape.104
  139.6 1.3 pad.8
  140.9 13.5 %all-to-all-done.2 = bf16[8,624,128]{2,1,0:T(8,128)(2,1)} async-done(((bf16[8,624,128]{2,1,0:T(8,128)(2,1)}), bf16[8,624,128]{2,1,0:T(8,128)(2,1)}, u32[]{:S(2)}, u32[]{:S(2)}) %all-to-all-start.2) | async-done | bytes 1277984 | tf_op jit(solution)/shard_map/all_to_all | solution.py:131
  154.5 2.5 %pad.9.data_ref = bf16[5120,128]{1,0:T(8,128)(2,1)} pad(bf16[4992,128]{1,0:T(8,128)(2,1)} %bitcast.7, bf16[]{:T(256)} %constant.14.clone.1), padding=0_128x0_0 | pad | bytes 2588674 | tf_op jit(solution)/shard_map/jit(_pad)/pad | solution.py:42
  156.9 1.1 iota.21.left_ref
  158.1 13.0 %shard_map.130 = f32[2496,128]{1,0:T(8,128)} custom-call(s32[2496,1]{1,0:T(8,128)} %iota.21.left_ref, s32[1,5120]{1,0:T(1,128)} %bitcast.37, bf16[5120,128]{1,0:T(8,128)(2,1)} %pad.9.data_ref), custom_call_target="tpu_custom_call" | custom-call | flops 3271557120 | bytes 2588672 | tf_op jit(solution)/shard_map/pallas_call | solution.py:44
  171.1 2.2 convert_element_type.41
  173.3 0.0 all-reduce.4.cloned.1.call-update
  173.3 1.4 slice.22
  174.7 2.1 fusion.1
  176.8 40.1 %psum.15 = f32[3456]{0:T(1024)} all-reduce(f32[3456]{0:T(1024)} %fusion.1), channel_id=1, replica_groups=mesh['grp'=4,'emb'=8] {'grp','emb'}, use_global_device_ids=true, to_apply=%region_9.10 | all-reduce | flops 3456 | bytes 27648 | tf_op jit(solution)/shard_map/psum | solution.py:147
  216.9 0.0 all-reduce.4.cloned.1.call-done
  216.9 2.3 %reshape.113 = f32[26,96,128]{2,1,0:T(8,128)} convert(bf16[26,96,128]{2,1,0:T(8,128)(2,1)} %all-reduce.4.cloned.1.call-done) | non-fusion elementwise | flops 319488 | bytes 1916928 | tf_op jit(solution)/shard_map/reshape | solution.py:145
  (1 shorter events, 0.0 us)
Async XLA Ops:
  7.2 92.5 %copy-start = (bf16[3456,512]{1,0:T(8,128)(2,1)S(1)}, bf16[3456,512]{1,0:T(8,128)(2,1)}, u32[]{:S(2)}) copy-start(bf16[3456,512]{1,0:T(8,128)(2,1)} %param.17) | copy-start | bytes 10616836
  22.2 41.2 %copy-start.2 = (s32[3328]{0:T(1024)}, s32[3328]{0:T(1024)S(1)}, u32[]{:S(2)}) copy-start(s32[3328]{0:T(1024)S(1)} %fusion.18) | copy-start | bytes 39940
  47.1 0.6 copy-start.1
  63.4 22.1 %all-to-all-start.1 = ((bf16[8,624,128]{2,1,0:T(8,128)(2,1)}), bf16[8,624,128]{2,1,0:T(8,128)(2,1)}, u32[]{:S(2)}, u32[]{:S(2)}) async-start(bf16[8,624,128]{2,1,0:T(8,128)(2,1)} %bitcast.34), calls=%async_computation.1 | async-start | bytes 2555904 | tf_op jit(solution)/shard_map/all_to_all | solution.py:99
  132.3 22.2 %all-to-all-start.2 = ((bf16[8,624,128]{2,1,0:T(8,128)(2,1)}), bf16[8,624,128]{2,1,0:T(8,128)(2,1)}, u32[]{:S(2)}, u32[]{:S(2)}) async-start(bf16[8,624,128]{2,1,0:T(8,128)(2,1)} %bitcast.33), calls=%async_computation.2 | async-start | bytes 2555904 | tf_op jit(solution)/shard_map/all_to_all | solution.py:131
  136.6 80.3 %all-reduce.4.cloned.1.call-start = ((), (), s32[]{:S(2)}) async-start(), calls=%async_computation.3 | async-start | bytes 1277952 | tf_op jit(solution)/shard_map/psum | solution.py:144
Sparse Core Ops, SparseCore 0:
  173.4 39.9 all-reduce.3

commit v10 on v9

--- a/solution.py
+++ b/solution.py
@@ -6,9 +6,6 @@
 from jax.experimental import pallas as pl
 from jax.experimental.pallas import tpu as pltpu
 from jax.sharding import PartitionSpec as P
-
-CHUNK = 512
-
 
 def _row_block(rows):
     if rows <= 4096:
@@ -19,34 +16,43 @@
     return rows
 
 
-def _select_kernel(chunks, left_ref, right_ref, data_ref, out_ref):
-    left = left_ref[...]
+def _chunk_of(count):
+    for size in (512, 384, 256, 128):
+        if count % size == 0:
+            return size
+    return 512
+
+
+def _select_kernel(chunk, chunks, right_ref, data_ref, out_ref):
+    block = out_ref.shape[0]
+    left = lax.broadcasted_iota(jnp.int32, (block, 1), 0) + pl.program_id(0) * block
 
     def step(j, acc):
-        start = pl.multiple_of(j * CHUNK, CHUNK)
-        right = right_ref[:, pl.ds(start, CHUNK)]
+        start = pl.multiple_of(j * chunk, chunk)
+        right = right_ref[:, pl.ds(start, chunk)]
         picks = jnp.where(left == right, 1.0, 0.0).astype(data_ref.dtype)
-        block = data_ref[pl.ds(start, CHUNK), :]
-        return acc + jnp.dot(picks, block, preferred_element_type=jnp.float32)
+        part = data_ref[pl.ds(start, chunk), :]
+        return acc + jnp.dot(picks, part, preferred_element_type=jnp.float32)
 
     acc = jnp.zeros(out_ref.shape, jnp.float32)
     acc = lax.fori_loop(0, chunks, step, acc)
     out_ref[...] = acc.astype(out_ref.dtype)
 
 
-def select_rows(left, right, data, out_dtype):
-    rows = left.shape[0]
+def add_rows(rows, right, data, out_dtype):
     count, width = data.shape
-    padded = -(-count // CHUNK) * CHUNK
-    right = jnp.pad(right, (0, padded - count), constant_values=-1).reshape(1, padded)
-    data = jnp.pad(data, ((0, padded - count), (0, 0)))
+    chunk = _chunk_of(count)
+    padded = -(-count // chunk) * chunk
+    if padded != count:
+        right = jnp.pad(right, (0, padded - count), constant_values=-1)
+        data = jnp.pad(data, ((0, padded - count), (0, 0)))
+    right = right.reshape(1, padded)
     block = _row_block(rows)
     return pl.pallas_call(
-        functools.partial(_select_kernel, padded // CHUNK),
+        functools.partial(_select_kernel, chunk, padded // chunk),
         out_shape=jax.ShapeDtypeStruct((rows, width), out_dtype),
         grid=(rows // block,),
         in_specs=[
-            pl.BlockSpec((block, 1), lambda i: (i, 0)),
             pl.BlockSpec((1, padded), lambda i: (0, 0)),
             pl.BlockSpec((padded, width), lambda i: (0, 0)),
         ],
@@ -57,7 +63,7 @@
             bytes_accessed=padded * width * data.dtype.itemsize
             + rows * width * jnp.dtype(out_dtype).itemsize,
         ),
-    )(left.reshape(rows, 1), right, data)
+    )(right, data)
 
 
 def local(
@@ -135,8 +141,8 @@
         concat_axis=0,
         tiled=True,
     )
-    local_grad = select_rows(
-        jnp.arange(table_count * rows_local, dtype=jnp.int32),
+    local_grad = add_rows(
+        table_count * rows_local,
         received_flat,
         incoming.reshape(slot_count, row_width),
         jnp.float32,

time: 228 us -> 225 us (0.987)
  local copies, waits for them, and re-layouts: 76.4 us -> 71.5 us
    pad x2 -> x0, local copies, waits for them, and re-layouts: 3.78 us -> none  [the longest x1 2.45 us: select_rows(): data = jnp.pad(data, ((0, padded - count), (0, 0)))]
where the time goes in v10:
time: 225 us; the launch traced here: 222 us
  local copies, waits for them, and re-layouts  71.5 us (32%)
  blocking collectives  50.1 us (22%)
  waiting for transfers between devices  28.3 us (13%)
  other arithmetic  25.3 us (11%)
  between operations  14.1 us (6%)
  Pallas kernels  12.9 us (6%)
  matrix products  11.6 us (5%)
  starting transfers between devices  8.55 us (4%)
    psum x1, blocking collectives, local(): bias_grad = lax.psum(bias_local, ('grp', 'emb'))  40.2 us
    all_to_all x1, waiting for transfers between devices, local(): lax.all_to_all(outgoing.reshape(owner_count, capacity, row_width), 'emb',...  15 us
    scatter x1, local copies, waits for them, and re-layouts, local(): jnp.zeros((slot_count, row_width), jnp.bfloat16).at[buffer_place]  14.9 us
    scatter x1, local copies, waits for them, and re-layouts, local(): jnp.zeros((owner_count * capacity,), jnp.int32).at[buffer_place]  13.5 us
    all_to_all x1, waiting for transfers between devices, local(): lax.all_to_all(fetched, 'emb', split_axis=0, concat_axis=0, tiled=True)  13.2 us
    pallas_call x1, Pallas kernels, add_rows(): pl.pallas_call(functools.partial(_select_kernel, chunk, padded // chunk),...  12.9 us
    gather x1, local copies, waits for them, and re-layouts, local(): fetched = flat_table[received]  12.3 us
    all_to_all x1, blocking collectives, local(): lax.all_to_all(request, 'emb', split_axis=0, concat_axis=0, tiled=True)  9.94 us
  transfers between devices with their start and end apart: 3, of which 2 were waited for; matrix products, arithmetic and copies ran while one was open for 5% of the time, Pallas kernels for 0%

profile of v10, /device:TPU:0, one launch (start us, length us, event | category | flops | bytes accessed | tf_op | source)
XLA Modules:
  0.0 222.4 jit_solution(12743702642150297300)
XLA Ops:
  7.2 0.0 copy-start
  7.2 0.9 broadcast_add_fusion
  8.1 0.7 copy.16
  8.9 1.6 reshape.125
  10.4 0.7 reduce
  11.2 0.7 fusion.14
  11.9 5.2 %reduce-window.6 = s32[8,26,128]{2,1,0:T(8,128)} reduce-window(s32[8,26,128]{2,1,0:T(8,128)} %fusion.14, s32[]{:T(128)} %constant.9.clone.1), window={size=1x1x128 pad=0_0x0_0x127_0}, to_apply=%region_0.0 | reduce-window | flops 3381248 | bytes 212996 | tf_op jit(solution)/shard_map/reduce-window
  17.1 1.8 slice_reduce_fusion
  18.9 1.5 reduce-window.9
  20.3 1.0 add_bitcast_fusion
  21.4 0.1 fusion.16
  21.5 0.8 fusion.18
  22.2 0.0 copy-start.2
  22.2 13.5 %scatter_custom_fusion = s32[4992]{0:T(1024)} fusion(s32[3328]{0:T(1024)S(1)} %fusion.18, s32[3328]{0:T(1024)} %reshape.125, s32[]{:T(128)} %constant.9.clone.1), kind=kCustom, calls=%fused_computation.34 | custom fusion | bytes 20480 | tf_op jit(solution)/shard_map/scatter | solution.py:99
  35.7 1.4 all_to_all.14
  37.1 9.9 %all_to_all.22 = s32[8,1,624]{2,1,0:T(1,128)S(1)} all-to-all(s32[8,1,624]{2,1,0:T(1,128)} %all_to_all.14), channel_id=1, replica_groups=mesh['grp'=4,'emb'=8] {'emb'}, dimensions={0} | all-to-all | bytes 39936 | tf_op jit(solution)/shard_map/all_to_all | solution.py:101
  47.1 0.0 copy-start.1
  47.1 0.6 copy-done.1
  47.7 0.7 fusion.17
  48.3 1.4 reshape.107
  49.8 1.3 pad_clamp_fusion
  51.1 12.3 %gather_fusion = bf16[4992,128]{1,0:T(8,128)(2,1)} fusion(bf16[2496,128]{1,0:T(8,128)(2,1)} %bitcast.31, s32[5120]{0:T(1024)} %pad_clamp_fusion), kind=kCustom, calls=%fused_computation | custom fusion | bytes 2575872 | tf_op jit(solution)/shard_map/gather | solution.py:104
  63.4 0.0 copy-done.2
  63.4 4.3 %all-to-all-start.1 = ((bf16[8,624,128]{2,1,0:T(8,128)(2,1)}), bf16[8,624,128]{2,1,0:T(8,128)(2,1)}, u32[]{:S(2)}, u32[]{:S(2)}) async-start(bf16[8,624,128]{2,1,0:T(8,128)(2,1)} %bitcast.33), calls=%async_computation.1 | async-start | bytes 2555904 | tf_op jit(solution)/shard_map/all_to_all | solution.py:105
  67.6 0.7 convert_element_type.34
  68.3 1.3 pad_clamp_fusion.1
  69.7 1.4 constant_dynamic-update-slice_fusion.1
  71.1 1.2 select_reduce_fusion
  72.3 13.2 %all-to-all-done.1 = bf16[8,624,128]{2,1,0:T(8,128)(2,1)} async-done(((bf16[8,624,128]{2,1,0:T(8,128)(2,1)}), bf16[8,624,128]{2,1,0:T(8,128)(2,1)}, u32[]{:S(2)}, u32[]{:S(2)}) %all-to-all-start.1) | async-done | bytes 1277984 | tf_op jit(solution)/shard_map/all_to_all | solution.py:105
  85.5 9.2 %gather_fusion.1 = bf16[3328,128]{1,0:T(8,128)(2,1)} fusion(bf16[4992,128]{1,0:T(8,128)(2,1)} %bitcast.4, s32[4096]{0:T(1024)} %pad_clamp_fusion.1), kind=kCustom, calls=%fused_computation.1 | custom fusion | bytes 1717248 | tf_op jit(solution)/shard_map/gather | solution.py:106
  94.7 2.8 %reshape.99 = bf16[128,3328]{1,0:T(8,128)(2,1)} reshape(bf16[3328,128]{1,0:T(8,128)(2,1)} %gather_fusion.1) | data formatting | bytes 1703936 | tf_op jit(solution)/shard_map/reshape | solution.py:106
  97.5 2.1 constant_dynamic-update-slice_fusion
  99.6 0.0 copy-done
  99.6 5.6 %fusion.4 = (f32[128]{0:T(128)}, f32[128,3456]{1,0:T(8,128)}) fusion(bf16[128,3456]{1,0:T(8,128)(2,1)} %constant_dynamic-update-slice_fusion, f32[3456]{0:T(1024)S(1)} %convert_element_type.34, f32[3456]{0:T(1024)} %param.19, bf16[512,3456]{1,0:T(8,128)(2,1)} %param.18, bf16[3456,512]{1,0:T(8,128)(2,1)S(1)} %copy-done), kind=kOutput, calls=%fused_computation.13 | convolution fusion | flops 908689280 | bytes 9760256 | tf_op jit(solution)/shard_map/dot_general | solution.py:113
  105.2 1.2 divide_subtract_fusion
  106.4 6.1 %fusion = bf16[128,3456]{1,0:T(8,128)(2,1)} fusion(bf16[3456,512]{1,0:T(8,128)(2,1)S(1)} %copy-done, f32[128,3456]{1,0:T(8,128)} %get-tuple-element.4, bf16[512,3456]{1,0:T(8,128)(2,1)} %param.18, bf16[128,3456]{1,0:T(8,128)(2,1)} %constant_dynamic-update-slice_fusion, f32[128]{0:T(128)} %divide_subtract_fusion, f32[3456]{0:T(1024)S(1)} %convert_element_type.34), kind=kOutput, calls=%fused_computation.6 | convolution fusion | flops 910016512 | bytes 10631168 | tf_op jit(solution)/shard_map/dot_general | solution.py:130
  112.4 2.1 slice.21
  114.5 2.9 %reshape.133 = bf16[3328,128]{1,0:T(8,128)(2,1)} reshape(bf16[128,3328]{1,0:T(8,128)(2,1)} %slice.21) | data formatting | bytes 1703936 | tf_op jit(solution)/shard_map/reshape | solution.py:135
  117.4 14.9 %scatter_custom_fusion.1 = bf16[4992,128]{1,0:T(8,128)(2,1)} fusion(s32[3328]{0:T(1024)} %copy-done.2, bf16[3328,128]{1,0:T(8,128)(2,1)} %reshape.133, bf16[]{:T(256)} %constant.5.clone.1), kind=kCustom, calls=%fused_computation.18 | custom fusion | bytes 1278464 | tf_op jit(solution)/shard_map/scatter | solution.py:136
  132.3 4.3 %all-to-all-start.2 = ((bf16[8,624,128]{2,1,0:T(8,128)(2,1)}), bf16[8,624,128]{2,1,0:T(8,128)(2,1)}, u32[]{:S(2)}, u32[]{:S(2)}) async-start(bf16[8,624,128]{2,1,0:T(8,128)(2,1)} %bitcast.32), calls=%async_computation.2 | async-start | bytes 2555904 | tf_op jit(solution)/shard_map/all_to_all | solution.py:137
  136.5 0.0 all-reduce.2.cloned.1.call-start
  136.6 1.4 reduce.4
  138.0 1.4 reshape_reshape.4.right_ref
  139.4 15.0 %all-to-all-done.2 = bf16[8,624,128]{2,1,0:T(8,128)(2,1)} async-done(((bf16[8,624,128]{2,1,0:T(8,128)(2,1)}), bf16[8,624,128]{2,1,0:T(8,128)(2,1)}, u32[]{:S(2)}, u32[]{:S(2)}) %all-to-all-start.2) | async-done | bytes 1277984 | tf_op jit(solution)/shard_map/all_to_all | solution.py:137
  154.4 12.9 %shard_map.130 = f32[2496,128]{1,0:T(8,128)} custom-call(s32[1,4992]{1,0:T(1,128)} %reshape_reshape.4.right_ref, bf16[4992,128]{1,0:T(8,128)(2,1)} %bitcast.6.data_ref), custom_call_target="tpu_custom_call" | custom-call | flops 3189768192 | bytes 2555904 | tf_op jit(solution)/shard_map/pallas_call | solution.py:51
  167.4 2.2 convert_element_type.39
  169.6 0.0 all-reduce.2.cloned.1.call-update
  169.6 1.4 slice.22
  171.0 2.1 fusion.1
  173.1 40.2 %psum.15 = f32[3456]{0:T(1024)} all-reduce(f32[3456]{0:T(1024)} %fusion.1), channel_id=1, replica_groups=mesh['grp'=4,'emb'=8] {'grp','emb'}, use_global_device_ids=true, to_apply=%region_9.10 | all-reduce | flops 3456 | bytes 27648 | tf_op jit(solution)/shard_map/psum | solution.py:153
  213.2 0.0 all-reduce.2.cloned.1.call-done
  213.3 2.3 %reshape.104 = f32[26,96,128]{2,1,0:T(8,128)} convert(bf16[26,96,128]{2,1,0:T(8,128)(2,1)} %all-reduce.2.cloned.1.call-done) | non-fusion elementwise | flops 319488 | bytes 1916928 | tf_op jit(solution)/shard_map/reshape | solution.py:151
  (1 shorter events, 0.0 us)
Async XLA Ops:
  7.2 92.5 %copy-start = (bf16[3456,512]{1,0:T(8,128)(2,1)S(1)}, bf16[3456,512]{1,0:T(8,128)(2,1)}, u32[]{:S(2)}) copy-start(bf16[3456,512]{1,0:T(8,128)(2,1)} %param.17) | copy-start | bytes 10616836
  22.2 41.2 %copy-start.2 = (s32[3328]{0:T(1024)}, s32[3328]{0:T(1024)S(1)}, u32[]{:S(2)}) copy-start(s32[3328]{0:T(1024)S(1)} %fusion.18) | copy-start | bytes 39940
  47.1 0.6 copy-start.1
  63.4 22.1 %all-to-all-start.1 = ((bf16[8,624,128]{2,1,0:T(8,128)(2,1)}), bf16[8,624,128]{2,1,0:T(8,128)(2,1)}, u32[]{:S(2)}, u32[]{:S(2)}) async-start(bf16[8,624,128]{2,1,0:T(8,128)(2,1)} %bitcast.33), calls=%async_computation.1 | async-start | bytes 2555904 | tf_op jit(solution)/shard_map/all_to_all | solution.py:105
  132.3 22.1 %all-to-all-start.2 = ((bf16[8,624,128]{2,1,0:T(8,128)(2,1)}), bf16[8,624,128]{2,1,0:T(8,128)(2,1)}, u32[]{:S(2)}, u32[]{:S(2)}) async-start(bf16[8,624,128]{2,1,0:T(8,128)(2,1)} %bitcast.32), calls=%async_computation.2 | async-start | bytes 2555904 | tf_op jit(solution)/shard_map/all_to_all | solution.py:137
  136.5 76.7 %all-reduce.2.cloned.1.call-start = ((), (), s32[]{:S(2)}) async-start(), calls=%async_computation.3 | async-start | bytes 1277952 | tf_op jit(solution)/shard_map/psum | solution.py:150
Sparse Core Ops, SparseCore 0:
  169.7 40.0 all-reduce.1

commit v11 on v10

--- a/solution.py
+++ b/solution.py
@@ -145,9 +145,9 @@
         table_count * rows_local,
         received_flat,
         incoming.reshape(slot_count, row_width),
-        jnp.float32,
+        jnp.bfloat16,
     )
-    summed_grad = lax.psum(local_grad.astype(jnp.bfloat16), "grp").astype(jnp.float32)
+    summed_grad = lax.psum(local_grad, "grp").astype(jnp.float32)
     table_grad = summed_grad.reshape(table_count, rows_local, row_width)
     bias_local = jnp.sum(scaled, axis=0)
     bias_grad = lax.psum(bias_local, ("grp", "emb"))

time: 225 us -> 222 us (0.987)
  no operation moved by 1% of the time
where the time goes in v11:
time: 222 us; the launch traced here: 220 us
  local copies, waits for them, and re-layouts  71.5 us (32%)
  blocking collectives  50.1 us (23%)
  waiting for transfers between devices  28.3 us (13%)
  other arithmetic  23.1 us (10%)
  between operations  14.1 us (6%)
  Pallas kernels  12.7 us (6%)
  matrix products  11.6 us (5%)
  starting transfers between devices  8.55 us (4%)
    psum x1, blocking collectives, local(): bias_grad = lax.psum(bias_local, ('grp', 'emb'))  40.2 us
    all_to_all x1, waiting for transfers between devices, local(): lax.all_to_all(outgoing.reshape(owner_count, capacity, row_width), 'emb',...  15 us
    scatter x1, local copies, waits for them, and re-layouts, local(): jnp.zeros((slot_count, row_width), jnp.bfloat16).at[buffer_place]  14.9 us
    scatter x1, local copies, waits for them, and re-layouts, local(): jnp.zeros((owner_count * capacity,), jnp.int32).at[buffer_place]  13.5 us
    all_to_all x1, waiting for transfers between devices, local(): lax.all_to_all(fetched, 'emb', split_axis=0, concat_axis=0, tiled=True)  13.2 us
    pallas_call x1, Pallas kernels, add_rows(): pl.pallas_call(functools.partial(_select_kernel, chunk, padded // chunk),...  12.7 us
    gather x1, local copies, waits for them, and re-layouts, local(): fetched = flat_table[received]  12.3 us
    all_to_all x1, blocking collectives, local(): lax.all_to_all(request, 'emb', split_axis=0, concat_axis=0, tiled=True)  9.94 us
  transfers between devices with their start and end apart: 3, of which 2 were waited for; matrix products, arithmetic and copies ran while one was open for 5% of the time, Pallas kernels for 0%

profile of v11, /device:TPU:0, one launch (start us, length us, event | category | flops | bytes accessed | tf_op | source)
XLA Modules:
  0.0 219.9 jit_solution(5813715203490944605)
XLA Ops:
  7.2 0.0 copy-start
  7.2 0.9 broadcast_add_fusion
  8.1 0.7 copy.16
  8.9 1.6 reshape.125
  10.4 0.7 reduce
  11.2 0.7 fusion.14
  11.9 5.2 %reduce-window.6 = s32[8,26,128]{2,1,0:T(8,128)} reduce-window(s32[8,26,128]{2,1,0:T(8,128)} %fusion.14, s32[]{:T(128)} %constant.9.clone.1), window={size=1x1x128 pad=0_0x0_0x127_0}, to_apply=%region_0.0 | reduce-window | flops 3381248 | bytes 212996 | tf_op jit(solution)/shard_map/reduce-window
  17.1 1.8 slice_reduce_fusion
  18.9 1.5 reduce-window.9
  20.3 1.0 add_bitcast_fusion
  21.4 0.1 fusion.16
  21.5 0.8 fusion.18
  22.2 0.0 copy-start.2
  22.2 13.5 %scatter_custom_fusion = s32[4992]{0:T(1024)} fusion(s32[3328]{0:T(1024)S(1)} %fusion.18, s32[3328]{0:T(1024)} %reshape.125, s32[]{:T(128)} %constant.9.clone.1), kind=kCustom, calls=%fused_computation.34 | custom fusion | bytes 20480 | tf_op jit(solution)/shard_map/scatter | solution.py:99
  35.7 1.4 all_to_all.14
  37.1 9.9 %all_to_all.22 = s32[8,1,624]{2,1,0:T(1,128)S(1)} all-to-all(s32[8,1,624]{2,1,0:T(1,128)} %all_to_all.14), channel_id=1, replica_groups=mesh['grp'=4,'emb'=8] {'emb'}, dimensions={0} | all-to-all | bytes 39936 | tf_op jit(solution)/shard_map/all_to_all | solution.py:101
  47.1 0.0 copy-start.1
  47.1 0.6 copy-done.1
  47.7 0.7 fusion.17
  48.3 1.4 reshape.107
  49.8 1.3 pad_clamp_fusion
  51.1 12.3 %gather_fusion = bf16[4992,128]{1,0:T(8,128)(2,1)} fusion(bf16[2496,128]{1,0:T(8,128)(2,1)} %bitcast.31, s32[5120]{0:T(1024)} %pad_clamp_fusion), kind=kCustom, calls=%fused_computation | custom fusion | bytes 2575872 | tf_op jit(solution)/shard_map/gather | solution.py:104
  63.4 0.0 copy-done.2
  63.4 4.3 %all-to-all-start.1 = ((bf16[8,624,128]{2,1,0:T(8,128)(2,1)}), bf16[8,624,128]{2,1,0:T(8,128)(2,1)}, u32[]{:S(2)}, u32[]{:S(2)}) async-start(bf16[8,624,128]{2,1,0:T(8,128)(2,1)} %bitcast.33), calls=%async_computation.1 | async-start | bytes 2555904 | tf_op jit(solution)/shard_map/all_to_all | solution.py:105
  67.6 0.7 convert_element_type.31
  68.3 1.3 pad_clamp_fusion.1
  69.7 1.4 constant_dynamic-update-slice_fusion.1
  71.1 1.2 select_reduce_fusion
  72.3 13.2 %all-to-all-done.1 = bf16[8,624,128]{2,1,0:T(8,128)(2,1)} async-done(((bf16[8,624,128]{2,1,0:T(8,128)(2,1)}), bf16[8,624,128]{2,1,0:T(8,128)(2,1)}, u32[]{:S(2)}, u32[]{:S(2)}) %all-to-all-start.1) | async-done | bytes 1277984 | tf_op jit(solution)/shard_map/all_to_all | solution.py:105
  85.5 9.2 %gather_fusion.1 = bf16[3328,128]{1,0:T(8,128)(2,1)} fusion(bf16[4992,128]{1,0:T(8,128)(2,1)} %bitcast.4, s32[4096]{0:T(1024)} %pad_clamp_fusion.1), kind=kCustom, calls=%fused_computation.1 | custom fusion | bytes 1717248 | tf_op jit(solution)/shard_map/gather | solution.py:106
  94.7 2.8 %reshape.99 = bf16[128,3328]{1,0:T(8,128)(2,1)} reshape(bf16[3328,128]{1,0:T(8,128)(2,1)} %gather_fusion.1) | data formatting | bytes 1703936 | tf_op jit(solution)/shard_map/reshape | solution.py:106
  97.5 2.1 constant_dynamic-update-slice_fusion
  99.6 0.0 copy-done
  99.6 5.6 %fusion.4 = (f32[128]{0:T(128)}, f32[128,3456]{1,0:T(8,128)}) fusion(bf16[128,3456]{1,0:T(8,128)(2,1)} %constant_dynamic-update-slice_fusion, f32[3456]{0:T(1024)S(1)} %convert_element_type.31, f32[3456]{0:T(1024)} %param.19, bf16[512,3456]{1,0:T(8,128)(2,1)} %param.18, bf16[3456,512]{1,0:T(8,128)(2,1)S(1)} %copy-done), kind=kOutput, calls=%fused_computation.13 | convolution fusion | flops 908689280 | bytes 9760256 | tf_op jit(solution)/shard_map/dot_general | solution.py:113
  105.2 1.2 divide_subtract_fusion
  106.4 6.1 %fusion = bf16[128,3456]{1,0:T(8,128)(2,1)} fusion(bf16[3456,512]{1,0:T(8,128)(2,1)S(1)} %copy-done, f32[128,3456]{1,0:T(8,128)} %get-tuple-element.4, bf16[512,3456]{1,0:T(8,128)(2,1)} %param.18, bf16[128,3456]{1,0:T(8,128)(2,1)} %constant_dynamic-update-slice_fusion, f32[128]{0:T(128)} %divide_subtract_fusion, f32[3456]{0:T(1024)S(1)} %convert_element_type.31), kind=kOutput, calls=%fused_computation.6 | convolution fusion | flops 910016512 | bytes 10631168 | tf_op jit(solution)/shard_map/dot_general | solution.py:130
  112.4 2.1 slice.21
  114.5 2.9 %reshape.133 = bf16[3328,128]{1,0:T(8,128)(2,1)} reshape(bf16[128,3328]{1,0:T(8,128)(2,1)} %slice.21) | data formatting | bytes 1703936 | tf_op jit(solution)/shard_map/reshape | solution.py:135
  117.4 14.9 %scatter_custom_fusion.1 = bf16[4992,128]{1,0:T(8,128)(2,1)} fusion(s32[3328]{0:T(1024)} %copy-done.2, bf16[3328,128]{1,0:T(8,128)(2,1)} %reshape.133, bf16[]{:T(256)} %constant.5.clone.1), kind=kCustom, calls=%fused_computation.18 | custom fusion | bytes 1278464 | tf_op jit(solution)/shard_map/scatter | solution.py:136
  132.3 4.3 %all-to-all-start.2 = ((bf16[8,624,128]{2,1,0:T(8,128)(2,1)}), bf16[8,624,128]{2,1,0:T(8,128)(2,1)}, u32[]{:S(2)}, u32[]{:S(2)}) async-start(bf16[8,624,128]{2,1,0:T(8,128)(2,1)} %bitcast.32), calls=%async_computation.2 | async-start | bytes 2555904 | tf_op jit(solution)/shard_map/all_to_all | solution.py:137
  136.5 0.0 all-reduce.2.cloned.1.call-start
  136.6 1.4 reduce.4
  138.0 1.4 reshape_reshape.4.right_ref
  139.4 15.0 %all-to-all-done.2 = bf16[8,624,128]{2,1,0:T(8,128)(2,1)} async-done(((bf16[8,624,128]{2,1,0:T(8,128)(2,1)}), bf16[8,624,128]{2,1,0:T(8,128)(2,1)}, u32[]{:S(2)}, u32[]{:S(2)}) %all-to-all-start.2) | async-done | bytes 1277984 | tf_op jit(solution)/shard_map/all_to_all | solution.py:137
  154.4 12.7 %shard_map.130 = bf16[2496,128]{1,0:T(8,128)(2,1)} custom-call(s32[1,4992]{1,0:T(1,128)} %reshape_reshape.4.right_ref, bf16[4992,128]{1,0:T(8,128)(2,1)} %bitcast.6.data_ref), custom_call_target="tpu_custom_call" | custom-call | flops 3189768192 | bytes 1916928 | tf_op jit(solution)/shard_map/pallas_call | solution.py:51
  167.1 0.0 all-reduce.2.cloned.1.call-update
  167.2 1.4 slice.22
  168.5 2.1 fusion.1
  170.6 40.2 %psum.15 = f32[3456]{0:T(1024)} all-reduce(f32[3456]{0:T(1024)} %fusion.1), channel_id=1, replica_groups=mesh['grp'=4,'emb'=8] {'grp','emb'}, use_global_device_ids=true, to_apply=%region_9.10 | all-reduce | flops 3456 | bytes 27648 | tf_op jit(solution)/shard_map/psum | solution.py:153
  210.8 0.0 all-reduce.2.cloned.1.call-done
  210.8 2.3 %reshape.104 = f32[26,96,128]{2,1,0:T(8,128)} convert(bf16[26,96,128]{2,1,0:T(8,128)(2,1)} %all-reduce.2.cloned.1.call-done) | non-fusion elementwise | flops 319488 | bytes 1916928 | tf_op jit(solution)/shard_map/reshape | solution.py:151
  (1 shorter events, 0.0 us)
Async XLA Ops:
  7.2 92.5 %copy-start = (bf16[3456,512]{1,0:T(8,128)(2,1)S(1)}, bf16[3456,512]{1,0:T(8,128)(2,1)}, u32[]{:S(2)}) copy-start(bf16[3456,512]{1,0:T(8,128)(2,1)} %param.17) | copy-start | bytes 10616836
  22.2 41.2 %copy-start.2 = (s32[3328]{0:T(1024)}, s32[3328]{0:T(1024)S(1)}, u32[]{:S(2)}) copy-start(s32[3328]{0:T(1024)S(1)} %fusion.18) | copy-start | bytes 39940
  47.1 0.6 copy-start.1
  63.4 22.1 %all-to-all-start.1 = ((bf16[8,624,128]{2,1,0:T(8,128)(2,1)}), bf16[8,624,128]{2,1,0:T(8,128)(2,1)}, u32[]{:S(2)}, u32[]{:S(2)}) async-start(bf16[8,624,128]{2,1,0:T(8,128)(2,1)} %bitcast.33), calls=%async_computation.1 | async-start | bytes 2555904 | tf_op jit(solution)/shard_map/all_to_all | solution.py:105
  132.3 22.1 %all-to-all-start.2 = ((bf16[8,624,128]{2,1,0:T(8,128)(2,1)}), bf16[8,624,128]{2,1,0:T(8,128)(2,1)}, u32[]{:S(2)}, u32[]{:S(2)}) async-start(bf16[8,624,128]{2,1,0:T(8,128)(2,1)} %bitcast.32), calls=%async_computation.2 | async-start | bytes 2555904 | tf_op jit(solution)/shard_map/all_to_all | solution.py:137
  136.5 74.3 %all-reduce.2.cloned.1.call-start = ((), (), s32[]{:S(2)}) async-start(), calls=%async_computation.3 | async-start | bytes 1277952 | tf_op jit(solution)/shard_map/psum | solution.py:150
Sparse Core Ops, SparseCore 0:
  167.3 40.0 all-reduce.1

commit v12 on v11

--- a/solution.py
+++ b/solution.py
@@ -141,6 +141,8 @@
         concat_axis=0,
         tiled=True,
     )
+    bias_local = jnp.sum(scaled, axis=0)
+    bias_local, bottom_grad, incoming = lax.optimization_barrier((bias_local, bottom_grad, incoming))
     local_grad = add_rows(
         table_count * rows_local,
         received_flat,
@@ -149,7 +151,6 @@
     )
     summed_grad = lax.psum(local_grad, "grp").astype(jnp.float32)
     table_grad = summed_grad.reshape(table_count, rows_local, row_width)
-    bias_local = jnp.sum(scaled, axis=0)
     bias_grad = lax.psum(bias_local, ("grp", "emb"))
     return (table_grad, bottom_grad, bias_grad)
 

time: 222 us -> 219 us (0.986)
  waiting for transfers between devices: 28.3 us -> 25 us
    all_to_all x1, waiting for transfers between devices: 15 us -> 11.5 us  [local(): lax.all_to_all(outgoing.reshape(owner_count, capacity, row_width), 'emb',...]
  transfers between devices with their start and end apart: 3 -> 3, of which waited for: 2 -> 3; matrix products, arithmetic and copies ran while one was open for 5% -> 5% of each run, Pallas kernels for 0% -> 0%
where the time goes in v12:
time: 219 us; the launch traced here: 216 us
  local copies, waits for them, and re-layouts  71.5 us (33%)
  blocking collectives  49.7 us (23%)
  waiting for transfers between devices  25 us (11%)
  other arithmetic  23.1 us (11%)
  between operations  14.1 us (6%)
  Pallas kernels  12.7 us (6%)
  matrix products  11.6 us (5%)
  starting transfers between devices  8.55 us (4%)
    psum x1, blocking collectives, local(): bias_grad = lax.psum(bias_local, ('grp', 'emb'))  39.8 us
    scatter x1, local copies, waits for them, and re-layouts, local(): jnp.zeros((slot_count, row_width), jnp.bfloat16).at[buffer_place]  14.9 us
    scatter x1, local copies, waits for them, and re-layouts, local(): jnp.zeros((owner_count * capacity,), jnp.int32).at[buffer_place]  13.5 us
    all_to_all x1, waiting for transfers between devices, local(): lax.all_to_all(fetched, 'emb', split_axis=0, concat_axis=0, tiled=True)  13.2 us
    pallas_call x1, Pallas kernels, add_rows(): pl.pallas_call(functools.partial(_select_kernel, chunk, padded // chunk),...  12.7 us
    gather x1, local copies, waits for them, and re-layouts, local(): fetched = flat_table[received]  12.3 us
    all_to_all x1, waiting for transfers between devices, local(): lax.all_to_all(outgoing.reshape(owner_count, capacity, row_width), 'emb',...  11.5 us
    all_to_all x1, blocking collectives, local(): lax.all_to_all(request, 'emb', split_axis=0, concat_axis=0, tiled=True)  9.94 us
  transfers between devices with their start and end apart: 3, of which 3 were waited for; matrix products, arithmetic and copies ran while one was open for 5% of the time, Pallas kernels for 0%

profile of v12, /device:TPU:0, one launch (start us, length us, event | category | flops | bytes accessed | tf_op | source)
XLA Modules:
  0.0 216.3 jit_solution(1463810025913351922)
XLA Ops:
  7.2 0.0 copy-start
  7.2 0.9 broadcast_add_fusion
  8.1 0.7 copy.16
  8.9 1.6 reshape.125
  10.4 0.7 reduce
  11.2 0.7 fusion.14
  11.9 5.2 %reduce-window.6 = s32[8,26,128]{2,1,0:T(8,128)} reduce-window(s32[8,26,128]{2,1,0:T(8,128)} %fusion.14, s32[]{:T(128)} %constant.9.clone.1), window={size=1x1x128 pad=0_0x0_0x127_0}, to_apply=%region_0.0 | reduce-window | flops 3381248 | bytes 212996 | tf_op jit(solution)/shard_map/reduce-window
  17.1 1.8 slice_reduce_fusion
  18.9 1.5 reduce-window.9
  20.3 1.0 add_bitcast_fusion
  21.4 0.1 fusion.16
  21.5 0.8 fusion.18
  22.2 0.0 copy-start.3
  22.2 13.5 %scatter_custom_fusion = s32[4992]{0:T(1024)} fusion(s32[3328]{0:T(1024)S(1)} %fusion.18, s32[3328]{0:T(1024)} %reshape.125, s32[]{:T(128)} %constant.9.clone.1), kind=kCustom, calls=%fused_computation.34 | custom fusion | bytes 20480 | tf_op jit(solution)/shard_map/scatter | solution.py:99
  35.7 1.4 all_to_all.14
  37.1 9.9 %all_to_all.22 = s32[8,1,624]{2,1,0:T(1,128)S(1)} all-to-all(s32[8,1,624]{2,1,0:T(1,128)} %all_to_all.14), channel_id=1, replica_groups=mesh['grp'=4,'emb'=8] {'emb'}, dimensions={0} | all-to-all | bytes 39936 | tf_op jit(solution)/shard_map/all_to_all | solution.py:101
  47.1 0.0 copy-start.1
  47.1 0.6 copy-done.1
  47.7 0.7 fusion.17
  48.3 1.4 reshape.107
  49.8 1.3 pad_clamp_fusion
  51.1 12.3 %gather_fusion = bf16[4992,128]{1,0:T(8,128)(2,1)} fusion(bf16[2496,128]{1,0:T(8,128)(2,1)} %bitcast.31, s32[5120]{0:T(1024)} %pad_clamp_fusion), kind=kCustom, calls=%fused_computation | custom fusion | bytes 2575872 | tf_op jit(solution)/shard_map/gather | solution.py:104
  63.4 0.0 copy-done.3
  63.4 4.3 %all-to-all-start.1 = ((bf16[8,624,128]{2,1,0:T(8,128)(2,1)}), bf16[8,624,128]{2,1,0:T(8,128)(2,1)}, u32[]{:S(2)}, u32[]{:S(2)}) async-start(bf16[8,624,128]{2,1,0:T(8,128)(2,1)} %bitcast.33), calls=%async_computation.1 | async-start | bytes 2555904 | tf_op jit(solution)/shard_map/all_to_all | solution.py:105
  67.6 0.7 convert_element_type.31
  68.3 1.3 pad_clamp_fusion.1
  69.7 1.4 constant_dynamic-update-slice_fusion.1
  71.1 1.2 select_reduce_fusion
  72.3 13.2 %all-to-all-done.1 = bf16[8,624,128]{2,1,0:T(8,128)(2,1)} async-done(((bf16[8,624,128]{2,1,0:T(8,128)(2,1)}), bf16[8,624,128]{2,1,0:T(8,128)(2,1)}, u32[]{:S(2)}, u32[]{:S(2)}) %all-to-all-start.1) | async-done | bytes 1277984 | tf_op jit(solution)/shard_map/all_to_all | solution.py:105
  85.5 9.2 %gather_fusion.1 = bf16[3328,128]{1,0:T(8,128)(2,1)} fusion(bf16[4992,128]{1,0:T(8,128)(2,1)} %bitcast.4, s32[4096]{0:T(1024)} %pad_clamp_fusion.1), kind=kCustom, calls=%fused_computation.1 | custom fusion | bytes 1717248 | tf_op jit(solution)/shard_map/gather | solution.py:106
  94.7 2.8 %reshape.99 = bf16[128,3328]{1,0:T(8,128)(2,1)} reshape(bf16[3328,128]{1,0:T(8,128)(2,1)} %gather_fusion.1) | data formatting | bytes 1703936 | tf_op jit(solution)/shard_map/reshape | solution.py:106
  97.5 2.1 constant_dynamic-update-slice_fusion
  99.6 0.0 copy-done
  99.6 5.6 %fusion.4 = (f32[128]{0:T(128)}, f32[128,3456]{1,0:T(8,128)}) fusion(bf16[128,3456]{1,0:T(8,128)(2,1)} %constant_dynamic-update-slice_fusion, f32[3456]{0:T(1024)S(1)} %convert_element_type.31, f32[3456]{0:T(1024)} %param.19, bf16[512,3456]{1,0:T(8,128)(2,1)} %param.18, bf16[3456,512]{1,0:T(8,128)(2,1)S(1)} %copy-done), kind=kOutput, calls=%fused_computation.13 | convolution fusion | flops 908689280 | bytes 9760256 | tf_op jit(solution)/shard_map/dot_general | solution.py:113
  105.2 1.2 divide_subtract_fusion
  106.4 6.1 %fusion = bf16[128,3456]{1,0:T(8,128)(2,1)} fusion(bf16[3456,512]{1,0:T(8,128)(2,1)S(1)} %copy-done, f32[128,3456]{1,0:T(8,128)} %get-tuple-element.10, bf16[512,3456]{1,0:T(8,128)(2,1)} %param.18, bf16[128,3456]{1,0:T(8,128)(2,1)} %constant_dynamic-update-slice_fusion, f32[128]{0:T(128)} %divide_subtract_fusion, f32[3456]{0:T(1024)S(1)} %convert_element_type.31), kind=kOutput, calls=%fused_computation.6 | convolution fusion | flops 910016512 | bytes 10631168 | tf_op jit(solution)/shard_map/dot_general | solution.py:130
  112.4 2.1 slice.22
  114.5 2.9 %reshape.133 = bf16[3328,128]{1,0:T(8,128)(2,1)} reshape(bf16[128,3328]{1,0:T(8,128)(2,1)} %slice.22) | data formatting | bytes 1703936 | tf_op jit(solution)/shard_map/reshape | solution.py:135
  117.4 14.9 %scatter_custom_fusion.1 = bf16[4992,128]{1,0:T(8,128)(2,1)} fusion(s32[3328]{0:T(1024)} %copy-done.3, bf16[3328,128]{1,0:T(8,128)(2,1)} %reshape.133, bf16[]{:T(256)} %constant.8.clone.1), kind=kCustom, calls=%fused_computation.18 | custom fusion | bytes 1278464 | tf_op jit(solution)/shard_map/scatter | solution.py:136
  132.3 4.3 %all-to-all-start.2 = ((bf16[8,624,128]{2,1,0:T(8,128)(2,1)}), bf16[8,624,128]{2,1,0:T(8,128)(2,1)}, u32[]{:S(2)}, u32[]{:S(2)}) async-start(bf16[8,624,128]{2,1,0:T(8,128)(2,1)} %bitcast.32), calls=%async_computation.2 | async-start | bytes 2555904 | tf_op jit(solution)/shard_map/all_to_all | solution.py:137
  136.5 0.0 all-reduce.2.cloned.1.call-start
  136.6 1.4 reduce.4
  138.0 1.4 reshape_reshape.4.right_ref
  139.4 1.4 slice.21
  140.8 2.1 fusion.2
  142.9 11.5 %all-to-all-done.2 = bf16[8,624,128]{2,1,0:T(8,128)(2,1)} async-done(((bf16[8,624,128]{2,1,0:T(8,128)(2,1)}), bf16[8,624,128]{2,1,0:T(8,128)(2,1)}, u32[]{:S(2)}, u32[]{:S(2)}) %all-to-all-start.2) | async-done | bytes 1277984 | tf_op jit(solution)/shard_map/all_to_all | solution.py:137
  154.4 0.0 copy-start.2
  154.4 12.7 %shard_map.130 = bf16[2496,128]{1,0:T(8,128)(2,1)} custom-call(s32[1,4992]{1,0:T(1,128)} %reshape_reshape.4.right_ref, bf16[4992,128]{1,0:T(8,128)(2,1)} %bitcast.6.data_ref), custom_call_target="tpu_custom_call" | custom-call | flops 3189768192 | bytes 1916928 | tf_op jit(solution)/shard_map/pallas_call | solution.py:51
  167.2 0.0 all-reduce.2.cloned.1.call-update
  167.2 0.0 copy-done.2
  167.2 39.8 %psum.15 = f32[3456]{0:T(1024)} all-reduce(f32[3456]{0:T(1024)S(1)} %copy-done.2), channel_id=1, replica_groups=mesh['grp'=4,'emb'=8] {'grp','emb'}, use_global_device_ids=true, to_apply=%region_9.10 | all-reduce | flops 3456 | bytes 27648 | tf_op jit(solution)/shard_map/psum | solution.py:154
  207.0 0.3 all-reduce.2.cloned.1.call-done
  207.2 2.3 %reshape.104 = f32[26,96,128]{2,1,0:T(8,128)} convert(bf16[26,96,128]{2,1,0:T(8,128)(2,1)} %all-reduce.2.cloned.1.call-done) | non-fusion elementwise | flops 319488 | bytes 1916928 | tf_op jit(solution)/shard_map/reshape | solution.py:153
  (1 shorter events, 0.0 us)
Async XLA Ops:
  7.2 92.5 %copy-start = (bf16[3456,512]{1,0:T(8,128)(2,1)S(1)}, bf16[3456,512]{1,0:T(8,128)(2,1)}, u32[]{:S(2)}) copy-start(bf16[3456,512]{1,0:T(8,128)(2,1)} %param.17) | copy-start | bytes 10616836
  22.2 41.2 %copy-start.3 = (s32[3328]{0:T(1024)}, s32[3328]{0:T(1024)S(1)}, u32[]{:S(2)}) copy-start(s32[3328]{0:T(1024)S(1)} %fusion.18) | copy-start | bytes 39940
  47.1 0.6 copy-start.1
  63.4 22.1 %all-to-all-start.1 = ((bf16[8,624,128]{2,1,0:T(8,128)(2,1)}), bf16[8,624,128]{2,1,0:T(8,128)(2,1)}, u32[]{:S(2)}, u32[]{:S(2)}) async-start(bf16[8,624,128]{2,1,0:T(8,128)(2,1)} %bitcast.33), calls=%async_computation.1 | async-start | bytes 2555904 | tf_op jit(solution)/shard_map/all_to_all | solution.py:105
  132.3 22.1 %all-to-all-start.2 = ((bf16[8,624,128]{2,1,0:T(8,128)(2,1)}), bf16[8,624,128]{2,1,0:T(8,128)(2,1)}, u32[]{:S(2)}, u32[]{:S(2)}) async-start(bf16[8,624,128]{2,1,0:T(8,128)(2,1)} %bitcast.32), calls=%async_computation.2 | async-start | bytes 2555904 | tf_op jit(solution)/shard_map/all_to_all | solution.py:137
  136.5 70.7 %all-reduce.2.cloned.1.call-start = ((), (), s32[]{:S(2)}) async-start(), calls=%async_computation.3 | async-start | bytes 1277952 | tf_op jit(solution)/shard_map/psum | solution.py:152
  154.4 12.8 %copy-start.2 = (f32[3456]{0:T(1024)S(1)}, f32[3456]{0:T(1024)}, u32[]{:S(2)}) copy-start(f32[3456]{0:T(1024)} %fusion.2) | copy-start | bytes 41476
Sparse Core Ops, SparseCore 0:
  167.3 39.8 all-reduce.1

commit v13 on v12

--- a/solution.py
+++ b/solution.py
@@ -17,7 +17,7 @@
 
 
 def _chunk_of(count):
-    for size in (512, 384, 256, 128):
+    for size in (1664, 512, 384, 256, 128):
         if count % size == 0:
             return size
     return 512

time: 219 us -> 216 us (0.986)
  Pallas kernels: 12.7 us -> 9.7 us
    pallas_call x1, Pallas kernels: 12.7 us -> 9.7 us  [add_rows(): pl.pallas_call(functools.partial(_select_kernel, chunk, padded // chunk),...]
where the time goes in v13:
time: 216 us; the launch traced here: 213 us
  local copies, waits for them, and re-layouts  71.5 us (33%)
  blocking collectives  49.7 us (23%)
  waiting for transfers between devices  24.9 us (12%)
  other arithmetic  23.1 us (11%)
  between operations  14.1 us (7%)
  matrix products  11.6 us (5%)
  Pallas kernels  9.7 us (4%)
  starting transfers between devices  8.73 us (4%)
    psum x1, blocking collectives, local(): bias_grad = lax.psum(bias_local, ('grp', 'emb'))  39.8 us
    scatter x1, local copies, waits for them, and re-layouts, local(): jnp.zeros((slot_count, row_width), jnp.bfloat16).at[buffer_place]  14.9 us
    scatter x1, local copies, waits for them, and re-layouts, local(): jnp.zeros((owner_count * capacity,), jnp.int32).at[buffer_place]  13.5 us
    all_to_all x1, waiting for transfers between devices, local(): lax.all_to_all(fetched, 'emb', split_axis=0, concat_axis=0, tiled=True)  13.2 us
    gather x1, local copies, waits for them, and re-layouts, local(): fetched = flat_table[received]  12.3 us
    all_to_all x1, waiting for transfers between devices, local(): lax.all_to_all(outgoing.reshape(owner_count, capacity, row_width), 'emb',...  11.4 us
    all_to_all x1, blocking collectives, local(): lax.all_to_all(request, 'emb', split_axis=0, concat_axis=0, tiled=True)  9.94 us
    pallas_call x1, Pallas kernels, add_rows(): pl.pallas_call(functools.partial(_select_kernel, chunk, padded // chunk),...  9.7 us
  transfers between devices with their start and end apart: 3, of which 3 were waited for; matrix products, arithmetic and copies ran while one was open for 5% of the time, Pallas kernels for 0%

profile of v13, /device:TPU:0, one launch (start us, length us, event | category | flops | bytes accessed | tf_op | source)
XLA Modules:
  0.0 213.3 jit_solution(14074254123782818309)
XLA Ops:
  7.2 0.0 copy-start
  7.2 0.9 broadcast_add_fusion
  8.1 0.7 copy.16
  8.9 1.6 reshape.125
  10.4 0.7 reduce
  11.2 0.7 fusion.14
  11.9 5.2 %reduce-window.6 = s32[8,26,128]{2,1,0:T(8,128)} reduce-window(s32[8,26,128]{2,1,0:T(8,128)} %fusion.14, s32[]{:T(128)} %constant.9.clone.1), window={size=1x1x128 pad=0_0x0_0x127_0}, to_apply=%region_0.0 | reduce-window | flops 3381248 | bytes 212996 | tf_op jit(solution)/shard_map/reduce-window
  17.1 1.8 slice_reduce_fusion
  18.9 1.5 reduce-window.9
  20.3 1.0 add_bitcast_fusion
  21.4 0.1 fusion.16
  21.5 0.8 fusion.18
  22.2 0.0 copy-start.3
  22.2 13.5 %scatter_custom_fusion = s32[4992]{0:T(1024)} fusion(s32[3328]{0:T(1024)S(1)} %fusion.18, s32[3328]{0:T(1024)} %reshape.125, s32[]{:T(128)} %constant.9.clone.1), kind=kCustom, calls=%fused_computation.34 | custom fusion | bytes 20480 | tf_op jit(solution)/shard_map/scatter | solution.py:99
  35.7 1.4 all_to_all.14
  37.1 9.9 %all_to_all.22 = s32[8,1,624]{2,1,0:T(1,128)S(1)} all-to-all(s32[8,1,624]{2,1,0:T(1,128)} %all_to_all.14), channel_id=1, replica_groups=mesh['grp'=4,'emb'=8] {'emb'}, dimensions={0} | all-to-all | bytes 39936 | tf_op jit(solution)/shard_map/all_to_all | solution.py:101
  47.1 0.0 copy-start.1
  47.1 0.6 copy-done.1
  47.7 0.7 fusion.17
  48.3 1.4 reshape.107
  49.8 1.3 pad_clamp_fusion
  51.1 12.3 %gather_fusion = bf16[4992,128]{1,0:T(8,128)(2,1)} fusion(bf16[2496,128]{1,0:T(8,128)(2,1)} %bitcast.31, s32[5120]{0:T(1024)} %pad_clamp_fusion), kind=kCustom, calls=%fused_computation | custom fusion | bytes 2575872 | tf_op jit(solution)/shard_map/gather | solution.py:104
  63.4 0.0 copy-done.3
  63.4 4.3 %all-to-all-start.1 = ((bf16[8,624,128]{2,1,0:T(8,128)(2,1)}), bf16[8,624,128]{2,1,0:T(8,128)(2,1)}, u32[]{:S(2)}, u32[]{:S(2)}) async-start(bf16[8,624,128]{2,1,0:T(8,128)(2,1)} %bitcast.33), calls=%async_computation.1 | async-start | bytes 2555904 | tf_op jit(solution)/shard_map/all_to_all | solution.py:105
  67.6 0.7 convert_element_type.31
  68.3 1.3 pad_clamp_fusion.1
  69.7 1.4 constant_dynamic-update-slice_fusion.1
  71.1 1.2 select_reduce_fusion
  72.3 13.2 %all-to-all-done.1 = bf16[8,624,128]{2,1,0:T(8,128)(2,1)} async-done(((bf16[8,624,128]{2,1,0:T(8,128)(2,1)}), bf16[8,624,128]{2,1,0:T(8,128)(2,1)}, u32[]{:S(2)}, u32[]{:S(2)}) %all-to-all-start.1) | async-done | bytes 1277984 | tf_op jit(solution)/shard_map/all_to_all | solution.py:105
  85.5 9.2 %gather_fusion.1 = bf16[3328,128]{1,0:T(8,128)(2,1)} fusion(bf16[4992,128]{1,0:T(8,128)(2,1)} %bitcast.4, s32[4096]{0:T(1024)} %pad_clamp_fusion.1), kind=kCustom, calls=%fused_computation.1 | custom fusion | bytes 1717248 | tf_op jit(solution)/shard_map/gather | solution.py:106
  94.7 2.8 %reshape.99 = bf16[128,3328]{1,0:T(8,128)(2,1)} reshape(bf16[3328,128]{1,0:T(8,128)(2,1)} %gather_fusion.1) | data formatting | bytes 1703936 | tf_op jit(solution)/shard_map/reshape | solution.py:106
  97.5 2.1 constant_dynamic-update-slice_fusion
  99.6 0.0 copy-done
  99.6 5.6 %fusion.4 = (f32[128]{0:T(128)}, f32[128,3456]{1,0:T(8,128)}) fusion(bf16[128,3456]{1,0:T(8,128)(2,1)} %constant_dynamic-update-slice_fusion, f32[3456]{0:T(1024)S(1)} %convert_element_type.31, f32[3456]{0:T(1024)} %param.19, bf16[512,3456]{1,0:T(8,128)(2,1)} %param.18, bf16[3456,512]{1,0:T(8,128)(2,1)S(1)} %copy-done), kind=kOutput, calls=%fused_computation.13 | convolution fusion | flops 908689280 | bytes 9760256 | tf_op jit(solution)/shard_map/dot_general | solution.py:113
  105.2 1.2 divide_subtract_fusion
  106.4 6.1 %fusion = bf16[128,3456]{1,0:T(8,128)(2,1)} fusion(bf16[3456,512]{1,0:T(8,128)(2,1)S(1)} %copy-done, f32[128,3456]{1,0:T(8,128)} %get-tuple-element.10, bf16[512,3456]{1,0:T(8,128)(2,1)} %param.18, bf16[128,3456]{1,0:T(8,128)(2,1)} %constant_dynamic-update-slice_fusion, f32[128]{0:T(128)} %divide_subtract_fusion, f32[3456]{0:T(1024)S(1)} %convert_element_type.31), kind=kOutput, calls=%fused_computation.6 | convolution fusion | flops 910016512 | bytes 10631168 | tf_op jit(solution)/shard_map/dot_general | solution.py:130
  112.4 2.1 slice.22
  114.5 2.9 %reshape.133 = bf16[3328,128]{1,0:T(8,128)(2,1)} reshape(bf16[128,3328]{1,0:T(8,128)(2,1)} %slice.22) | data formatting | bytes 1703936 | tf_op jit(solution)/shard_map/reshape | solution.py:135
  117.4 14.9 %scatter_custom_fusion.1 = bf16[4992,128]{1,0:T(8,128)(2,1)} fusion(s32[3328]{0:T(1024)} %copy-done.3, bf16[3328,128]{1,0:T(8,128)(2,1)} %reshape.133, bf16[]{:T(256)} %constant.8.clone.1), kind=kCustom, calls=%fused_computation.18 | custom fusion | bytes 1278464 | tf_op jit(solution)/shard_map/scatter | solution.py:136
  132.3 4.3 %all-to-all-start.2 = ((bf16[8,624,128]{2,1,0:T(8,128)(2,1)}), bf16[8,624,128]{2,1,0:T(8,128)(2,1)}, u32[]{:S(2)}, u32[]{:S(2)}) async-start(bf16[8,624,128]{2,1,0:T(8,128)(2,1)} %bitcast.32), calls=%async_computation.2 | async-start | bytes 2555904 | tf_op jit(solution)/shard_map/all_to_all | solution.py:137
  136.6 0.2 all-reduce.2.cloned.1.call-start
  136.8 1.4 reduce.4
  138.2 1.4 reshape_reshape.4.right_ref
  139.6 1.4 slice.21
  141.0 2.1 fusion.2
  143.1 11.4 %all-to-all-done.2 = bf16[8,624,128]{2,1,0:T(8,128)(2,1)} async-done(((bf16[8,624,128]{2,1,0:T(8,128)(2,1)}), bf16[8,624,128]{2,1,0:T(8,128)(2,1)}, u32[]{:S(2)}, u32[]{:S(2)}) %all-to-all-start.2) | async-done | bytes 1277984 | tf_op jit(solution)/shard_map/all_to_all | solution.py:137
  154.4 0.0 copy-start.2
  154.4 9.7 %shard_map.130 = bf16[2496,128]{1,0:T(8,128)(2,1)} custom-call(s32[1,4992]{1,0:T(1,128)} %reshape_reshape.4.right_ref, bf16[4992,128]{1,0:T(8,128)(2,1)} %bitcast.6.data_ref), custom_call_target="tpu_custom_call" | custom-call | flops 3189768192 | bytes 1916928 | tf_op jit(solution)/shard_map/pallas_call | solution.py:51
  164.1 0.0 all-reduce.2.cloned.1.call-update
  164.2 0.0 copy-done.2
  164.2 39.8 %psum.15 = f32[3456]{0:T(1024)} all-reduce(f32[3456]{0:T(1024)S(1)} %copy-done.2), channel_id=1, replica_groups=mesh['grp'=4,'emb'=8] {'grp','emb'}, use_global_device_ids=true, to_apply=%region_9.10 | all-reduce | flops 3456 | bytes 27648 | tf_op jit(solution)/shard_map/psum | solution.py:154
  203.9 0.3 all-reduce.2.cloned.1.call-done
  204.2 2.3 %reshape.104 = f32[26,96,128]{2,1,0:T(8,128)} convert(bf16[26,96,128]{2,1,0:T(8,128)(2,1)} %all-reduce.2.cloned.1.call-done) | non-fusion elementwise | flops 319488 | bytes 1916928 | tf_op jit(solution)/shard_map/reshape | solution.py:153
  (1 shorter events, 0.0 us)
Async XLA Ops:
  7.2 92.5 %copy-start = (bf16[3456,512]{1,0:T(8,128)(2,1)S(1)}, bf16[3456,512]{1,0:T(8,128)(2,1)}, u32[]{:S(2)}) copy-start(bf16[3456,512]{1,0:T(8,128)(2,1)} %param.17) | copy-start | bytes 10616836
  22.2 41.2 %copy-start.3 = (s32[3328]{0:T(1024)}, s32[3328]{0:T(1024)S(1)}, u32[]{:S(2)}) copy-start(s32[3328]{0:T(1024)S(1)} %fusion.18) | copy-start | bytes 39940
  47.1 0.6 copy-start.1
  63.4 22.1 %all-to-all-start.1 = ((bf16[8,624,128]{2,1,0:T(8,128)(2,1)}), bf16[8,624,128]{2,1,0:T(8,128)(2,1)}, u32[]{:S(2)}, u32[]{:S(2)}) async-start(bf16[8,624,128]{2,1,0:T(8,128)(2,1)} %bitcast.33), calls=%async_computation.1 | async-start | bytes 2555904 | tf_op jit(solution)/shard_map/all_to_all | solution.py:105
  132.3 22.1 %all-to-all-start.2 = ((bf16[8,624,128]{2,1,0:T(8,128)(2,1)}), bf16[8,624,128]{2,1,0:T(8,128)(2,1)}, u32[]{:S(2)}, u32[]{:S(2)}) async-start(bf16[8,624,128]{2,1,0:T(8,128)(2,1)} %bitcast.32), calls=%async_computation.2 | async-start | bytes 2555904 | tf_op jit(solution)/shard_map/all_to_all | solution.py:137
  136.6 67.6 %all-reduce.2.cloned.1.call-start = ((), (), s32[]{:S(2)}) async-start(), calls=%async_computation.3 | async-start | bytes 1277952 | tf_op jit(solution)/shard_map/psum | solution.py:152
  154.4 9.7 %copy-start.2 = (f32[3456]{0:T(1024)S(1)}, f32[3456]{0:T(1024)}, u32[]{:S(2)}) copy-start(f32[3456]{0:T(1024)} %fusion.2) | copy-start | bytes 41476
Sparse Core Ops, SparseCore 0:
  164.3 39.8 all-reduce.1

commit v14 on v13

--- a/solution.py
+++ b/solution.py
@@ -17,7 +17,7 @@
 
 
 def _chunk_of(count):
-    for size in (1664, 512, 384, 256, 128):
+    for size in (4992, 1664, 512, 384, 256, 128):
         if count % size == 0:
             return size
     return 512

time: 216 us -> 215 us (level)
  no operation moved by 1% of the time
where the time goes in v14:
time: 215 us; the launch traced here: 213 us
  local copies, waits for them, and re-layouts  71.5 us (33%)
  blocking collectives  49.6 us (23%)
  waiting for transfers between devices  25 us (12%)
  other arithmetic  23.1 us (11%)
  between operations  14.1 us (7%)
  matrix products  11.6 us (5%)
  Pallas kernels  8.83 us (4%)
  starting transfers between devices  8.73 us (4%)
    psum x1, blocking collectives, local(): bias_grad = lax.psum(bias_local, ('grp', 'emb'))  39.7 us
    scatter x1, local copies, waits for them, and re-layouts, local(): jnp.zeros((slot_count, row_width), jnp.bfloat16).at[buffer_place]  14.9 us
    scatter x1, local copies, waits for them, and re-layouts, local(): jnp.zeros((owner_count * capacity,), jnp.int32).at[buffer_place]  13.5 us
    all_to_all x1, waiting for transfers between devices, local(): lax.all_to_all(fetched, 'emb', split_axis=0, concat_axis=0, tiled=True)  13.2 us
    gather x1, local copies, waits for them, and re-layouts, local(): fetched = flat_table[received]  12.3 us
    all_to_all x1, waiting for transfers between devices, local(): lax.all_to_all(outgoing.reshape(owner_count, capacity, row_width), 'emb',...  11.4 us
    all_to_all x1, blocking collectives, local(): lax.all_to_all(request, 'emb', split_axis=0, concat_axis=0, tiled=True)  9.94 us
    gather x1, local copies, waits for them, and re-layouts, local(): arrived.reshape(slot_count, row_width)[buffer_place]  9.21 us
  transfers between devices with their start and end apart: 3, of which 3 were waited for; matrix products, arithmetic and copies ran while one was open for 5% of the time, Pallas kernels for 0%

profile of v14, /device:TPU:0, one launch (start us, length us, event | category | flops | bytes accessed | tf_op | source)
XLA Modules:
  0.0 212.5 jit_solution(2349860490385800096)
XLA Ops:
  7.2 0.0 copy-start
  7.2 0.9 broadcast_add_fusion
  8.1 0.7 copy.16
  8.9 1.6 reshape.125
  10.4 0.7 reduce
  11.2 0.7 fusion.14
  11.9 5.2 %reduce-window.6 = s32[8,26,128]{2,1,0:T(8,128)} reduce-window(s32[8,26,128]{2,1,0:T(8,128)} %fusion.14, s32[]{:T(128)} %constant.9.clone.1), window={size=1x1x128 pad=0_0x0_0x127_0}, to_apply=%region_0.0 | reduce-window | flops 3381248 | bytes 212996 | tf_op jit(solution)/shard_map/reduce-window
  17.1 1.8 slice_reduce_fusion
  18.9 1.5 reduce-window.9
  20.3 1.0 add_bitcast_fusion
  21.4 0.1 fusion.16
  21.5 0.8 fusion.18
  22.2 0.0 copy-start.3
  22.2 13.5 %scatter_custom_fusion = s32[4992]{0:T(1024)} fusion(s32[3328]{0:T(1024)S(1)} %fusion.18, s32[3328]{0:T(1024)} %reshape.125, s32[]{:T(128)} %constant.9.clone.1), kind=kCustom, calls=%fused_computation.34 | custom fusion | bytes 20480 | tf_op jit(solution)/shard_map/scatter | solution.py:99
  35.7 1.4 all_to_all.14
  37.1 9.9 %all_to_all.22 = s32[8,1,624]{2,1,0:T(1,128)S(1)} all-to-all(s32[8,1,624]{2,1,0:T(1,128)} %all_to_all.14), channel_id=1, replica_groups=mesh['grp'=4,'emb'=8] {'emb'}, dimensions={0} | all-to-all | bytes 39936 | tf_op jit(solution)/shard_map/all_to_all | solution.py:101
  47.1 0.0 copy-start.1
  47.1 0.6 copy-done.1
  47.7 0.7 fusion.17
  48.3 1.4 reshape.107
  49.8 1.3 pad_clamp_fusion
  51.1 12.3 %gather_fusion = bf16[4992,128]{1,0:T(8,128)(2,1)} fusion(bf16[2496,128]{1,0:T(8,128)(2,1)} %bitcast.31, s32[5120]{0:T(1024)} %pad_clamp_fusion), kind=kCustom, calls=%fused_computation | custom fusion | bytes 2575872 | tf_op jit(solution)/shard_map/gather | solution.py:104
  63.4 0.0 copy-done.3
  63.4 4.3 %all-to-all-start.1 = ((bf16[8,624,128]{2,1,0:T(8,128)(2,1)}), bf16[8,624,128]{2,1,0:T(8,128)(2,1)}, u32[]{:S(2)}, u32[]{:S(2)}) async-start(bf16[8,624,128]{2,1,0:T(8,128)(2,1)} %bitcast.33), calls=%async_computation.1 | async-start | bytes 2555904 | tf_op jit(solution)/shard_map/all_to_all | solution.py:105
  67.6 0.7 convert_element_type.31
  68.3 1.3 pad_clamp_fusion.1
  69.7 1.4 constant_dynamic-update-slice_fusion.1
  71.1 1.2 select_reduce_fusion
  72.3 13.2 %all-to-all-done.1 = bf16[8,624,128]{2,1,0:T(8,128)(2,1)} async-done(((bf16[8,624,128]{2,1,0:T(8,128)(2,1)}), bf16[8,624,128]{2,1,0:T(8,128)(2,1)}, u32[]{:S(2)}, u32[]{:S(2)}) %all-to-all-start.1) | async-done | bytes 1277984 | tf_op jit(solution)/shard_map/all_to_all | solution.py:105
  85.5 9.2 %gather_fusion.1 = bf16[3328,128]{1,0:T(8,128)(2,1)} fusion(bf16[4992,128]{1,0:T(8,128)(2,1)} %bitcast.4, s32[4096]{0:T(1024)} %pad_clamp_fusion.1), kind=kCustom, calls=%fused_computation.1 | custom fusion | bytes 1717248 | tf_op jit(solution)/shard_map/gather | solution.py:106
  94.7 2.8 %reshape.99 = bf16[128,3328]{1,0:T(8,128)(2,1)} reshape(bf16[3328,128]{1,0:T(8,128)(2,1)} %gather_fusion.1) | data formatting | bytes 1703936 | tf_op jit(solution)/shard_map/reshape | solution.py:106
  97.5 2.1 %constant_dynamic-update-slice_fusion = bf16[128,3456]{1,0:T(8,128)(2,1)} fusion(bf16[128,3456]{1,0:T(8,128)(2,1)} %constant_dynamic-update-slice_fusion.1, bf16[128,3328]{1,0:T(8,128)(2,1)} %reshape.99), kind=kLoop, calls=%fused_computation.39 | loop fusion | bytes 1703936 | tf_op jit(solution)/shard_map/concatenate | solution.py:109
  99.6 0.0 copy-done
  99.6 5.6 %fusion.4 = (f32[128]{0:T(128)}, f32[128,3456]{1,0:T(8,128)}) fusion(bf16[128,3456]{1,0:T(8,128)(2,1)} %constant_dynamic-update-slice_fusion, f32[3456]{0:T(1024)S(1)} %convert_element_type.31, f32[3456]{0:T(1024)} %param.19, bf16[512,3456]{1,0:T(8,128)(2,1)} %param.18, bf16[3456,512]{1,0:T(8,128)(2,1)S(1)} %copy-done), kind=kOutput, calls=%fused_computation.13 | convolution fusion | flops 908689280 | bytes 9760256 | tf_op jit(solution)/shard_map/dot_general | solution.py:113
  105.2 1.2 divide_subtract_fusion
  106.4 6.1 %fusion = bf16[128,3456]{1,0:T(8,128)(2,1)} fusion(bf16[3456,512]{1,0:T(8,128)(2,1)S(1)} %copy-done, f32[128,3456]{1,0:T(8,128)} %get-tuple-element.10, bf16[512,3456]{1,0:T(8,128)(2,1)} %param.18, bf16[128,3456]{1,0:T(8,128)(2,1)} %constant_dynamic-update-slice_fusion, f32[128]{0:T(128)} %divide_subtract_fusion, f32[3456]{0:T(1024)S(1)} %convert_element_type.31), kind=kOutput, calls=%fused_computation.6 | convolution fusion | flops 910016512 | bytes 10631168 | tf_op jit(solution)/shard_map/dot_general | solution.py:130
  112.4 2.1 slice.22
  114.5 2.9 %reshape.133 = bf16[3328,128]{1,0:T(8,128)(2,1)} reshape(bf16[128,3328]{1,0:T(8,128)(2,1)} %slice.22) | data formatting | bytes 1703936 | tf_op jit(solution)/shard_map/reshape | solution.py:135
  117.4 14.9 %scatter_custom_fusion.1 = bf16[4992,128]{1,0:T(8,128)(2,1)} fusion(s32[3328]{0:T(1024)} %copy-done.3, bf16[3328,128]{1,0:T(8,128)(2,1)} %reshape.133, bf16[]{:T(256)} %constant.8.clone.1), kind=kCustom, calls=%fused_computation.18 | custom fusion | bytes 1278464 | tf_op jit(solution)/shard_map/scatter | solution.py:136
  132.3 4.3 %all-to-all-start.2 = ((bf16[8,624,128]{2,1,0:T(8,128)(2,1)}), bf16[8,624,128]{2,1,0:T(8,128)(2,1)}, u32[]{:S(2)}, u32[]{:S(2)}) async-start(bf16[8,624,128]{2,1,0:T(8,128)(2,1)} %bitcast.32), calls=%async_computation.2 | async-start | bytes 2555904 | tf_op jit(solution)/shard_map/all_to_all | solution.py:137
  136.5 0.2 all-reduce.2.cloned.1.call-start
  136.8 1.4 reduce.4
  138.1 1.4 reshape_reshape.4.right_ref
  139.6 1.4 slice.21
  141.0 2.1 fusion.2
  143.0 11.4 %all-to-all-done.2 = bf16[8,624,128]{2,1,0:T(8,128)(2,1)} async-done(((bf16[8,624,128]{2,1,0:T(8,128)(2,1)}), bf16[8,624,128]{2,1,0:T(8,128)(2,1)}, u32[]{:S(2)}, u32[]{:S(2)}) %all-to-all-start.2) | async-done | bytes 1277984 | tf_op jit(solution)/shard_map/all_to_all | solution.py:137
  154.4 0.0 copy-start.2
  154.4 8.8 %shard_map.130 = bf16[2496,128]{1,0:T(8,128)(2,1)} custom-call(s32[1,4992]{1,0:T(1,128)} %reshape_reshape.4.right_ref, bf16[4992,128]{1,0:T(8,128)(2,1)} %bitcast.6.data_ref), custom_call_target="tpu_custom_call" | custom-call | flops 3189768192 | bytes 1916928 | tf_op jit(solution)/shard_map/pallas_call | solution.py:51
  163.2 0.0 all-reduce.2.cloned.1.call-update
  163.3 0.0 copy-done.2
  163.3 39.7 %psum.15 = f32[3456]{0:T(1024)} all-reduce(f32[3456]{0:T(1024)S(1)} %copy-done.2), channel_id=1, replica_groups=mesh['grp'=4,'emb'=8] {'grp','emb'}, use_global_device_ids=true, to_apply=%region_9.10 | all-reduce | flops 3456 | bytes 27648 | tf_op jit(solution)/shard_map/psum | solution.py:154
  203.0 0.4 all-reduce.2.cloned.1.call-done
  203.4 2.3 %reshape.104 = f32[26,96,128]{2,1,0:T(8,128)} convert(bf16[26,96,128]{2,1,0:T(8,128)(2,1)} %all-reduce.2.cloned.1.call-done) | non-fusion elementwise | flops 319488 | bytes 1916928 | tf_op jit(solution)/shard_map/reshape | solution.py:153
  (1 shorter events, 0.0 us)
Async XLA Ops:
  7.2 92.5 %copy-start = (bf16[3456,512]{1,0:T(8,128)(2,1)S(1)}, bf16[3456,512]{1,0:T(8,128)(2,1)}, u32[]{:S(2)}) copy-start(bf16[3456,512]{1,0:T(8,128)(2,1)} %param.17) | copy-start | bytes 10616836
  22.2 41.2 %copy-start.3 = (s32[3328]{0:T(1024)}, s32[3328]{0:T(1024)S(1)}, u32[]{:S(2)}) copy-start(s32[3328]{0:T(1024)S(1)} %fusion.18) | copy-start | bytes 39940
  47.1 0.6 copy-start.1
  63.4 22.1 %all-to-all-start.1 = ((bf16[8,624,128]{2,1,0:T(8,128)(2,1)}), bf16[8,624,128]{2,1,0:T(8,128)(2,1)}, u32[]{:S(2)}, u32[]{:S(2)}) async-start(bf16[8,624,128]{2,1,0:T(8,128)(2,1)} %bitcast.33), calls=%async_computation.1 | async-start | bytes 2555904 | tf_op jit(solution)/shard_map/all_to_all | solution.py:105
  132.3 22.1 %all-to-all-start.2 = ((bf16[8,624,128]{2,1,0:T(8,128)(2,1)}), bf16[8,624,128]{2,1,0:T(8,128)(2,1)}, u32[]{:S(2)}, u32[]{:S(2)}) async-start(bf16[8,624,128]{2,1,0:T(8,128)(2,1)} %bitcast.32), calls=%async_computation.2 | async-start | bytes 2555904 | tf_op jit(solution)/shard_map/all_to_all | solution.py:137
  136.5 66.9 %all-reduce.2.cloned.1.call-start = ((), (), s32[]{:S(2)}) async-start(), calls=%async_computation.3 | async-start | bytes 1277952 | tf_op jit(solution)/shard_map/psum | solution.py:152
  154.4 8.9 %copy-start.2 = (f32[3456]{0:T(1024)S(1)}, f32[3456]{0:T(1024)}, u32[]{:S(2)}) copy-start(f32[3456]{0:T(1024)} %fusion.2) | copy-start | bytes 41476
Sparse Core Ops, SparseCore 0:
  163.4 39.9 all-reduce.1
